TPU v7x, 256 devices: a whole 4x4x8 slice. The times are simulated.
256 devices in a mesh: dp: 16 (over z, x_lo), own: 16 (over x_hi, y, core).
Axes of the slice: x: 4 (x_hi: 2, x_lo: 2; x = x_hi * 2 + x_lo), y: 4, z: 8, core: 2. Of those that a mesh axis runs over, the one named last changes fastest.
Arguments:
- grads: float32 [16, 16, 1024, 1024], P('dp', None, 'own'), may hold values from -0.27 to 0.27
- owner_map: int32 [16], replicated, may hold values from 0 to 31, as said below
- stat_left: float32 [32, 1024, 1024], P('own', 'dp'), as said below
- stat_right: float32 [32, 1024, 1024], P('own', 'dp'), as said below
- root_left: bfloat16 [32, 1024, 1024], P('own', 'dp'), as said below
- root_right: bfloat16 [32, 1024, 1024], P('own', 'dp'), as said below
- master: float32 [32, 1024, 1024], P('own', 'dp'), may hold values from -4 to 4
- moment_first: float32 [32, 1024, 1024], P('own', 'dp'), may hold values from -0.6 to 0.6
- moment_second: float32 [32, 1024, 1024], P('own', 'dp'), may hold values from 0.001 to 1, as said below
Outputs:
- left_next: float32 [32, 1024, 1024], P('own', 'dp')
- right_next: float32 [32, 1024, 1024], P('own', 'dp')
- master_next: float32 [32, 1024, 1024], P('own', 'dp')
- first_next: float32 [32, 1024, 1024], P('own', 'dp')
- second_next: float32 [32, 1024, 1024], P('own', 'dp')
- weights_out: bfloat16 [16, 1024, 1024], P(None, ('dp', 'own'))
Inputs may be any that keep to these rules, and one draw needn't show every extreme that they name: `owner_map`: no two blocks share a slot. In every draw all 2 slots of some owner are taken, and so are slots 0 and 31. `root_left`: symmetric in its last two dimensions. `root_right`: symmetric in its last two dimensions. `stat_left`: symmetric in its last two dimensions. `stat_right`: symmetric in its last two dimensions. `moment_second`: Positive.
All inputs are finite; a program needn't handle non-finite values.
Results may differ from a plain program's by a relative error of at most 0.0045.
Values may be sent and summed in bfloat16 or wider, within the bound.
No kernel may reach another device: no remote copies, remote signals or barrier semaphores. Data moves between devices by JAX's collectives and lax.ppermute only.
A program may use at most 128 MiB of HBM per device.

v0:
```python
import jax
import jax.numpy as jnp
from jax import lax
from jax.sharding import PartitionSpec as P

stat_decay = 0.9
first_decay = 0.9
second_decay = 0.99
learn_rate = 0.25


def per_device(
    grads,
    owner_map,
    stat_left,
    stat_right,
    root_left,
    root_right,
    master,
    moment_first,
    moment_second,
):
    owners = lax.axis_size("own")
    slot_count = stat_left.shape[0]
    rows_dev = stat_left.shape[1]
    order_size = stat_left.shape[2]
    blocks = owner_map.shape[0]
    owned_slots = owners * slot_count
    highest = lax.Precision.HIGHEST
    matches = owner_map[:, None] == jnp.arange(owned_slots, dtype=jnp.int32)[None, :]
    occupied = jnp.any(matches, axis=0)
    block_of = jnp.sum(jnp.where(matches, jnp.arange(blocks, dtype=jnp.int32)[:, None], 0), axis=0)
    partials = grads[0]
    summed = lax.psum(partials, "dp")
    packed = jnp.where(occupied[:, None, None], jnp.take(summed, block_of, axis=0), 0.0)
    packed = packed.reshape(owners, slot_count, summed.shape[1], order_size)
    arrived = lax.all_to_all(
        packed.astype(jnp.bfloat16), "own", split_axis=0, concat_axis=2, tiled=True
    ).astype(packed.dtype)
    whole_grad = arrived.reshape(slot_count, order_size, order_size)
    first_row = lax.axis_index("dp") * rows_dev
    own_rows = lax.dynamic_slice_in_dim(whole_grad, first_row, rows_dev, 1)
    own_cols = lax.dynamic_slice_in_dim(whole_grad, first_row, rows_dev, 2)
    left_new = stat_decay * stat_left + (1.0 - stat_decay) * jnp.einsum(
        "srk,snk->srn", own_rows, whole_grad, precision=highest, preferred_element_type=jnp.float32
    )
    right_new = stat_decay * stat_right + (1.0 - stat_decay) * jnp.einsum(
        "skr,skn->srn", own_cols, whole_grad, precision=highest, preferred_element_type=jnp.float32
    )
    first_new = first_decay * moment_first + (1.0 - first_decay) * own_rows
    second_new = second_decay * moment_second + (1.0 - second_decay) * own_rows * own_rows
    adam_step = first_new / (jnp.sqrt(second_new) + 1e-08)
    rounded = whole_grad.astype(jnp.bfloat16)
    partial_product = jnp.einsum(
        "skn,srn->skr", rounded, root_right, preferred_element_type=jnp.float32
    ).astype(jnp.bfloat16)
    direction = jnp.einsum(
        "srk,skn->srn",
        root_left,
        lax.all_gather(partial_product, "dp", axis=2, tiled=True),
        preferred_element_type=jnp.float32,
    )
    square_sums = lax.psum(
        (jnp.sum(adam_step * adam_step, axis=(1, 2)), jnp.sum(direction * direction, axis=(1, 2))),
        "dp",
    )
    graft = jnp.sqrt(square_sums[0]) / (jnp.sqrt(square_sums[1]) + 1e-06)
    master_new = master - learn_rate * graft[:, None, None] * direction
    occupied_mine = lax.dynamic_slice_in_dim(
        occupied, lax.axis_index("own") * slot_count, slot_count
    )[:, None, None]
    left_next = jnp.where(occupied_mine, left_new, stat_left)
    right_next = jnp.where(occupied_mine, right_new, stat_right)
    master_next = jnp.where(occupied_mine, master_new, master)
    first_next = jnp.where(occupied_mine, first_new, moment_first)
    second_next = jnp.where(occupied_mine, second_new, moment_second)
    shares = master_new.astype(jnp.bfloat16).reshape(
        slot_count, owners, rows_dev // owners, order_size
    )
    delivered = lax.all_to_all(shares, "own", split_axis=1, concat_axis=0, tiled=True)
    delivered = delivered.reshape(owned_slots, rows_dev // owners, order_size)
    weights_out = jnp.take(delivered, owner_map, axis=0)
    return (left_next, right_next, master_next, first_next, second_next, weights_out)


def solution(mesh):
    return jax.shard_map(
        per_device,
        mesh=mesh,
        in_specs=(
            P("dp", None, "own", None),
            P(),
            P("own", "dp", None),
            P("own", "dp", None),
            P("own", "dp", None),
            P("own", "dp", None),
            P("own", "dp", None),
            P("own", "dp", None),
            P("own", "dp", None),
        ),
        out_specs=(
            P("own", "dp", None),
            P("own", "dp", None),
            P("own", "dp", None),
            P("own", "dp", None),
            P("own", "dp", None),
            P(None, ("dp", "own"), None),
        ),
        check_vma=False,
    )
```

profile of v0, /device:TPU:1, one launch (start us, length us, event | category | flops | bytes accessed | tf_op | source)
XLA Modules:
  0.0 420.0 jit_solution(211106581229123987)
XLA Ops:
  7.2 0.8 fusion.13
  8.0 0.7 select_reduce_fusion
  8.8 0.1 reduce_sum.32
  8.8 0.1 broadcast_in_dim.75
  9.0 179.9 %all-reduce.2 = bf16[16,64,1024]{2,1,0:T(8,128)(2,1)S(1)} all-reduce(f32[16,64,1024]{2,1,0:T(8,128)} %bitcast.52), channel_id=1, replica_groups=mesh['dp'=16,'own'=16] {'dp'}, use_global_device_ids=true, to_apply=%region_2.3 | all-reduce | flops 1048576 | bytes 6291456 | tf_op jit(solution)/shard_map/psum | solution.py:34
  188.9 2.8 gather_fusion
  191.6 4.3 %select_convert_fusion = bf16[16,2,64,1024]{3,2,1,0:T(8,128)(2,1)S(1)} fusion(bf16[16,2,64,1024]{3,2,1,0:T(8,128)(2,1)} %bitcast.51, pred[16,2]{1,0:T(8,128)(4,1)S(1)} %compare_and_fusion, pred[16,2]{1,0:T(8,128)(4,1)S(1)} %broadcast_in_dim.75), kind=kLoop, calls=%fused_computation.2 | loop fusion | flops 4194304 | bytes 8388672 | tf_op jit(solution)/shard_map/convert_element_type | solution.py:38
  195.9 61.4 %all_to_all.30 = bf16[16,2,64,1024]{3,2,1,0:T(8,128)(2,1)S(1)} all-to-all(bf16[16,2,64,1024]{3,2,1,0:T(8,128)(2,1)S(1)} %select_convert_fusion), channel_id=1, replica_groups=mesh['dp'=16,'own'=16] {'own'}, dimensions={0} | all-to-all | bytes 8388608 | tf_op jit(solution)/shard_map/all_to_all | solution.py:37
  257.4 0.7 copy.30
  258.1 1.9 copy-done.1
  260.1 2.1 convolution_convert_fusion
  262.3 2.4 fusion.7
  264.8 4.5 %fusion.3 = f32[2,64,1024]{2,1,0:T(8,128)} fusion(f32[2,64,1024]{2,1,0:T(8,128)S(1)} %copy-done.5, bf16[2,1024,1024]{2,1,0:T(8,128)(2,1)} %bitcast.49, s32[]{:T(128)S(6)} %select_n.69, pred[2]{0:T(512)(128)(4,1)S(1)} %dynamic_slice.13), kind=kOutput, calls=%fused_computation.8 | convolution fusion | flops 268959744 | bytes 5505030 | tf_op jit(solution)/shard_map/srk,snk->srn/dot_general | solution.py:44
  269.3 86.4 %all-gather.2.cloned.1.call-done = bf16[2,1024,1024]{1,2,0:T(8,128)(2,1)} async-done(((bf16[2,1024,64]{1,2,0:T(8,128)(2,1)}), bf16[2,1024,1024]{1,2,0:T(8,128)(2,1)}) %all-gather.2.cloned.1.call-update) | async-done | bytes 4194320 | tf_op jit(solution)/shard_map/all_gather | solution.py:60
  355.7 3.7 multiply_reduce_fusion
  359.4 26.4 %all-reduce = (f32[2]{0:T(128)S(1)}, f32[2]{0:T(128)S(1)}) all-reduce(f32[2]{0:T(128)S(1)} %get-tuple-element.13, f32[2]{0:T(128)S(1)} %get-tuple-element.9), channel_id=1, replica_groups=mesh['dp'=16,'own'=16] {'dp'}, use_global_device_ids=true, to_apply=%region_6.7 | all-reduce | flops 4 | bytes 32 | tf_op jit(solution)/shard_map/psum | solution.py:63
  385.8 1.0 fusion.10
  386.8 0.1 reshape.74
  386.9 0.8 copy.32
  387.7 15.3 %all-to-all-start.1 = ((bf16[2,16,4,1024]{3,2,0,1:T(4,128)(2,1)}), bf16[2,16,4,1024]{3,2,0,1:T(4,128)(2,1)S(1)}, u32[]{:S(2)}, u32[]{:S(2)}) async-start(bf16[2,16,4,1024]{3,2,0,1:T(4,128)(2,1)} %copy.32), calls=%async_computation.1 | async-start | bytes 524288 | tf_op jit(solution)/shard_map/all_to_all | solution.py:80
  403.0 4.3 %fusion.1 = f32[2,64,1024]{2,1,0:T(8,128)} fusion(f32[2,64,1024]{2,1,0:T(8,128)S(1)} %copy-done.2, bf16[2,1024,1024]{2,1,0:T(8,128)(2,1)} %bitcast.50, s32[]{:T(128)S(6)} %select_n.69, pred[2]{0:T(512)(128)(4,1)S(1)} %dynamic_slice.13), kind=kOutput, calls=%fused_computation.5 | convolution fusion | flops 268959744 | bytes 5767174 | tf_op jit(solution)/shard_map/skr,skn->srn/dot_general | solution.py:47
  407.3 4.4 %all-to-all-done.1 = bf16[2,16,4,1024]{3,2,0,1:T(4,128)(2,1)S(1)} async-done(((bf16[2,16,4,1024]{3,2,0,1:T(4,128)(2,1)}), bf16[2,16,4,1024]{3,2,0,1:T(4,128)(2,1)S(1)}, u32[]{:S(2)}, u32[]{:S(2)}) %all-to-all-start.1) | async-done | bytes 262176 | tf_op jit(solution)/shard_map/all_to_all | solution.py:80
  411.7 0.7 gather_fusion.1
  412.4 0.8 broadcast_select_fusion
  (27 shorter events, 0.2 us)
Async XLA Ops:
  7.2 348.5 %copy-start = (bf16[2,64,1024]{2,1,0:T(8,128)(2,1)S(1)}, bf16[2,64,1024]{2,1,0:T(8,128)(2,1)}, u32[]{:S(2)}) copy-start(bf16[2,64,1024]{2,1,0:T(8,128)(2,1)} %param.13) | copy-start | bytes 786436
  7.2 348.5 %all-gather.2.cloned.1.call-start = ((), (), s32[]{:S(2)}) async-start(), calls=%async_computation.2 | async-start | bytes 4456448 | tf_op jit(solution)/shard_map/all_gather | solution.py:60
  257.4 2.7 copy-start.7
  258.1 2.0 copy-start.1
  258.1 4.2 copy-start.8
  258.1 4.2 %copy-start.3 = (f32[2,64,1024]{2,1,0:T(8,128)S(1)}, f32[2,64,1024]{2,1,0:T(8,128)}, u32[]{:S(2)}) copy-start(f32[2,64,1024]{2,1,0:T(8,128)} %param.17) | copy-start | bytes 1572868
  258.1 4.2 %copy-start.4 = (f32[2,64,1024]{2,1,0:T(8,128)S(1)}, f32[2,64,1024]{2,1,0:T(8,128)}, u32[]{:S(2)}) copy-start(f32[2,64,1024]{2,1,0:T(8,128)} %param.16) | copy-start | bytes 1572868
  258.1 6.6 %copy-start.5 = (f32[2,64,1024]{2,1,0:T(8,128)S(1)}, f32[2,64,1024]{2,1,0:T(8,128)}, u32[]{:S(2)}) copy-start(f32[2,64,1024]{2,1,0:T(8,128)} %param.11) | copy-start | bytes 1572868
  264.8 121.1 %copy-start.6 = (f32[2,64,1024]{2,1,0:T(8,128)S(1)}, f32[2,64,1024]{2,1,0:T(8,128)}, u32[]{:S(2)}) copy-start(f32[2,64,1024]{2,1,0:T(8,128)} %param.15) | copy-start | bytes 1572868
  269.3 133.7 %copy-start.2 = (f32[2,64,1024]{2,1,0:T(8,128)S(1)}, f32[2,64,1024]{2,1,0:T(8,128)}, u32[]{:S(2)}) copy-start(f32[2,64,1024]{2,1,0:T(8,128)} %param.12) | copy-start | bytes 1572868
  387.7 24.0 %all-to-all-start.1 = ((bf16[2,16,4,1024]{3,2,0,1:T(4,128)(2,1)}), bf16[2,16,4,1024]{3,2,0,1:T(4,128)(2,1)S(1)}, u32[]{:S(2)}, u32[]{:S(2)}) async-start(bf16[2,16,4,1024]{3,2,0,1:T(4,128)(2,1)} %copy.32), calls=%async_computation.1 | async-start | bytes 524288 | tf_op jit(solution)/shard_map/all_to_all | solution.py:80
Sparse Core Ops, SparseCore 0:
  262.3 93.3 all-gather.1
where the time goes:
time: 420 us
  blocking collectives  268 us (64%)
  waiting for transfers between devices  90.8 us (22%)
  starting transfers between devices  15.3 us (4%)
  matrix products  14.6 us (3%)
  between operations  14.2 us (3%)
  other arithmetic  10.1 us (2%)
  local copies, waits for them, and re-layouts  7.27 us (2%)
    psum x1, blocking collectives, per_device(): summed = lax.psum(partials, 'dp')  180 us
    all_gather x1, waiting for transfers between devices, per_device(): lax.all_gather(partial_product, 'dp', axis=2, tiled=True)  86.4 us
    all_to_all x1, blocking collectives, per_device(): lax.all_to_all(packed.astype(jnp.bfloat16), 'own', split_axis=0, concat_a...  61.4 us
    psum x1, blocking collectives, per_device(): lax.psum((jnp.sum(adam_step * adam_step, axis=(1, 2)), jnp.sum(direction...  26.4 us
    all_to_all x1, starting transfers between devices, per_device(): lax.all_to_all(shares, 'own', split_axis=1, concat_axis=0, tiled=True)  15.3 us
  transfers between devices with their start and end apart: 2, of which 2 were waited for; matrix products, arithmetic and copies ran while one was open for 3% of the time, Pallas kernels for 0%

commit v1 on v0

--- a/solution.py
+++ b/solution.py
@@ -26,7 +26,6 @@
     order_size = stat_left.shape[2]
     blocks = owner_map.shape[0]
     owned_slots = owners * slot_count
-    highest = lax.Precision.HIGHEST
     matches = owner_map[:, None] == jnp.arange(owned_slots, dtype=jnp.int32)[None, :]
     occupied = jnp.any(matches, axis=0)
     block_of = jnp.sum(jnp.where(matches, jnp.arange(blocks, dtype=jnp.int32)[:, None], 0), axis=0)
@@ -36,29 +35,27 @@
     packed = packed.reshape(owners, slot_count, summed.shape[1], order_size)
     arrived = lax.all_to_all(
         packed.astype(jnp.bfloat16), "own", split_axis=0, concat_axis=2, tiled=True
-    ).astype(packed.dtype)
-    whole_grad = arrived.reshape(slot_count, order_size, order_size)
+    )
+    right_full = lax.all_gather(root_right, "dp", axis=1, tiled=True)
     first_row = lax.axis_index("dp") * rows_dev
-    own_rows = lax.dynamic_slice_in_dim(whole_grad, first_row, rows_dev, 1)
-    own_cols = lax.dynamic_slice_in_dim(whole_grad, first_row, rows_dev, 2)
+    rounded = arrived.reshape(slot_count, order_size, order_size)
+    row_part = lax.dynamic_slice_in_dim(rounded, first_row, rows_dev, 1)
+    col_part = lax.dynamic_slice_in_dim(rounded, first_row, rows_dev, 2)
+    own_rows = row_part.astype(jnp.float32)
     left_new = stat_decay * stat_left + (1.0 - stat_decay) * jnp.einsum(
-        "srk,snk->srn", own_rows, whole_grad, precision=highest, preferred_element_type=jnp.float32
+        "srk,snk->srn", row_part, rounded, preferred_element_type=jnp.float32
     )
     right_new = stat_decay * stat_right + (1.0 - stat_decay) * jnp.einsum(
-        "skr,skn->srn", own_cols, whole_grad, precision=highest, preferred_element_type=jnp.float32
+        "skr,skn->srn", col_part, rounded, preferred_element_type=jnp.float32
     )
     first_new = first_decay * moment_first + (1.0 - first_decay) * own_rows
     second_new = second_decay * moment_second + (1.0 - second_decay) * own_rows * own_rows
     adam_step = first_new / (jnp.sqrt(second_new) + 1e-08)
-    rounded = whole_grad.astype(jnp.bfloat16)
-    partial_product = jnp.einsum(
-        "skn,srn->skr", rounded, root_right, preferred_element_type=jnp.float32
+    product = jnp.einsum(
+        "skn,snr->skr", rounded, right_full, preferred_element_type=jnp.float32
     ).astype(jnp.bfloat16)
     direction = jnp.einsum(
-        "srk,skn->srn",
-        root_left,
-        lax.all_gather(partial_product, "dp", axis=2, tiled=True),
-        preferred_element_type=jnp.float32,
+        "srk,skn->srn", root_left, product, preferred_element_type=jnp.float32
     )
     square_sums = lax.psum(
         (jnp.sum(adam_step * adam_step, axis=(1, 2)), jnp.sum(direction * direction, axis=(1, 2))),

time: 420 us -> 429 us (1.021)
  waiting for transfers between devices: 90.8 us -> 60.3 us
  blocking collectives: 268 us -> 293 us
  starting transfers between devices: 15.3 us -> 27.4 us
    psum x1, blocking collectives: 180 us -> 269 us  [per_device(): summed = lax.psum(partials, 'dp')]
    all_gather x1, waiting for transfers between devices: 86.4 us -> 0.01 us  [per_device(): right_full = lax.all_gather(root_right, 'dp', axis=1, tiled=True)]
    all_to_all x1 -> x0, blocking collectives: 61.4 us -> none  [per_device(): lax.all_to_all(packed.astype(jnp.bfloat16), 'own', split_axis=0, concat_a...]
    all_to_all x0 -> x1, waiting for transfers between devices: none -> 55.2 us  [per_device(): lax.all_to_all(packed.astype(jnp.bfloat16), 'own', split_axis=0, concat_a...]
    all_to_all x1, starting transfers between devices: 15.3 us -> 21.8 us  [per_device(): lax.all_to_all(shares, 'own', split_axis=1, concat_axis=0, tiled=True)]
    all_to_all x0 -> x1, starting transfers between devices: none -> 5.63 us  [per_device(): lax.all_to_all(packed.astype(jnp.bfloat16), 'own', split_axis=0, concat_a...]
    dot_general x4 -> x3, matrix products: 14.6 us -> 14.4 us  [the longest x1 7.84 us: per_device(): jnp.einsum('srk,skn->srn', root_left, product, preferred_element_type=jnp...]
  transfers between devices with their start and end apart: 2 -> 3, of which waited for: 2 -> 2; matrix products, arithmetic and copies ran while one was open for 3% -> 5% of each run, Pallas kernels for 0% -> 0%
where the time goes in v1:
time: 429 us; the launch traced here: 428 us
  blocking collectives  293 us (68%)
  waiting for transfers between devices  60.3 us (14%)
  starting transfers between devices  27.4 us (6%)
  matrix products  14.4 us (3%)
  between operations  14.1 us (3%)
  other arithmetic  11.4 us (3%)
  local copies, waits for them, and re-layouts  7.71 us (2%)
    psum x1, blocking collectives, per_device(): summed = lax.psum(partials, 'dp')  269 us
    all_to_all x1, waiting for transfers between devices, per_device(): lax.all_to_all(packed.astype(jnp.bfloat16), 'own', split_axis=0, concat_a...  55.2 us
    psum x1, blocking collectives, per_device(): lax.psum((jnp.sum(adam_step * adam_step, axis=(1, 2)), jnp.sum(direction...  24.1 us
    all_to_all x1, starting transfers between devices, per_device(): lax.all_to_all(shares, 'own', split_axis=1, concat_axis=0, tiled=True)  21.8 us
  transfers between devices with their start and end apart: 3, of which 2 were waited for; matrix products, arithmetic and copies ran while one was open for 5% of the time, Pallas kernels for 0%

profile of v1, /device:TPU:1, one launch (start us, length us, event | category | flops | bytes accessed | tf_op | source)
XLA Modules:
  0.0 428.3 jit_solution(11233501601034054247)
XLA Ops:
  7.2 0.7 all-gather.2.cloned.1.call-update
  7.9 0.7 select_reduce_fusion
  8.7 0.1 reduce_sum.32
  8.7 0.8 fusion.16
  9.5 0.1 broadcast_in_dim.75
  9.6 268.8 %all-reduce.2 = bf16[16,64,1024]{2,1,0:T(8,128)(2,1)S(1)} all-reduce(f32[16,64,1024]{2,1,0:T(8,128)} %bitcast.31), channel_id=1, replica_groups=mesh['dp'=16,'own'=16] {'dp'}, use_global_device_ids=true, to_apply=%region_2.3 | all-reduce | flops 1048576 | bytes 6291456 | tf_op jit(solution)/shard_map/psum | solution.py:33
  278.4 2.8 gather_fusion
  281.2 6.3 %select_convert_fusion = bf16[16,2,64,1024]{3,2,1,0:T(8,128)(2,1)} fusion(bf16[16,2,64,1024]{3,2,1,0:T(8,128)(2,1)} %bitcast.30, pred[16,2]{1,0:T(8,128)(4,1)S(1)} %compare_and_fusion, pred[16,2]{1,0:T(8,128)(4,1)S(1)} %broadcast_in_dim.75), kind=kLoop, calls=%fused_computation.2 | loop fusion | flops 4194304 | bytes 8388672 | tf_op jit(solution)/shard_map/convert_element_type | solution.py:37
  287.5 5.6 %all-to-all-start = ((bf16[16,2,64,1024]{3,2,1,0:T(8,128)(2,1)}), bf16[16,2,64,1024]{3,2,1,0:T(8,128)(2,1)}, u32[]{:S(2)}, u32[]{:S(2)}) async-start(bf16[16,2,64,1024]{3,2,1,0:T(8,128)(2,1)} %select_convert_fusion), calls=%async_computation | async-start | bytes 8388608 | tf_op jit(solution)/shard_map/all_to_all | solution.py:36
  293.2 55.2 %all-to-all-done = bf16[16,2,64,1024]{3,2,1,0:T(8,128)(2,1)} async-done(((bf16[16,2,64,1024]{3,2,1,0:T(8,128)(2,1)}), bf16[16,2,64,1024]{3,2,1,0:T(8,128)(2,1)}, u32[]{:S(2)}, u32[]{:S(2)}) %all-to-all-start) | async-done | bytes 4194336 | tf_op jit(solution)/shard_map/all_to_all | solution.py:36
  348.5 2.7 copy.27
  351.2 1.9 fusion.10
  353.1 0.3 copy-done.1
  353.5 2.2 fusion.7
  355.7 7.8 %multiply_reduce_fusion = (f32[2]{0:T(128)S(1)}, f32[2,1024,64]{1,2,0:T(8,128)S(1)}) fusion(bf16[2,64,1024]{2,1,0:T(8,128)(2,1)S(1)} %copy-done, bf16[2,1024,1024]{2,1,0:T(8,128)(2,1)} %bitcast.28, bf16[2,1024,1024]{2,1,0:T(8,128)(2,1)} %all-gather.2.cloned.1.call-done), kind=kOutput, calls=%fused_computation.17 | convolution fusion | flops 4565762048 | bytes 9175048 | tf_op jit(solution)/shard_map/srk,skn->srn/dot_general | solution.py:57
  363.5 24.1 %all-reduce = (f32[2]{0:T(128)S(1)}, f32[2]{0:T(128)S(1)}) all-reduce(f32[2]{0:T(128)S(1)} %get-tuple-element.13, f32[2]{0:T(128)S(1)} %get-tuple-element.9), channel_id=1, replica_groups=mesh['dp'=16,'own'=16] {'dp'}, use_global_device_ids=true, to_apply=%region_6.7 | all-reduce | flops 4 | bytes 32 | tf_op jit(solution)/shard_map/psum | solution.py:60
  387.6 1.0 fusion.13
  388.6 0.1 reshape.58
  388.7 0.8 copy.29
  389.5 21.8 %all-to-all-start.1 = ((bf16[2,16,4,1024]{3,2,0,1:T(4,128)(2,1)}), bf16[2,16,4,1024]{3,2,0,1:T(4,128)(2,1)S(1)}, u32[]{:S(2)}, u32[]{:S(2)}) async-start(bf16[2,16,4,1024]{3,2,0,1:T(4,128)(2,1)} %copy.29), calls=%async_computation.1 | async-start | bytes 524288 | tf_op jit(solution)/shard_map/all_to_all | solution.py:77
  411.3 4.3 %fusion.5 = f32[2,64,1024]{2,1,0:T(8,128)} fusion(f32[2,64,1024]{2,1,0:T(8,128)S(1)} %copy-done.2, bf16[2,1024,1024]{2,1,0:T(8,128)(2,1)} %bitcast.29, s32[]{:T(128)S(6)} %select_n.69, pred[2]{0:T(512)(128)(4,1)S(1)} %dynamic_slice.9), kind=kOutput, calls=%fused_computation.8 | convolution fusion | flops 268959744 | bytes 5767174 | tf_op jit(solution)/shard_map/skr,skn->srn/dot_general | solution.py:48
  415.6 4.4 %all-to-all-done.1 = bf16[2,16,4,1024]{3,2,0,1:T(4,128)(2,1)S(1)} async-done(((bf16[2,16,4,1024]{3,2,0,1:T(4,128)(2,1)}), bf16[2,16,4,1024]{3,2,0,1:T(4,128)(2,1)S(1)}, u32[]{:S(2)}, u32[]{:S(2)}) %all-to-all-start.1) | async-done | bytes 262176 | tf_op jit(solution)/shard_map/all_to_all | solution.py:77
  420.0 0.7 gather_fusion.1
  420.6 0.8 broadcast_select_fusion
  (25 shorter events, 0.2 us)
Async XLA Ops:
  7.2 348.5 %copy-start = (bf16[2,64,1024]{2,1,0:T(8,128)(2,1)S(1)}, bf16[2,64,1024]{2,1,0:T(8,128)(2,1)}, u32[]{:S(2)}) copy-start(bf16[2,64,1024]{2,1,0:T(8,128)(2,1)} %param.13) | copy-start | bytes 786436
  7.2 348.5 %all-gather.2.cloned.1.call-start = ((), (), s32[]{:S(2)}) async-start(), calls=%async_computation.2 | async-start | bytes 4456448 | tf_op jit(solution)/shard_map/all_gather | solution.py:39
  287.5 5.7 %copy-start.7 = (s32[16]{0:T(128)S(1)}, s32[16]{0:T(128)}, u32[]{:S(2)}) copy-start(s32[16]{0:T(128)} %param.10) | copy-start | bytes 196
  287.5 61.0 %all-to-all-start = ((bf16[16,2,64,1024]{3,2,1,0:T(8,128)(2,1)}), bf16[16,2,64,1024]{3,2,1,0:T(8,128)(2,1)}, u32[]{:S(2)}, u32[]{:S(2)}) async-start(bf16[16,2,64,1024]{3,2,1,0:T(8,128)(2,1)} %select_convert_fusion), calls=%async_computation | async-start | bytes 8388608 | tf_op jit(solution)/shard_map/all_to_all | solution.py:36
  348.4 2.8 copy-start.3
  348.4 2.8 copy-start.4
  348.5 5.0 %copy-start.5 = (f32[2,64,1024]{2,1,0:T(8,128)S(1)}, f32[2,64,1024]{2,1,0:T(8,128)}, u32[]{:S(2)}) copy-start(f32[2,64,1024]{2,1,0:T(8,128)} %param.11) | copy-start | bytes 1572868
  351.2 2.3 copy-start.1
  355.7 32.0 %copy-start.6 = (f32[2,64,1024]{2,1,0:T(8,128)S(1)}, f32[2,64,1024]{2,1,0:T(8,128)}, u32[]{:S(2)}) copy-start(f32[2,64,1024]{2,1,0:T(8,128)} %param.15) | copy-start | bytes 1572868
  355.7 55.6 %copy-start.2 = (f32[2,64,1024]{2,1,0:T(8,128)S(1)}, f32[2,64,1024]{2,1,0:T(8,128)}, u32[]{:S(2)}) copy-start(f32[2,64,1024]{2,1,0:T(8,128)} %param.12) | copy-start | bytes 1572868
  389.5 30.5 %all-to-all-start.1 = ((bf16[2,16,4,1024]{3,2,0,1:T(4,128)(2,1)}), bf16[2,16,4,1024]{3,2,0,1:T(4,128)(2,1)S(1)}, u32[]{:S(2)}, u32[]{:S(2)}) async-start(bf16[2,16,4,1024]{3,2,0,1:T(4,128)(2,1)} %copy.29), calls=%async_computation.1 | async-start | bytes 524288 | tf_op jit(solution)/shard_map/all_to_all | solution.py:77
Sparse Core Ops, SparseCore 0:
  9.8 180.4 all-gather.1

commit v2 on v1

--- a/solution.py
+++ b/solution.py
@@ -1,12 +1,28 @@
 import jax
 import jax.numpy as jnp
 from jax import lax
-from jax.sharding import PartitionSpec as P
+from jax.sharding import Mesh, PartitionSpec as P
 
 stat_decay = 0.9
 first_decay = 0.9
 second_decay = 0.99
 learn_rate = 0.25
+DP = ("z", "xlo")
+
+
+def dp_index():
+    return lax.axis_index("z") * lax.axis_size("xlo") + lax.axis_index("xlo")
+
+
+def dp_gather(x, axis):
+    x = lax.all_gather(x, "xlo", axis=axis, tiled=True)
+    return lax.all_gather(x, "z", axis=axis, tiled=True)
+
+
+def dp_sum(x):
+    x = lax.psum_scatter(x, "xlo", scatter_dimension=1, tiled=True)
+    x = lax.psum(x, "z")
+    return lax.all_gather(x, "xlo", axis=1, tiled=True)
 
 
 def per_device(
@@ -29,15 +45,13 @@
     matches = owner_map[:, None] == jnp.arange(owned_slots, dtype=jnp.int32)[None, :]
     occupied = jnp.any(matches, axis=0)
     block_of = jnp.sum(jnp.where(matches, jnp.arange(blocks, dtype=jnp.int32)[:, None], 0), axis=0)
-    partials = grads[0]
-    summed = lax.psum(partials, "dp")
+    summed = dp_sum(grads[0].astype(jnp.bfloat16))
+    summed, root_right = lax.optimization_barrier((summed, root_right))
     packed = jnp.where(occupied[:, None, None], jnp.take(summed, block_of, axis=0), 0.0)
     packed = packed.reshape(owners, slot_count, summed.shape[1], order_size)
-    arrived = lax.all_to_all(
-        packed.astype(jnp.bfloat16), "own", split_axis=0, concat_axis=2, tiled=True
-    )
-    right_full = lax.all_gather(root_right, "dp", axis=1, tiled=True)
-    first_row = lax.axis_index("dp") * rows_dev
+    arrived = lax.all_to_all(packed, "own", split_axis=0, concat_axis=2, tiled=True)
+    right_full = dp_gather(root_right, 1)
+    first_row = dp_index() * rows_dev
     rounded = arrived.reshape(slot_count, order_size, order_size)
     row_part = lax.dynamic_slice_in_dim(rounded, first_row, rows_dev, 1)
     col_part = lax.dynamic_slice_in_dim(rounded, first_row, rows_dev, 2)
@@ -59,8 +73,9 @@
     )
     square_sums = lax.psum(
         (jnp.sum(adam_step * adam_step, axis=(1, 2)), jnp.sum(direction * direction, axis=(1, 2))),
-        "dp",
+        "xlo",
     )
+    square_sums = lax.psum(square_sums, "z")
     graft = jnp.sqrt(square_sums[0]) / (jnp.sqrt(square_sums[1]) + 1e-06)
     master_new = master - learn_rate * graft[:, None, None] * direction
     occupied_mine = lax.dynamic_slice_in_dim(
@@ -81,27 +96,29 @@
 
 
 def solution(mesh):
+    dp, own = mesh.shape["dp"], mesh.shape["own"]
+    split = Mesh(mesh.devices.reshape(dp // 2, 2, own), ("z", "xlo", "own"))
     return jax.shard_map(
         per_device,
-        mesh=mesh,
+        mesh=split,
         in_specs=(
-            P("dp", None, "own", None),
+            P(DP, None, "own", None),
             P(),
-            P("own", "dp", None),
-            P("own", "dp", None),
-            P("own", "dp", None),
-            P("own", "dp", None),
-            P("own", "dp", None),
-            P("own", "dp", None),
-            P("own", "dp", None),
+            P("own", DP, None),
+            P("own", DP, None),
+            P("own", DP, None),
+            P("own", DP, None),
+            P("own", DP, None),
+            P("own", DP, None),
+            P("own", DP, None),
         ),
         out_specs=(
-            P("own", "dp", None),
-            P("own", "dp", None),
-            P("own", "dp", None),
-            P("own", "dp", None),
-            P("own", "dp", None),
-            P(None, ("dp", "own"), None),
+            P("own", DP, None),
+            P("own", DP, None),
+            P("own", DP, None),
+            P("own", DP, None),
+            P("own", DP, None),
+            P(None, ("z", "xlo", "own"), None),
         ),
         check_vma=False,
     )

time: 429 us -> 320 us (0.75)
  blocking collectives: 293 us -> 25.2 us
  waiting for transfers between devices: 60.3 us -> 218 us
    psum x1, blocking collectives: 269 us -> 13.7 us  [per_device(): square_sums = lax.psum(square_sums, 'z')]
    psum x0 -> x1, waiting for transfers between devices: none -> 75.1 us  [dp_sum(): x = lax.psum(x, 'z')]
    all_gather x1 -> x2, waiting for transfers between devices: 0.01 us -> 42.6 us  [the longest x1 42.6 us: dp_sum(): return lax.all_gather(x, 'xlo', axis=1, tiled=True)]
    reduce_scatter x0 -> x1, waiting for transfers between devices: none -> 40.7 us  [dp_sum(): x = lax.psum_scatter(x, 'xlo', scatter_dimension=1, tiled=True)]
    psum x1, blocking collectives: 24.1 us -> 3.76 us  [per_device(): lax.psum((jnp.sum(adam_step * adam_step, axis=(1, 2)), jnp.sum(direction...]
    all_gather x0 -> x1, blocking collectives: none -> 7.78 us  [dp_gather(): x = lax.all_gather(x, 'xlo', axis=axis, tiled=True)]
    select_n x0 -> x1, other arithmetic: none -> 4.68 us  [per_device(): jnp.where(occupied[:, None, None], jnp.take(summed, block_of, axis=0), 0.0)]
  transfers between devices with their start and end apart: 3 -> 6, of which waited for: 2 -> 5; matrix products, arithmetic and copies ran while one was open for 5% -> 6% of each run, Pallas kernels for 0% -> 0%
where the time goes in v2:
time: 320 us
  waiting for transfers between devices  218 us (68%)
  starting transfers between devices  26.2 us (8%)
  blocking collectives  25.2 us (8%)
  matrix products  14.4 us (4%)
  between operations  13.9 us (4%)
  other arithmetic  12.5 us (4%)
  local copies, waits for them, and re-layouts  9.37 us (3%)
    psum x1, waiting for transfers between devices, dp_sum(): x = lax.psum(x, 'z')  75.1 us
    all_to_all x1, waiting for transfers between devices, per_device(): lax.all_to_all(packed, 'own', split_axis=0, concat_axis=2, tiled=True)  55.2 us
    all_gather x1, waiting for transfers between devices, dp_sum(): return lax.all_gather(x, 'xlo', axis=1, tiled=True)  42.6 us
    reduce_scatter x1, waiting for transfers between devices, dp_sum(): x = lax.psum_scatter(x, 'xlo', scatter_dimension=1, tiled=True)  40.7 us
    all_to_all x1, starting transfers between devices, per_device(): lax.all_to_all(shares, 'own', split_axis=1, concat_axis=0, tiled=True)  18 us
    psum x1, blocking collectives, per_device(): square_sums = lax.psum(square_sums, 'z')  13.7 us
    all_to_all x1, starting transfers between devices, per_device(): lax.all_to_all(packed, 'own', split_axis=0, concat_axis=2, tiled=True)  8.12 us
    dot_general x1, matrix products, per_device(): jnp.einsum('srk,skn->srn', root_left, product, preferred_element_type=jnp...  7.84 us
  transfers between devices with their start and end apart: 6, of which 5 were waited for; matrix products, arithmetic and copies ran while one was open for 6% of the time, Pallas kernels for 0%

profile of v2, /device:TPU:1, one launch (start us, length us, event | category | flops | bytes accessed | tf_op | source)
XLA Modules:
  0.0 319.6 jit_solution(1911710013704817737)
XLA Ops:
  7.2 3.9 %convert_bitcast_fusion = bf16[16,64,1024]{2,1,0:T(8,128)(2,1)} fusion(f32[1,16,64,1024]{3,2,1,0:T(8,128)} %param.9), kind=kLoop, calls=%fused_computation.5 | loop fusion | flops 1048576 | bytes 6291456 | tf_op jit(solution)/shard_map/convert_element_type | solution.py:48
  11.3 40.7 %reduce-scatter.2.cloned.1.call-done = bf16[16,32,1024]{2,1,0:T(8,128)(2,1)} async-done(((bf16[16,64,1024]{2,1,0:T(8,128)(2,1)}), bf16[16,32,1024]{2,1,0:T(8,128)(2,1)}) %reduce-scatter.2.cloned.1.call-update) | async-done | bytes 1048592 | tf_op jit(solution)/shard_map/reduce_scatter | solution.py:23
  52.0 75.1 %all-reduce.4.cloned.1.call-done = bf16[16,32,1024]{2,1,0:T(8,128)(2,1)} async-done(((bf16[16,32,1024]{2,1,0:T(8,128)(2,1)}), bf16[16,32,1024]{2,1,0:T(8,128)(2,1)}) %all-reduce.4.cloned.1.call-update) | async-done | bytes 1048592 | tf_op jit(solution)/shard_map/psum | solution.py:24
  127.2 42.6 %all-gather.3.cloned.1.call-done = bf16[16,64,1024]{2,1,0:T(8,128)(2,1)} async-done(((bf16[16,32,1024]{2,1,0:T(8,128)(2,1)}), bf16[16,64,1024]{2,1,0:T(8,128)(2,1)}) %all-gather.3.cloned.1.call-update) | async-done | bytes 2097168 | tf_op jit(solution)/shard_map/all_gather | solution.py:25
  169.8 7.8 %all_gather.10 = bf16[2,128,1024]{2,1,0:T(8,128)(2,1)} all-gather(bf16[2,64,1024]{2,1,0:T(8,128)(2,1)S(1)} %copy-done.7), channel_id=1, replica_groups=mesh['z'=8,'xlo'=2,'own'=16] {'xlo'}, dimensions={1}, use_global_device_ids=true | all-gather | bytes 786432 | tf_op jit(solution)/shard_map/all_gather | solution.py:18
  178.0 4.4 %gather_fusion = bf16[32,64,1024]{2,1,0:T(8,128)(2,1)} fusion(bf16[16,64,1024]{2,1,0:T(8,128)(2,1)} %all-gather.3.cloned.1.call-done, s32[1024]{0:T(1024)S(1)} %pad_clamp_fusion.1), kind=kCustom, calls=%fused_computation | custom fusion | bytes 8388736 | tf_op jit(solution)/shard_map/jit(_take)/gather | solution.py:50
  182.4 4.7 %select_select_fusion = bf16[16,2,64,1024]{3,2,1,0:T(8,128)(2,1)} fusion(bf16[16,2,64,1024]{3,2,1,0:T(8,128)(2,1)} %bitcast.31, pred[16,2]{1,0:T(8,128)(4,1)S(1)} %compare_and_fusion, pred[16,2]{1,0:T(8,128)(4,1)S(1)} %broadcast_in_dim.75), kind=kLoop, calls=%fused_computation.4 | loop fusion | flops 4194304 | bytes 8388672 | tf_op jit(solution)/shard_map/jit(_where)/select_n | solution.py:50
  187.1 8.1 %all-to-all-start = ((bf16[16,2,64,1024]{3,2,1,0:T(8,128)(2,1)}), bf16[16,2,64,1024]{3,2,1,0:T(8,128)(2,1)}, u32[]{:S(2)}, u32[]{:S(2)}) async-start(bf16[16,2,64,1024]{3,2,1,0:T(8,128)(2,1)} %select_select_fusion), calls=%async_computation.1 | async-start | bytes 8388608 | tf_op jit(solution)/shard_map/all_to_all | solution.py:52
  195.3 55.2 %all-to-all-done = bf16[16,2,64,1024]{3,2,1,0:T(8,128)(2,1)} async-done(((bf16[16,2,64,1024]{3,2,1,0:T(8,128)(2,1)}), bf16[16,2,64,1024]{3,2,1,0:T(8,128)(2,1)}, u32[]{:S(2)}, u32[]{:S(2)}) %all-to-all-start) | async-done | bytes 4194336 | tf_op jit(solution)/shard_map/all_to_all | solution.py:52
  250.5 2.7 copy.27
  253.3 1.9 fusion.10
  255.2 0.4 copy-done.1
  255.6 2.2 fusion.7
  257.8 7.8 %multiply_reduce_fusion = (f32[2]{0:T(128)S(1)}, f32[2,1024,64]{1,2,0:T(8,128)S(1)}) fusion(bf16[2,64,1024]{2,1,0:T(8,128)(2,1)S(1)} %copy-done, bf16[2,1024,1024]{2,1,0:T(8,128)(2,1)} %bitcast.29, bf16[2,1024,1024]{2,1,0:T(8,128)(2,1)} %all-gather.5.cloned.1.call-done), kind=kOutput, calls=%fused_computation.18 | convolution fusion | flops 4565762048 | bytes 9175048 | tf_op jit(solution)/shard_map/srk,skn->srn/dot_general | solution.py:71
  265.6 3.8 %all-reduce.1 = (f32[2]{0:T(128)S(1)}, f32[2]{0:T(128)S(1)}) all-reduce(f32[2]{0:T(128)S(1)} %get-tuple-element.19, f32[2]{0:T(128)S(1)} %get-tuple-element.15), channel_id=1, replica_groups=mesh['z'=8,'xlo'=2,'own'=16] {'xlo'}, use_global_device_ids=true, to_apply=%region_8.9 | all-reduce | flops 4 | bytes 32 | tf_op jit(solution)/shard_map/psum | solution.py:74
  269.4 13.7 %all-reduce = (f32[2]{0:T(128)S(1)}, f32[2]{0:T(128)S(1)}) all-reduce(f32[2]{0:T(128)S(1)} %get-tuple-element.12, f32[2]{0:T(128)S(1)} %get-tuple-element.13), channel_id=1, replica_groups=mesh['z'=8,'xlo'=2,'own'=16] {'z'}, use_global_device_ids=true, to_apply=%region_9.10 | all-reduce | flops 4 | bytes 32 | tf_op jit(solution)/shard_map/psum | solution.py:78
  283.1 1.0 fusion.13
  284.0 0.1 reshape.59
  284.2 0.8 copy.29
  285.0 18.0 %all-to-all-start.1 = ((bf16[2,16,4,1024]{3,2,0,1:T(4,128)(2,1)}), bf16[2,16,4,1024]{3,2,0,1:T(4,128)(2,1)S(1)}, u32[]{:S(2)}, u32[]{:S(2)}) async-start(bf16[2,16,4,1024]{3,2,0,1:T(4,128)(2,1)} %copy.29), calls=%async_computation.2 | async-start | bytes 524288 | tf_op jit(solution)/shard_map/all_to_all | solution.py:92
  302.9 4.3 %fusion.5 = f32[2,64,1024]{2,1,0:T(8,128)} fusion(f32[2,64,1024]{2,1,0:T(8,128)S(1)} %copy-done.2, bf16[2,1024,1024]{2,1,0:T(8,128)(2,1)} %bitcast.30, s32[]{:T(128)S(6)} %select_n.69, pred[2]{0:T(512)(128)(4,1)S(1)} %dynamic_slice.9), kind=kOutput, calls=%fused_computation.9 | convolution fusion | flops 268959744 | bytes 5767174 | tf_op jit(solution)/shard_map/skr,skn->srn/dot_general | solution.py:62
  307.3 4.4 %all-to-all-done.1 = bf16[2,16,4,1024]{3,2,0,1:T(4,128)(2,1)S(1)} async-done(((bf16[2,16,4,1024]{3,2,0,1:T(4,128)(2,1)}), bf16[2,16,4,1024]{3,2,0,1:T(4,128)(2,1)S(1)}, u32[]{:S(2)}, u32[]{:S(2)}) %all-to-all-start.1) | async-done | bytes 262176 | tf_op jit(solution)/shard_map/all_to_all | solution.py:92
  311.6 0.7 gather_fusion.1
  312.3 0.8 broadcast_select_fusion
  (38 shorter events, 0.7 us)
Async XLA Ops:
  7.2 250.6 %copy-start = (bf16[2,64,1024]{2,1,0:T(8,128)(2,1)S(1)}, bf16[2,64,1024]{2,1,0:T(8,128)(2,1)}, u32[]{:S(2)}) copy-start(bf16[2,64,1024]{2,1,0:T(8,128)(2,1)} %param.13) | copy-start | bytes 786436
  7.2 162.6 %copy-start.7 = (bf16[2,64,1024]{2,1,0:T(8,128)(2,1)S(1)}, bf16[2,64,1024]{2,1,0:T(8,128)(2,1)}, u32[]{:S(2)}) copy-start(bf16[2,64,1024]{2,1,0:T(8,128)(2,1)} %param.14) | copy-start | bytes 786436
  7.2 44.8 %reduce-scatter.2.cloned.1.call-start = ((), (), s32[]{:S(2)}) async-start(), calls=%async_computation.3 | async-start | bytes 3145728 | tf_op jit(solution)/shard_map/reduce_scatter | solution.py:23
  11.2 166.4 %copy-start.8 = (s32[16]{0:T(128)S(1)}, s32[16]{0:T(128)}, u32[]{:S(2)}) copy-start(s32[16]{0:T(128)} %param.10) | copy-start | bytes 196
  11.2 115.9 %all-reduce.4.cloned.1.call-start = ((), (), s32[]{:S(2)}) async-start(), calls=%async_computation.4 | async-start | bytes 2097152 | tf_op jit(solution)/shard_map/psum | solution.py:24
  52.0 117.8 %all-gather.3.cloned.1.call-start = ((), (), s32[]{:S(2)}) async-start(), calls=%async_computation.5 | async-start | bytes 3145728 | tf_op jit(solution)/shard_map/all_gather | solution.py:25
  127.1 130.6 %all-gather.5.cloned.1.call-start = ((), (), s32[]{:S(2)}) async-start(), calls=%async_computation.6 | async-start | bytes 4718592 | tf_op jit(solution)/shard_map/all_gather | solution.py:19
  187.1 63.4 %all-to-all-start = ((bf16[16,2,64,1024]{3,2,1,0:T(8,128)(2,1)}), bf16[16,2,64,1024]{3,2,1,0:T(8,128)(2,1)}, u32[]{:S(2)}, u32[]{:S(2)}) async-start(bf16[16,2,64,1024]{3,2,1,0:T(8,128)(2,1)} %select_select_fusion), calls=%async_computation.1 | async-start | bytes 8388608 | tf_op jit(solution)/shard_map/all_to_all | solution.py:52
  250.5 2.8 copy-start.3
  250.5 2.8 copy-start.4
  250.5 5.0 %copy-start.5 = (f32[2,64,1024]{2,1,0:T(8,128)S(1)}, f32[2,64,1024]{2,1,0:T(8,128)}, u32[]{:S(2)}) copy-start(f32[2,64,1024]{2,1,0:T(8,128)} %param.11) | copy-start | bytes 1572868
  253.3 2.3 copy-start.1
  257.8 25.3 %copy-start.6 = (f32[2,64,1024]{2,1,0:T(8,128)S(1)}, f32[2,64,1024]{2,1,0:T(8,128)}, u32[]{:S(2)}) copy-start(f32[2,64,1024]{2,1,0:T(8,128)} %param.15) | copy-start | bytes 1572868
  257.8 45.2 %copy-start.2 = (f32[2,64,1024]{2,1,0:T(8,128)S(1)}, f32[2,64,1024]{2,1,0:T(8,128)}, u32[]{:S(2)}) copy-start(f32[2,64,1024]{2,1,0:T(8,128)} %param.12) | copy-start | bytes 1572868
  285.0 26.7 %all-to-all-start.1 = ((bf16[2,16,4,1024]{3,2,0,1:T(4,128)(2,1)}), bf16[2,16,4,1024]{3,2,0,1:T(4,128)(2,1)S(1)}, u32[]{:S(2)}, u32[]{:S(2)}) async-start(bf16[2,16,4,1024]{3,2,0,1:T(4,128)(2,1)} %copy.29), calls=%async_computation.2 | async-start | bytes 524288 | tf_op jit(solution)/shard_map/all_to_all | solution.py:92
Sparse Core Ops, SparseCore 0:
  11.3 40.5 reduce-scatter.1
  54.3 72.7 all-reduce.3
  128.9 40.8 all-gather.2
  177.7 56.5 all-gather.4

commit v3 on v2

--- a/solution.py
+++ b/solution.py
@@ -20,9 +20,11 @@
 
 
 def dp_sum(x):
-    x = lax.psum_scatter(x, "xlo", scatter_dimension=1, tiled=True)
-    x = lax.psum(x, "z")
-    return lax.all_gather(x, "xlo", axis=1, tiled=True)
+    sources = lax.axis_size("z") * lax.axis_size("xlo")
+    x = x.reshape(x.shape[0], sources, x.shape[1] // sources, x.shape[2])
+    x = lax.all_to_all(x, DP, 1, 1, tiled=True)
+    x = jnp.sum(x.astype(jnp.float32), axis=1)
+    return dp_gather(x.astype(jnp.bfloat16), 1)
 
 
 def per_device(

time: 320 us -> 269 us (0.84)
  waiting for transfers between devices: 218 us -> 97 us
  blocking collectives: 25.2 us -> 86 us
  local copies, waits for them, and re-layouts: 9.37 us -> 16.5 us
  starting transfers between devices: 26.2 us -> 30.8 us
    psum x1 -> x0, waiting for transfers between devices: 75.1 us -> none  [dp_sum(): x = lax.psum(x, 'z')]
    all_to_all x0 -> x1, blocking collectives: none -> 59.3 us  [dp_sum(): x = lax.all_to_all(x, DP, 1, 1, tiled=True)]
    all_gather x1 -> x0, waiting for transfers between devices: 42.6 us -> none  [dp_sum(): return lax.all_gather(x, 'xlo', axis=1, tiled=True)]
    reduce_scatter x1 -> x0, waiting for transfers between devices: 40.7 us -> none  [dp_sum(): x = lax.psum_scatter(x, 'xlo', scatter_dimension=1, tiled=True)]
    all_gather x1 -> x2, waiting for transfers between devices: 0.01 us -> 37.3 us  [dp_gather(): return lax.all_gather(x, 'z', axis=axis, tiled=True)]
    all_to_all x1, starting transfers between devices: 8.12 us -> 12.7 us  [per_device(): lax.all_to_all(packed, 'own', split_axis=0, concat_axis=2, tiled=True)]
    unnamed x18 -> x19, local copies, waits for them, and re-layouts: 0.4 us -> 4.84 us
    convert_element_type x1 -> x0, other arithmetic: 3.94 us -> none  [per_device(): summed = dp_sum(grads[0].astype(jnp.bfloat16))]
  transfers between devices with their start and end apart: 6 -> 4, of which waited for: 5 -> 3; matrix products, arithmetic and copies ran while one was open for 6% -> 8% of each run, Pallas kernels for 0% -> 0%
where the time goes in v3:
time: 269 us; the launch traced here: 268 us
  waiting for transfers between devices  97 us (36%)
  blocking collectives  86 us (32%)
  starting transfers between devices  30.8 us (11%)
  local copies, waits for them, and re-layouts  16.5 us (6%)
  matrix products  14.4 us (5%)
  between operations  14.2 us (5%)
  other arithmetic  9.5 us (4%)
    all_to_all x1, blocking collectives, dp_sum(): x = lax.all_to_all(x, DP, 1, 1, tiled=True)  59.3 us
    all_to_all x1, waiting for transfers between devices, per_device(): lax.all_to_all(packed, 'own', split_axis=0, concat_axis=2, tiled=True)  55.2 us
    all_gather x2, waiting for transfers between devices, dp_gather(): return lax.all_gather(x, 'z', axis=axis, tiled=True)  37.3 us
    all_to_all x1, starting transfers between devices, per_device(): lax.all_to_all(shares, 'own', split_axis=1, concat_axis=0, tiled=True)  18 us
    all_to_all x1, starting transfers between devices, per_device(): lax.all_to_all(packed, 'own', split_axis=0, concat_axis=2, tiled=True)  12.7 us
    psum x1, blocking collectives, per_device(): square_sums = lax.psum(square_sums, 'z')  12.4 us
    all_gather x2, blocking collectives, dp_gather(): x = lax.all_gather(x, 'xlo', axis=axis, tiled=True)  10.5 us
    dot_general x1, matrix products, per_device(): jnp.einsum('srk,skn->srn', root_left, product, preferred_element_type=jnp...  7.84 us
  transfers between devices with their start and end apart: 4, of which 3 were waited for; matrix products, arithmetic and copies ran while one was open for 8% of the time, Pallas kernels for 0%

profile of v3, /device:TPU:1, one launch (start us, length us, event | category | flops | bytes accessed | tf_op | source)
XLA Modules:
  0.0 268.3 jit_solution(14365797323781383230)
XLA Ops:
  7.2 4.5 %copy.46 = bf16[1,16,64,1024]{3,1,2,0:T(8,128)(2,1)S(1)} copy(f32[1,16,64,1024]{3,2,1,0:T(8,128)} %param.9) | data formatting | bytes 6291456 | tf_op args[0]
  11.7 1.8 copy.38
  13.5 59.3 %all_to_all.35 = bf16[16,16,4,1024]{3,2,0,1:T(4,128)(2,1)S(1)} all-to-all(bf16[16,16,4,1024]{3,2,0,1:T(4,128)(2,1)S(1)} %copy.38), channel_id=1, replica_groups=mesh['z'=8,'xlo'=2,'own'=16] {'z','xlo'}, dimensions={1} | all-to-all | bytes 4194304 | tf_op jit(solution)/shard_map/all_to_all | solution.py:25
  72.8 1.0 reduce_sum.45
  73.9 4.5 %all_gather.12 = bf16[16,8,1024]{2,0,1:T(8,128)(2,1)S(1)} all-gather(bf16[16,4,1024]{2,0,1:T(8,128)(2,1)S(1)} %copy.39), channel_id=1, replica_groups=mesh['z'=8,'xlo'=2,'own'=16] {'xlo'}, dimensions={1}, use_global_device_ids=true | all-gather | bytes 393216 | tf_op jit(solution)/shard_map/all_gather | solution.py:18
  78.3 0.9 copy.40
  79.3 37.3 %all-gather.3.cloned.1.call-done = bf16[16,64,1024]{2,1,0:T(8,128)(2,1)} async-done(((bf16[16,8,1024]{2,1,0:T(8,128)(2,1)}), bf16[16,64,1024]{2,1,0:T(8,128)(2,1)}) %all-gather.3.cloned.1.call-update) | async-done | bytes 2097168 | tf_op jit(solution)/shard_map/all_gather | solution.py:19
  116.6 6.0 %all_gather.14 = bf16[2,128,1024]{2,1,0:T(8,128)(2,1)} all-gather(bf16[2,64,1024]{2,1,0:T(8,128)(2,1)S(1)} %copy-done.7), channel_id=1, replica_groups=mesh['z'=8,'xlo'=2,'own'=16] {'xlo'}, dimensions={1}, use_global_device_ids=true | all-gather | bytes 786432 | tf_op jit(solution)/shard_map/all_gather | solution.py:18
  123.0 4.4 %gather_fusion = bf16[32,64,1024]{2,1,0:T(8,128)(2,1)} fusion(bf16[16,64,1024]{2,1,0:T(8,128)(2,1)} %all-gather.3.cloned.1.call-done, s32[1024]{0:T(1024)S(1)} %pad_clamp_fusion.1), kind=kCustom, calls=%fused_computation | custom fusion | bytes 8388736 | tf_op jit(solution)/shard_map/jit(_take)/gather | solution.py:52
  127.4 4.7 %select_select_fusion = bf16[16,2,64,1024]{3,2,1,0:T(8,128)(2,1)} fusion(bf16[16,2,64,1024]{3,2,1,0:T(8,128)(2,1)} %bitcast.30, pred[16,2]{1,0:T(8,128)(4,1)S(1)} %compare_and_fusion, pred[16,2]{1,0:T(8,128)(4,1)S(1)} %broadcast_in_dim.75), kind=kLoop, calls=%fused_computation.5 | loop fusion | flops 4194304 | bytes 8388672 | tf_op jit(solution)/shard_map/jit(_where)/select_n | solution.py:52
  132.1 12.7 %all-to-all-start.1 = ((bf16[16,2,64,1024]{3,2,1,0:T(8,128)(2,1)}), bf16[16,2,64,1024]{3,2,1,0:T(8,128)(2,1)}, u32[]{:S(2)}, u32[]{:S(2)}) async-start(bf16[16,2,64,1024]{3,2,1,0:T(8,128)(2,1)} %select_select_fusion), calls=%async_computation.1 | async-start | bytes 8388608 | tf_op jit(solution)/shard_map/all_to_all | solution.py:54
  144.9 55.2 %all-to-all-done.1 = bf16[16,2,64,1024]{3,2,1,0:T(8,128)(2,1)} async-done(((bf16[16,2,64,1024]{3,2,1,0:T(8,128)(2,1)}), bf16[16,2,64,1024]{3,2,1,0:T(8,128)(2,1)}, u32[]{:S(2)}, u32[]{:S(2)}) %all-to-all-start.1) | async-done | bytes 4194336 | tf_op jit(solution)/shard_map/all_to_all | solution.py:54
  200.1 2.7 %copy.41 = bf16[1,2,16,64,1024]{4,3,2,1,0:T(8,128)(2,1)S(1)} copy(bf16[1,2,16,64,1024]{4,3,1,2,0:T(8,128)(2,1)} %bitcast.5) | data formatting | bytes 8388608 | tf_op jit(solution)/shard_map/all_to_all | solution.py:54
  202.9 1.9 fusion.10
  205.2 2.2 fusion.7
  207.4 7.8 %multiply_reduce_fusion = (f32[2]{0:T(128)S(1)}, f32[2,1024,64]{1,2,0:T(8,128)S(1)}) fusion(bf16[2,64,1024]{2,1,0:T(8,128)(2,1)S(1)} %copy-done, bf16[2,1024,1024]{2,1,0:T(8,128)(2,1)} %bitcast.28, bf16[2,1024,1024]{2,1,0:T(8,128)(2,1)} %all-gather.5.cloned.1.call-done), kind=kOutput, calls=%fused_computation.18 | convolution fusion | flops 4565762048 | bytes 9175048 | tf_op jit(solution)/shard_map/srk,skn->srn/dot_general | solution.py:73
  215.2 3.8 %all-reduce.1 = (f32[2]{0:T(128)S(1)}, f32[2]{0:T(128)S(1)}) all-reduce(f32[2]{0:T(128)S(1)} %get-tuple-element.19, f32[2]{0:T(128)S(1)} %get-tuple-element.15), channel_id=1, replica_groups=mesh['z'=8,'xlo'=2,'own'=16] {'xlo'}, use_global_device_ids=true, to_apply=%region_7.8 | all-reduce | flops 4 | bytes 32 | tf_op jit(solution)/shard_map/psum | solution.py:76
  219.0 12.4 %all-reduce = (f32[2]{0:T(128)S(1)}, f32[2]{0:T(128)S(1)}) all-reduce(f32[2]{0:T(128)S(1)} %get-tuple-element.12, f32[2]{0:T(128)S(1)} %get-tuple-element.13), channel_id=1, replica_groups=mesh['z'=8,'xlo'=2,'own'=16] {'z'}, use_global_device_ids=true, to_apply=%region_8.9 | all-reduce | flops 4 | bytes 32 | tf_op jit(solution)/shard_map/psum | solution.py:80
  231.4 1.0 fusion.13
  232.5 0.8 copy.43
  233.3 18.0 %all-to-all-start.2 = ((bf16[2,16,4,1024]{3,2,0,1:T(4,128)(2,1)}), bf16[2,16,4,1024]{3,2,0,1:T(4,128)(2,1)S(1)}, u32[]{:S(2)}, u32[]{:S(2)}) async-start(bf16[2,16,4,1024]{3,2,0,1:T(4,128)(2,1)} %copy.43), calls=%async_computation.2 | async-start | bytes 524288 | tf_op jit(solution)/shard_map/all_to_all | solution.py:94
  251.3 4.3 %fusion.5 = f32[2,64,1024]{2,1,0:T(8,128)} fusion(f32[2,64,1024]{2,1,0:T(8,128)S(1)} %copy-done.2, bf16[2,1024,1024]{2,1,0:T(8,128)(2,1)} %bitcast.29, s32[]{:T(128)S(6)} %select_n.69, pred[2]{0:T(512)(128)(4,1)S(1)} %dynamic_slice.9), kind=kOutput, calls=%fused_computation.9 | convolution fusion | flops 268959744 | bytes 5767174 | tf_op jit(solution)/shard_map/skr,skn->srn/dot_general | solution.py:64
  255.6 4.4 %all-to-all-done.2 = bf16[2,16,4,1024]{3,2,0,1:T(4,128)(2,1)S(1)} async-done(((bf16[2,16,4,1024]{3,2,0,1:T(4,128)(2,1)}), bf16[2,16,4,1024]{3,2,0,1:T(4,128)(2,1)S(1)}, u32[]{:S(2)}, u32[]{:S(2)}) %all-to-all-start.2) | async-done | bytes 262176 | tf_op jit(solution)/shard_map/all_to_all | solution.py:94
  260.6 0.8 broadcast_select_fusion
  (38 shorter events, 1.8 us)
Async XLA Ops:
  7.2 200.2 %copy-start = (bf16[2,64,1024]{2,1,0:T(8,128)(2,1)S(1)}, bf16[2,64,1024]{2,1,0:T(8,128)(2,1)}, u32[]{:S(2)}) copy-start(bf16[2,64,1024]{2,1,0:T(8,128)(2,1)} %param.13) | copy-start | bytes 786436
  7.2 109.4 %all-gather.3.cloned.1.call-start = ((), (), s32[]{:S(2)}) async-start(), calls=%async_computation.3 | async-start | bytes 2359296 | tf_op jit(solution)/shard_map/all_gather | solution.py:19
  13.5 103.2 %copy-start.7 = (bf16[2,64,1024]{2,1,0:T(8,128)(2,1)S(1)}, bf16[2,64,1024]{2,1,0:T(8,128)(2,1)}, u32[]{:S(2)}) copy-start(bf16[2,64,1024]{2,1,0:T(8,128)(2,1)} %param.14) | copy-start | bytes 786436
  13.5 109.1 %copy-start.8 = (s32[16]{0:T(128)S(1)}, s32[16]{0:T(128)}, u32[]{:S(2)}) copy-start(s32[16]{0:T(128)} %param.10) | copy-start | bytes 196
  79.2 128.1 %all-gather.5.cloned.1.call-start = ((), (), s32[]{:S(2)}) async-start(), calls=%async_computation.4 | async-start | bytes 4718592 | tf_op jit(solution)/shard_map/all_gather | solution.py:19
  132.1 68.1 %all-to-all-start.1 = ((bf16[16,2,64,1024]{3,2,1,0:T(8,128)(2,1)}), bf16[16,2,64,1024]{3,2,1,0:T(8,128)(2,1)}, u32[]{:S(2)}, u32[]{:S(2)}) async-start(bf16[16,2,64,1024]{3,2,1,0:T(8,128)(2,1)} %select_select_fusion), calls=%async_computation.1 | async-start | bytes 8388608 | tf_op jit(solution)/shard_map/all_to_all | solution.py:54
  200.1 2.8 %copy-start.3 = (f32[2,64,1024]{2,1,0:T(8,128)S(1)}, f32[2,64,1024]{2,1,0:T(8,128)}, u32[]{:S(2)}) copy-start(f32[2,64,1024]{2,1,0:T(8,128)} %param.17) | copy-start | bytes 1572868
  200.1 2.8 %copy-start.4 = (f32[2,64,1024]{2,1,0:T(8,128)S(1)}, f32[2,64,1024]{2,1,0:T(8,128)}, u32[]{:S(2)}) copy-start(f32[2,64,1024]{2,1,0:T(8,128)} %param.16) | copy-start | bytes 1572868
  200.1 5.0 %copy-start.5 = (f32[2,64,1024]{2,1,0:T(8,128)S(1)}, f32[2,64,1024]{2,1,0:T(8,128)}, u32[]{:S(2)}) copy-start(f32[2,64,1024]{2,1,0:T(8,128)} %param.11) | copy-start | bytes 1572868
  202.9 2.3 copy-start.1
  207.4 24.1 %copy-start.6 = (f32[2,64,1024]{2,1,0:T(8,128)S(1)}, f32[2,64,1024]{2,1,0:T(8,128)}, u32[]{:S(2)}) copy-start(f32[2,64,1024]{2,1,0:T(8,128)} %param.15) | copy-start | bytes 1572868
  207.4 43.9 %copy-start.2 = (f32[2,64,1024]{2,1,0:T(8,128)S(1)}, f32[2,64,1024]{2,1,0:T(8,128)}, u32[]{:S(2)}) copy-start(f32[2,64,1024]{2,1,0:T(8,128)} %param.12) | copy-start | bytes 1572868
  233.3 26.7 %all-to-all-start.2 = ((bf16[2,16,4,1024]{3,2,0,1:T(4,128)(2,1)}), bf16[2,16,4,1024]{3,2,0,1:T(4,128)(2,1)S(1)}, u32[]{:S(2)}, u32[]{:S(2)}) async-start(bf16[2,16,4,1024]{3,2,0,1:T(4,128)(2,1)} %copy.43), calls=%async_computation.2 | async-start | bytes 524288 | tf_op jit(solution)/shard_map/all_to_all | solution.py:94
Sparse Core Ops, SparseCore 0:
  79.3 37.2 all-gather.2
  122.7 58.4 all-gather.4

commit v4 on v3

--- a/solution.py
+++ b/solution.py
@@ -21,10 +21,9 @@
 
 def dp_sum(x):
     sources = lax.axis_size("z") * lax.axis_size("xlo")
-    x = x.reshape(x.shape[0], sources, x.shape[1] // sources, x.shape[2])
-    x = lax.all_to_all(x, DP, 1, 1, tiled=True)
-    x = jnp.sum(x.astype(jnp.float32), axis=1)
-    return dp_gather(x.astype(jnp.bfloat16), 1)
+    x = x.reshape(sources, x.shape[0] // sources, *x.shape[1:])
+    x = lax.all_to_all(x, DP, 0, 0, tiled=True)
+    return jnp.sum(x.astype(jnp.float32), axis=0).astype(jnp.bfloat16)
 
 
 def per_device(
@@ -47,11 +46,19 @@
     matches = owner_map[:, None] == jnp.arange(owned_slots, dtype=jnp.int32)[None, :]
     occupied = jnp.any(matches, axis=0)
     block_of = jnp.sum(jnp.where(matches, jnp.arange(blocks, dtype=jnp.int32)[:, None], 0), axis=0)
-    summed = dp_sum(grads[0].astype(jnp.bfloat16))
-    summed, root_right = lax.optimization_barrier((summed, root_right))
-    packed = jnp.where(occupied[:, None, None], jnp.take(summed, block_of, axis=0), 0.0)
-    packed = packed.reshape(owners, slot_count, summed.shape[1], order_size)
-    arrived = lax.all_to_all(packed, "own", split_axis=0, concat_axis=2, tiled=True)
+    mine = dp_sum(grads[0].astype(jnp.bfloat16))
+    chunks = 2
+    width = rows_dev // chunks
+    arrived = []
+    for c in range(chunks):
+        summed = dp_gather(mine[:, c * width:(c + 1) * width], 0)
+        if c == chunks - 1:
+            summed, root_right = lax.optimization_barrier((summed, root_right))
+        packed = jnp.where(occupied[:, None, None], jnp.take(summed, block_of, axis=0), 0.0)
+        packed = packed.reshape(owners, slot_count, width, order_size)
+        piece = lax.all_to_all(packed, "own", split_axis=0, concat_axis=2, tiled=True)
+        arrived.append(piece.reshape(slot_count, owners, width, order_size))
+    arrived = jnp.stack(arrived, axis=2)
     right_full = dp_gather(root_right, 1)
     first_row = dp_index() * rows_dev
     rounded = arrived.reshape(slot_count, order_size, order_size)

time: 269 us -> 288 us (1.071)
  blocking collectives: 86 us -> 129 us
  starting transfers between devices: 30.8 us -> 17.1 us
  local copies, waits for them, and re-layouts: 16.5 us -> 8.03 us
  waiting for transfers between devices: 97 us -> 93 us
    all_to_all x1 -> x2, blocking collectives: 59.3 us -> 99.6 us  [the longest x1 59.3 us: dp_sum(): x = lax.all_to_all(x, DP, 0, 0, tiled=True)]
    all_to_all x1, waiting for transfers between devices: 55.2 us -> 28.4 us  [per_device(): lax.all_to_all(packed, 'own', split_axis=0, concat_axis=2, tiled=True)]
    all_gather x2 -> x3, waiting for transfers between devices: 37.3 us -> 60.1 us  [dp_gather(): return lax.all_gather(x, 'z', axis=axis, tiled=True)]
    all_to_all x1, starting transfers between devices: 12.7 us -> 5.43 us  [per_device(): lax.all_to_all(packed, 'own', split_axis=0, concat_axis=2, tiled=True)]
    all_to_all x1, starting transfers between devices: 18 us -> 11.6 us  [per_device(): lax.all_to_all(shares, 'own', split_axis=1, concat_axis=0, tiled=True)]
    unnamed x19 -> x18, local copies, waits for them, and re-layouts: 4.84 us -> 0.4 us
    all_gather x2 -> x3, blocking collectives: 10.5 us -> 13.8 us  [dp_gather(): x = lax.all_gather(x, 'xlo', axis=axis, tiled=True)]
  transfers between devices with their start and end apart: 4 -> 5, of which waited for: 3 -> 4; matrix products, arithmetic and copies ran while one was open for 8% -> 7% of each run, Pallas kernels for 0% -> 0%
where the time goes in v4:
time: 288 us
  blocking collectives  129 us (45%)
  waiting for transfers between devices  93 us (32%)
  starting transfers between devices  17.1 us (6%)
  matrix products  14.4 us (5%)
  between operations  13.9 us (5%)
  other arithmetic  12.3 us (4%)
  local copies, waits for them, and re-layouts  8.03 us (3%)
    all_gather x3, waiting for transfers between devices, dp_gather(): return lax.all_gather(x, 'z', axis=axis, tiled=True)  60.1 us
    all_to_all x1, blocking collectives, dp_sum(): x = lax.all_to_all(x, DP, 0, 0, tiled=True)  59.3 us
    all_to_all x1, blocking collectives, per_device(): lax.all_to_all(packed, 'own', split_axis=0, concat_axis=2, tiled=True)  40.2 us
    all_to_all x1, waiting for transfers between devices, per_device(): lax.all_to_all(packed, 'own', split_axis=0, concat_axis=2, tiled=True)  28.4 us
    all_gather x3, blocking collectives, dp_gather(): x = lax.all_gather(x, 'xlo', axis=axis, tiled=True)  13.8 us
    psum x1, blocking collectives, per_device(): square_sums = lax.psum(square_sums, 'z')  11.9 us
    all_to_all x1, starting transfers between devices, per_device(): lax.all_to_all(shares, 'own', split_axis=1, concat_axis=0, tiled=True)  11.6 us
    dot_general x1, matrix products, per_device(): jnp.einsum('srk,skn->srn', root_left, product, preferred_element_type=jnp...  7.84 us
  transfers between devices with their start and end apart: 5, of which 4 were waited for; matrix products, arithmetic and copies ran while one was open for 7% of the time, Pallas kernels for 0%

profile of v4, /device:TPU:1, one launch (start us, length us, event | category | flops | bytes accessed | tf_op | source)
XLA Modules:
  0.0 287.7 jit_solution(7217019842211925006)
XLA Ops:
  7.2 2.5 convert_bitcast_fusion
  9.8 59.3 %all_to_all.50 = bf16[16,1,64,1024]{3,2,1,0:T(8,128)(2,1)S(1)} all-to-all(bf16[16,1,64,1024]{3,2,1,0:T(8,128)(2,1)S(1)} %convert_bitcast_fusion), channel_id=1, replica_groups=mesh['z'=8,'xlo'=2,'own'=16] {'z','xlo'}, dimensions={0} | all-to-all | bytes 4194304 | tf_op jit(solution)/shard_map/all_to_all | solution.py:25
  69.6 3.9 %all_gather.20 = bf16[2,32,1024]{2,1,0:T(8,128)(2,1)} all-gather(bf16[1,32,1024]{2,1,0:T(8,128)(2,1)S(1)} %get-tuple-element.21), channel_id=1, replica_groups=mesh['z'=8,'xlo'=2,'own'=16] {'xlo'}, dimensions={0}, use_global_device_ids=true | all-gather | bytes 196608 | tf_op jit(solution)/shard_map/all_gather | solution.py:18
  73.5 3.9 %all_gather.18 = bf16[2,32,1024]{2,1,0:T(8,128)(2,1)} all-gather(bf16[1,32,1024]{2,1,0:T(8,128)(2,1)S(1)} %get-tuple-element.20), channel_id=1, replica_groups=mesh['z'=8,'xlo'=2,'own'=16] {'xlo'}, dimensions={0}, use_global_device_ids=true | all-gather | bytes 196608 | tf_op jit(solution)/shard_map/all_gather | solution.py:18
  77.5 29.6 %all-gather.6.cloned.1.call-done = bf16[16,32,1024]{2,1,0:T(8,128)(2,1)} async-done(((bf16[2,32,1024]{2,1,0:T(8,128)(2,1)}), bf16[16,32,1024]{2,1,0:T(8,128)(2,1)}) %all-gather.6.cloned.1.call-update) | async-done | bytes 1048592 | tf_op jit(solution)/shard_map/all_gather | solution.py:19
  107.1 6.0 %all_gather.22 = bf16[2,128,1024]{2,1,0:T(8,128)(2,1)} all-gather(bf16[2,64,1024]{2,1,0:T(8,128)(2,1)S(1)} %copy-done.7), channel_id=1, replica_groups=mesh['z'=8,'xlo'=2,'own'=16] {'xlo'}, dimensions={1}, use_global_device_ids=true | all-gather | bytes 786432 | tf_op jit(solution)/shard_map/all_gather | solution.py:18
  113.4 1.9 gather_fusion.2
  115.3 30.5 %all-gather.4.cloned.1.call-done = bf16[16,32,1024]{2,1,0:T(8,128)(2,1)} async-done(((bf16[2,32,1024]{2,1,0:T(8,128)(2,1)}), bf16[16,32,1024]{2,1,0:T(8,128)(2,1)}) %all-gather.4.cloned.1.call-update) | async-done | bytes 1048592 | tf_op jit(solution)/shard_map/all_gather | solution.py:19
  145.8 3.3 %gather_fusion.1 = bf16[32,32,1024]{2,1,0:T(8,128)(2,1)} fusion(bf16[16,32,1024]{2,1,0:T(8,128)(2,1)} %all-gather.4.cloned.1.call-done, s32[1024]{0:T(1024)S(1)} %pad_clamp_fusion.1), kind=kCustom, calls=%fused_computation.clone | custom fusion | bytes 4194432 | tf_op jit(solution)/shard_map/jit(_take)/gather | solution.py:57
  149.0 3.5 %select_select_fusion.1 = (bf16[32,32,1024]{2,1,0:T(8,128)(2,1)}, bf16[32,32,1024]{2,1,0:T(8,128)(2,1)S(1)}) fusion(bf16[32,32,1024]{2,1,0:T(8,128)(2,1)} %gather_fusion.1, pred[32]{0:T(512)(128)(4,1)S(1)} %compare_and_fusion, pred[32]{0:T(512)(128)(4,1)S(1)} %fusion.16, bf16[32,32,1024]{2,1,0:T(8,128)(2,1)S(1)} %gather_fusion.2), kind=kLoop, calls=%fused_computation.7 | loop fusion | flops 4194304 | bytes 8388672 | tf_op jit(solution)/shard_map/jit(_where)/select_n | solution.py:57
  152.5 40.2 %all_to_all.51 = bf16[16,2,32,1024]{3,2,1,0:T(8,128)(2,1)S(1)} all-to-all(bf16[16,2,32,1024]{3,2,1,0:T(8,128)(2,1)S(1)} %bitcast.36), channel_id=1, replica_groups=mesh['z'=8,'xlo'=2,'own'=16] {'own'}, dimensions={0} | all-to-all | bytes 4194304 | tf_op jit(solution)/shard_map/all_to_all | solution.py:59
  192.7 5.4 %all-to-all-start.1 = ((bf16[16,2,32,1024]{3,2,1,0:T(8,128)(2,1)}), bf16[16,2,32,1024]{3,2,1,0:T(8,128)(2,1)}, u32[]{:S(2)}, u32[]{:S(2)}) async-start(bf16[16,2,32,1024]{3,2,1,0:T(8,128)(2,1)} %bitcast.2), calls=%async_computation.1 | async-start | bytes 4194304 | tf_op jit(solution)/shard_map/all_to_all | solution.py:59
  198.2 28.4 %all-to-all-done.1 = bf16[16,2,32,1024]{3,2,1,0:T(8,128)(2,1)} async-done(((bf16[16,2,32,1024]{3,2,1,0:T(8,128)(2,1)}), bf16[16,2,32,1024]{3,2,1,0:T(8,128)(2,1)}, u32[]{:S(2)}, u32[]{:S(2)}) %all-to-all-start.1) | async-done | bytes 2097184 | tf_op jit(solution)/shard_map/all_to_all | solution.py:59
  226.7 2.0 pad_maximum_fusion
  229.9 2.0 fusion.10
  231.9 2.2 fusion.7
  234.1 7.8 %multiply_reduce_fusion = (f32[2]{0:T(128)S(1)}, f32[2,1024,64]{1,2,0:T(8,128)S(1)}) fusion(bf16[2,64,1024]{2,1,0:T(8,128)(2,1)S(1)} %copy-done, bf16[2,1024,1024]{2,1,0:T(8,128)(2,1)} %bitcast.34, bf16[2,1024,1024]{2,1,0:T(8,128)(2,1)} %all-gather.8.cloned.1.call-done), kind=kOutput, calls=%fused_computation.21 | convolution fusion | flops 4565762048 | bytes 9175048 | tf_op jit(solution)/shard_map/srk,skn->srn/dot_general | solution.py:80
  241.9 3.8 %all-reduce.1 = (f32[2]{0:T(128)S(1)}, f32[2]{0:T(128)S(1)}) all-reduce(f32[2]{0:T(128)S(1)} %get-tuple-element.24, f32[2]{0:T(128)S(1)} %get-tuple-element.16), channel_id=1, replica_groups=mesh['z'=8,'xlo'=2,'own'=16] {'xlo'}, use_global_device_ids=true, to_apply=%region_7.9 | all-reduce | flops 4 | bytes 32 | tf_op jit(solution)/shard_map/psum | solution.py:83
  245.7 11.9 %all-reduce = (f32[2]{0:T(128)S(1)}, f32[2]{0:T(128)S(1)}) all-reduce(f32[2]{0:T(128)S(1)} %get-tuple-element.13, f32[2]{0:T(128)S(1)} %get-tuple-element.14), channel_id=1, replica_groups=mesh['z'=8,'xlo'=2,'own'=16] {'z'}, use_global_device_ids=true, to_apply=%region_8.10 | all-reduce | flops 4 | bytes 32 | tf_op jit(solution)/shard_map/psum | solution.py:87
  257.6 1.0 fusion.13
  258.6 0.8 copy.24
  259.5 11.6 %all-to-all-start.3 = ((bf16[2,16,4,1024]{3,2,0,1:T(4,128)(2,1)}), bf16[2,16,4,1024]{3,2,0,1:T(4,128)(2,1)S(1)}, u32[]{:S(2)}, u32[]{:S(2)}) async-start(bf16[2,16,4,1024]{3,2,0,1:T(4,128)(2,1)} %copy.24), calls=%async_computation.3 | async-start | bytes 524288 | tf_op jit(solution)/shard_map/all_to_all | solution.py:101
  271.0 4.3 %fusion.5 = f32[2,64,1024]{2,1,0:T(8,128)} fusion(f32[2,64,1024]{2,1,0:T(8,128)S(1)} %copy-done.2, bf16[2,1024,1024]{2,1,0:T(8,128)(2,1)} %bitcast.35, s32[]{:T(128)S(6)} %select_n.54, pred[2]{0:T(512)(128)(4,1)S(1)} %dynamic_slice.9), kind=kOutput, calls=%fused_computation.12 | convolution fusion | flops 268959744 | bytes 5767174 | tf_op jit(solution)/shard_map/skr,skn->srn/dot_general | solution.py:71
  275.4 4.4 %all-to-all-done.3 = bf16[2,16,4,1024]{3,2,0,1:T(4,128)(2,1)S(1)} async-done(((bf16[2,16,4,1024]{3,2,0,1:T(4,128)(2,1)}), bf16[2,16,4,1024]{3,2,0,1:T(4,128)(2,1)S(1)}, u32[]{:S(2)}, u32[]{:S(2)}) %all-to-all-start.3) | async-done | bytes 262176 | tf_op jit(solution)/shard_map/all_to_all | solution.py:101
  (41 shorter events, 3.6 us)
Async XLA Ops:
  7.2 226.9 %copy-start = (bf16[2,64,1024]{2,1,0:T(8,128)(2,1)S(1)}, bf16[2,64,1024]{2,1,0:T(8,128)(2,1)}, u32[]{:S(2)}) copy-start(bf16[2,64,1024]{2,1,0:T(8,128)(2,1)} %param.15) | copy-start | bytes 786436
  7.2 99.9 %all-gather.6.cloned.1.call-start = ((), (), s32[]{:S(2)}) async-start(), calls=%async_computation.5 | async-start | bytes 1179648 | tf_op jit(solution)/shard_map/all_gather | solution.py:19
  9.8 97.4 %copy-start.7 = (bf16[2,64,1024]{2,1,0:T(8,128)(2,1)S(1)}, bf16[2,64,1024]{2,1,0:T(8,128)(2,1)}, u32[]{:S(2)}) copy-start(bf16[2,64,1024]{2,1,0:T(8,128)(2,1)} %param.16) | copy-start | bytes 786436
  9.8 103.4 %copy-start.8 = (s32[16]{0:T(128)S(1)}, s32[16]{0:T(128)}, u32[]{:S(2)}) copy-start(s32[16]{0:T(128)} %param.12) | copy-start | bytes 196
  73.5 72.3 %all-gather.4.cloned.1.call-start = ((), (), s32[]{:S(2)}) async-start(), calls=%async_computation.4 | async-start | bytes 1179648 | tf_op jit(solution)/shard_map/all_gather | solution.py:19
  77.4 156.6 %all-gather.8.cloned.1.call-start = ((), (), s32[]{:S(2)}) async-start(), calls=%async_computation.6 | async-start | bytes 4718592 | tf_op jit(solution)/shard_map/all_gather | solution.py:19
  192.7 34.0 %all-to-all-start.1 = ((bf16[16,2,32,1024]{3,2,1,0:T(8,128)(2,1)}), bf16[16,2,32,1024]{3,2,1,0:T(8,128)(2,1)}, u32[]{:S(2)}, u32[]{:S(2)}) async-start(bf16[16,2,32,1024]{3,2,1,0:T(8,128)(2,1)} %bitcast.2), calls=%async_computation.1 | async-start | bytes 4194304 | tf_op jit(solution)/shard_map/all_to_all | solution.py:59
  228.7 1.0 copy-start.3
  228.7 1.2 copy-start.4
  228.7 3.2 %copy-start.5 = (f32[2,64,1024]{2,1,0:T(8,128)S(1)}, f32[2,64,1024]{2,1,0:T(8,128)}, u32[]{:S(2)}) copy-start(f32[2,64,1024]{2,1,0:T(8,128)} %param.13) | copy-start | bytes 1572868
  229.5 2.3 copy-start.1
  234.0 23.5 %copy-start.6 = (f32[2,64,1024]{2,1,0:T(8,128)S(1)}, f32[2,64,1024]{2,1,0:T(8,128)}, u32[]{:S(2)}) copy-start(f32[2,64,1024]{2,1,0:T(8,128)} %param.17) | copy-start | bytes 1572868
  234.0 37.0 %copy-start.2 = (f32[2,64,1024]{2,1,0:T(8,128)S(1)}, f32[2,64,1024]{2,1,0:T(8,128)}, u32[]{:S(2)}) copy-start(f32[2,64,1024]{2,1,0:T(8,128)} %param.14) | copy-start | bytes 1572868
  259.5 20.3 %all-to-all-start.3 = ((bf16[2,16,4,1024]{3,2,0,1:T(4,128)(2,1)}), bf16[2,16,4,1024]{3,2,0,1:T(4,128)(2,1)S(1)}, u32[]{:S(2)}, u32[]{:S(2)}) async-start(bf16[2,16,4,1024]{3,2,0,1:T(4,128)(2,1)} %copy.24), calls=%async_computation.3 | async-start | bytes 524288 | tf_op jit(solution)/shard_map/all_to_all | solution.py:101
Sparse Core Ops, SparseCore 0:
  73.6 33.4 all-gather.5
  108.9 36.7 all-gather.3
  147.6 58.0 all-gather.7

commit v5 on v3

--- a/solution.py
+++ b/solution.py
@@ -21,10 +21,9 @@
 
 def dp_sum(x):
     sources = lax.axis_size("z") * lax.axis_size("xlo")
-    x = x.reshape(x.shape[0], sources, x.shape[1] // sources, x.shape[2])
-    x = lax.all_to_all(x, DP, 1, 1, tiled=True)
-    x = jnp.sum(x.astype(jnp.float32), axis=1)
-    return dp_gather(x.astype(jnp.bfloat16), 1)
+    x = x.reshape(sources, x.shape[0] // sources, *x.shape[1:])
+    x = lax.all_to_all(x, DP, 0, 0, tiled=True)
+    return jnp.sum(x.astype(jnp.float32), axis=0).astype(jnp.bfloat16)
 
 
 def per_device(
@@ -47,10 +46,10 @@
     matches = owner_map[:, None] == jnp.arange(owned_slots, dtype=jnp.int32)[None, :]
     occupied = jnp.any(matches, axis=0)
     block_of = jnp.sum(jnp.where(matches, jnp.arange(blocks, dtype=jnp.int32)[:, None], 0), axis=0)
-    summed = dp_sum(grads[0].astype(jnp.bfloat16))
+    summed = dp_gather(dp_sum(grads[0].astype(jnp.bfloat16)), 0)
     summed, root_right = lax.optimization_barrier((summed, root_right))
     packed = jnp.where(occupied[:, None, None], jnp.take(summed, block_of, axis=0), 0.0)
-    packed = packed.reshape(owners, slot_count, summed.shape[1], order_size)
+    packed = packed.reshape(owners, slot_count, rows_dev, order_size)
     arrived = lax.all_to_all(packed, "own", split_axis=0, concat_axis=2, tiled=True)
     right_full = dp_gather(root_right, 1)
     first_row = dp_index() * rows_dev

time: 269 us -> 264 us (0.981)
  local copies, waits for them, and re-layouts: 16.5 us -> 9.33 us
    unnamed x19 -> x18, local copies, waits for them, and re-layouts: 4.84 us -> 0.38 us
where the time goes in v5:
time: 264 us; the launch traced here: 263 us
  waiting for transfers between devices  96.9 us (37%)
  blocking collectives  86.1 us (33%)
  starting transfers between devices  30.8 us (12%)
  matrix products  14.4 us (5%)
  between operations  14.2 us (5%)
  other arithmetic  11.5 us (4%)
  local copies, waits for them, and re-layouts  9.33 us (4%)
    all_to_all x1, blocking collectives, dp_sum(): x = lax.all_to_all(x, DP, 0, 0, tiled=True)  59.3 us
    all_to_all x1, waiting for transfers between devices, per_device(): lax.all_to_all(packed, 'own', split_axis=0, concat_axis=2, tiled=True)  55.2 us
    all_gather x2, waiting for transfers between devices, dp_gather(): return lax.all_gather(x, 'z', axis=axis, tiled=True)  37.3 us
    all_to_all x1, starting transfers between devices, per_device(): lax.all_to_all(shares, 'own', split_axis=1, concat_axis=0, tiled=True)  18 us
    all_to_all x1, starting transfers between devices, per_device(): lax.all_to_all(packed, 'own', split_axis=0, concat_axis=2, tiled=True)  12.7 us
    psum x1, blocking collectives, per_device(): square_sums = lax.psum(square_sums, 'z')  12.4 us
    all_gather x2, blocking collectives, dp_gather(): x = lax.all_gather(x, 'xlo', axis=axis, tiled=True)  10.6 us
    dot_general x1, matrix products, per_device(): jnp.einsum('srk,skn->srn', root_left, product, preferred_element_type=jnp...  7.84 us
  transfers between devices with their start and end apart: 4, of which 3 were waited for; matrix products, arithmetic and copies ran while one was open for 8% of the time, Pallas kernels for 0%

profile of v5, /device:TPU:1, one launch (start us, length us, event | category | flops | bytes accessed | tf_op | source)
XLA Modules:
  0.0 263.2 jit_solution(551132543874869681)
XLA Ops:
  7.2 2.5 convert_bitcast_fusion
  9.8 59.3 %all_to_all.35 = bf16[16,1,64,1024]{3,2,1,0:T(8,128)(2,1)S(1)} all-to-all(bf16[16,1,64,1024]{3,2,1,0:T(8,128)(2,1)S(1)} %convert_bitcast_fusion), channel_id=1, replica_groups=mesh['z'=8,'xlo'=2,'own'=16] {'z','xlo'}, dimensions={0} | all-to-all | bytes 4194304 | tf_op jit(solution)/shard_map/all_to_all | solution.py:25
  69.2 0.4 reduce_sum.47
  69.6 4.6 %all-gather = bf16[128,1024]{1,0:T(8,128)(2,1)} all-gather(bf16[64,1024]{1,0:T(8,128)(2,1)S(1)} %reduce_sum.47), channel_id=2, replica_groups=mesh['z'=8,'xlo'=2,'own'=16] {'xlo'}, dimensions={0}, use_global_device_ids=true | all-gather | bytes 393216 | tf_op jit(solution)/shard_map/all_gather | solution.py:18
  74.2 37.3 %all-gather.4.cloned.1.call-done = bf16[16,64,1024]{2,1,0:T(8,128)(2,1)} async-done(((bf16[2,64,1024]{2,1,0:T(8,128)(2,1)}), bf16[16,64,1024]{2,1,0:T(8,128)(2,1)}) %all-gather.4.cloned.1.call-update) | async-done | bytes 2097168 | tf_op jit(solution)/shard_map/all_gather | solution.py:19
  111.5 6.0 %all_gather.14 = bf16[2,128,1024]{2,1,0:T(8,128)(2,1)} all-gather(bf16[2,64,1024]{2,1,0:T(8,128)(2,1)S(1)} %copy-done.7), channel_id=1, replica_groups=mesh['z'=8,'xlo'=2,'own'=16] {'xlo'}, dimensions={1}, use_global_device_ids=true | all-gather | bytes 786432 | tf_op jit(solution)/shard_map/all_gather | solution.py:18
  118.0 4.4 %gather_fusion = bf16[32,64,1024]{2,1,0:T(8,128)(2,1)} fusion(bf16[16,64,1024]{2,1,0:T(8,128)(2,1)} %all-gather.4.cloned.1.call-done, s32[1024]{0:T(1024)S(1)} %pad_clamp_fusion.1), kind=kCustom, calls=%fused_computation | custom fusion | bytes 8388736 | tf_op jit(solution)/shard_map/jit(_take)/gather | solution.py:51
  122.3 4.7 %select_select_fusion = bf16[16,2,64,1024]{3,2,1,0:T(8,128)(2,1)} fusion(bf16[16,2,64,1024]{3,2,1,0:T(8,128)(2,1)} %bitcast.32, pred[16,2]{1,0:T(8,128)(4,1)S(1)} %compare_and_fusion, pred[16,2]{1,0:T(8,128)(4,1)S(1)} %broadcast_in_dim.75), kind=kLoop, calls=%fused_computation.4 | loop fusion | flops 4194304 | bytes 8388672 | tf_op jit(solution)/shard_map/jit(_where)/select_n | solution.py:51
  127.0 12.7 %all-to-all-start.1 = ((bf16[16,2,64,1024]{3,2,1,0:T(8,128)(2,1)}), bf16[16,2,64,1024]{3,2,1,0:T(8,128)(2,1)}, u32[]{:S(2)}, u32[]{:S(2)}) async-start(bf16[16,2,64,1024]{3,2,1,0:T(8,128)(2,1)} %select_select_fusion), calls=%async_computation.1 | async-start | bytes 8388608 | tf_op jit(solution)/shard_map/all_to_all | solution.py:53
  139.8 55.2 %all-to-all-done.1 = bf16[16,2,64,1024]{3,2,1,0:T(8,128)(2,1)} async-done(((bf16[16,2,64,1024]{3,2,1,0:T(8,128)(2,1)}), bf16[16,2,64,1024]{3,2,1,0:T(8,128)(2,1)}, u32[]{:S(2)}, u32[]{:S(2)}) %all-to-all-start.1) | async-done | bytes 4194336 | tf_op jit(solution)/shard_map/all_to_all | solution.py:53
  195.1 2.7 %copy.24 = bf16[1,2,16,64,1024]{4,3,2,1,0:T(8,128)(2,1)S(1)} copy(bf16[1,2,16,64,1024]{4,3,1,2,0:T(8,128)(2,1)} %bitcast.6) | data formatting | bytes 8388608 | tf_op jit(solution)/shard_map/all_to_all | solution.py:53
  197.8 1.9 fusion.10
  199.7 0.3 copy-done.1
  200.1 2.2 fusion.7
  202.3 7.8 %multiply_reduce_fusion = (f32[2]{0:T(128)S(1)}, f32[2,1024,64]{1,2,0:T(8,128)S(1)}) fusion(bf16[2,64,1024]{2,1,0:T(8,128)(2,1)S(1)} %copy-done, bf16[2,1024,1024]{2,1,0:T(8,128)(2,1)} %bitcast.30, bf16[2,1024,1024]{2,1,0:T(8,128)(2,1)} %all-gather.6.cloned.1.call-done), kind=kOutput, calls=%fused_computation.18 | convolution fusion | flops 4565762048 | bytes 9175048 | tf_op jit(solution)/shard_map/srk,skn->srn/dot_general | solution.py:72
  210.1 3.8 %all-reduce.1 = (f32[2]{0:T(128)S(1)}, f32[2]{0:T(128)S(1)}) all-reduce(f32[2]{0:T(128)S(1)} %get-tuple-element.19, f32[2]{0:T(128)S(1)} %get-tuple-element.15), channel_id=1, replica_groups=mesh['z'=8,'xlo'=2,'own'=16] {'xlo'}, use_global_device_ids=true, to_apply=%region_7.8 | all-reduce | flops 4 | bytes 32 | tf_op jit(solution)/shard_map/psum | solution.py:75
  213.9 12.4 %all-reduce = (f32[2]{0:T(128)S(1)}, f32[2]{0:T(128)S(1)}) all-reduce(f32[2]{0:T(128)S(1)} %get-tuple-element.12, f32[2]{0:T(128)S(1)} %get-tuple-element.13), channel_id=1, replica_groups=mesh['z'=8,'xlo'=2,'own'=16] {'z'}, use_global_device_ids=true, to_apply=%region_8.9 | all-reduce | flops 4 | bytes 32 | tf_op jit(solution)/shard_map/psum | solution.py:79
  226.3 1.0 fusion.13
  227.4 0.8 copy.26
  228.2 18.0 %all-to-all-start.2 = ((bf16[2,16,4,1024]{3,2,0,1:T(4,128)(2,1)}), bf16[2,16,4,1024]{3,2,0,1:T(4,128)(2,1)S(1)}, u32[]{:S(2)}, u32[]{:S(2)}) async-start(bf16[2,16,4,1024]{3,2,0,1:T(4,128)(2,1)} %copy.26), calls=%async_computation.2 | async-start | bytes 524288 | tf_op jit(solution)/shard_map/all_to_all | solution.py:93
  246.2 4.3 %fusion.5 = f32[2,64,1024]{2,1,0:T(8,128)} fusion(f32[2,64,1024]{2,1,0:T(8,128)S(1)} %copy-done.2, bf16[2,1024,1024]{2,1,0:T(8,128)(2,1)} %bitcast.31, s32[]{:T(128)S(6)} %select_n.69, pred[2]{0:T(512)(128)(4,1)S(1)} %dynamic_slice.9), kind=kOutput, calls=%fused_computation.9 | convolution fusion | flops 268959744 | bytes 5767174 | tf_op jit(solution)/shard_map/skr,skn->srn/dot_general | solution.py:63
  250.5 4.4 %all-to-all-done.2 = bf16[2,16,4,1024]{3,2,0,1:T(4,128)(2,1)S(1)} async-done(((bf16[2,16,4,1024]{3,2,0,1:T(4,128)(2,1)}), bf16[2,16,4,1024]{3,2,0,1:T(4,128)(2,1)S(1)}, u32[]{:S(2)}, u32[]{:S(2)}) %all-to-all-start.2) | async-done | bytes 262176 | tf_op jit(solution)/shard_map/all_to_all | solution.py:93
  254.9 0.7 gather_fusion.1
  255.6 0.8 broadcast_select_fusion
  (35 shorter events, 0.7 us)
Async XLA Ops:
  7.2 195.1 %copy-start = (bf16[2,64,1024]{2,1,0:T(8,128)(2,1)S(1)}, bf16[2,64,1024]{2,1,0:T(8,128)(2,1)}, u32[]{:S(2)}) copy-start(bf16[2,64,1024]{2,1,0:T(8,128)(2,1)} %param.13) | copy-start | bytes 786436
  7.2 104.4 %all-gather.4.cloned.1.call-start = ((), (), s32[]{:S(2)}) async-start(), calls=%async_computation.3 | async-start | bytes 2359296 | tf_op jit(solution)/shard_map/all_gather | solution.py:19
  9.8 101.8 %copy-start.7 = (bf16[2,64,1024]{2,1,0:T(8,128)(2,1)S(1)}, bf16[2,64,1024]{2,1,0:T(8,128)(2,1)}, u32[]{:S(2)}) copy-start(bf16[2,64,1024]{2,1,0:T(8,128)(2,1)} %param.14) | copy-start | bytes 786436
  9.8 107.8 %copy-start.8 = (s32[16]{0:T(128)S(1)}, s32[16]{0:T(128)}, u32[]{:S(2)}) copy-start(s32[16]{0:T(128)} %param.10) | copy-start | bytes 196
  74.2 128.1 %all-gather.6.cloned.1.call-start = ((), (), s32[]{:S(2)}) async-start(), calls=%async_computation.4 | async-start | bytes 4718592 | tf_op jit(solution)/shard_map/all_gather | solution.py:19
  127.0 68.1 %all-to-all-start.1 = ((bf16[16,2,64,1024]{3,2,1,0:T(8,128)(2,1)}), bf16[16,2,64,1024]{3,2,1,0:T(8,128)(2,1)}, u32[]{:S(2)}, u32[]{:S(2)}) async-start(bf16[16,2,64,1024]{3,2,1,0:T(8,128)(2,1)} %select_select_fusion), calls=%async_computation.1 | async-start | bytes 8388608 | tf_op jit(solution)/shard_map/all_to_all | solution.py:53
  195.1 2.8 %copy-start.3 = (f32[2,64,1024]{2,1,0:T(8,128)S(1)}, f32[2,64,1024]{2,1,0:T(8,128)}, u32[]{:S(2)}) copy-start(f32[2,64,1024]{2,1,0:T(8,128)} %param.17) | copy-start | bytes 1572868
  195.1 2.8 %copy-start.4 = (f32[2,64,1024]{2,1,0:T(8,128)S(1)}, f32[2,64,1024]{2,1,0:T(8,128)}, u32[]{:S(2)}) copy-start(f32[2,64,1024]{2,1,0:T(8,128)} %param.16) | copy-start | bytes 1572868
  195.1 5.0 %copy-start.5 = (f32[2,64,1024]{2,1,0:T(8,128)S(1)}, f32[2,64,1024]{2,1,0:T(8,128)}, u32[]{:S(2)}) copy-start(f32[2,64,1024]{2,1,0:T(8,128)} %param.11) | copy-start | bytes 1572868
  197.8 2.3 copy-start.1
  202.3 24.1 %copy-start.6 = (f32[2,64,1024]{2,1,0:T(8,128)S(1)}, f32[2,64,1024]{2,1,0:T(8,128)}, u32[]{:S(2)}) copy-start(f32[2,64,1024]{2,1,0:T(8,128)} %param.15) | copy-start | bytes 1572868
  202.3 43.9 %copy-start.2 = (f32[2,64,1024]{2,1,0:T(8,128)S(1)}, f32[2,64,1024]{2,1,0:T(8,128)}, u32[]{:S(2)}) copy-start(f32[2,64,1024]{2,1,0:T(8,128)} %param.12) | copy-start | bytes 1572868
  228.2 26.7 %all-to-all-start.2 = ((bf16[2,16,4,1024]{3,2,0,1:T(4,128)(2,1)}), bf16[2,16,4,1024]{3,2,0,1:T(4,128)(2,1)S(1)}, u32[]{:S(2)}, u32[]{:S(2)}) async-start(bf16[2,16,4,1024]{3,2,0,1:T(4,128)(2,1)} %copy.26), calls=%async_computation.2 | async-start | bytes 524288 | tf_op jit(solution)/shard_map/all_to_all | solution.py:93
Sparse Core Ops, SparseCore 0:
  74.3 37.2 all-gather.3
  117.7 58.4 all-gather.5

commit v6 on v5

--- a/solution.py
+++ b/solution.py
@@ -46,12 +46,15 @@
     matches = owner_map[:, None] == jnp.arange(owned_slots, dtype=jnp.int32)[None, :]
     occupied = jnp.any(matches, axis=0)
     block_of = jnp.sum(jnp.where(matches, jnp.arange(blocks, dtype=jnp.int32)[:, None], 0), axis=0)
+    partner = lax.ppermute(root_right, "xlo", [(0, 1), (1, 0)])
+    pair = jnp.where(lax.axis_index("xlo") == 0, jnp.stack([root_right, partner]), jnp.stack([partner, root_right]))
+    pair = jnp.swapaxes(pair, 0, 1).reshape(slot_count, 2 * rows_dev, order_size)
     summed = dp_gather(dp_sum(grads[0].astype(jnp.bfloat16)), 0)
-    summed, root_right = lax.optimization_barrier((summed, root_right))
-    packed = jnp.where(occupied[:, None, None], jnp.take(summed, block_of, axis=0), 0.0)
+    summed, pair = lax.optimization_barrier((summed, pair))
+    packed = jnp.take(summed, block_of, axis=0)
     packed = packed.reshape(owners, slot_count, rows_dev, order_size)
     arrived = lax.all_to_all(packed, "own", split_axis=0, concat_axis=2, tiled=True)
-    right_full = dp_gather(root_right, 1)
+    right_full = lax.all_gather(pair, "z", axis=1, tiled=True)
     first_row = dp_index() * rows_dev
     rounded = arrived.reshape(slot_count, order_size, order_size)
     row_part = lax.dynamic_slice_in_dim(rounded, first_row, rows_dev, 1)

time: 264 us -> 256 us (0.970)
  blocking collectives: 86.1 us -> 80.1 us
    all_gather x2 -> x1, waiting for transfers between devices: 37.3 us -> 30.8 us  [dp_gather(): return lax.all_gather(x, 'z', axis=axis, tiled=True)]
    all_gather x2 -> x1, blocking collectives: 10.6 us -> 4.59 us  [dp_gather(): x = lax.all_gather(x, 'xlo', axis=axis, tiled=True)]
    ppermute x0 -> x1, waiting for transfers between devices: none -> 5.56 us  [per_device(): partner = lax.ppermute(root_right, 'xlo', [(0, 1), (1, 0)])]
    select_n x2 -> x3, other arithmetic: 4.67 us -> 5.44 us  [the longest x2 4.6 us: per_device(): packed = jnp.take(summed, block_of, axis=0)]
  transfers between devices with their start and end apart: 4 -> 5, of which waited for: 3 -> 4; matrix products, arithmetic and copies ran while one was open for 8% -> 8% of each run, Pallas kernels for 0% -> 0%
where the time goes in v6:
time: 256 us
  waiting for transfers between devices  95.9 us (37%)
  blocking collectives  80.1 us (31%)
  starting transfers between devices  29.7 us (12%)
  matrix products  14.4 us (6%)
  between operations  14.2 us (6%)
  other arithmetic  12.3 us (5%)
  local copies, waits for them, and re-layouts  9.23 us (4%)
    all_to_all x1, blocking collectives, dp_sum(): x = lax.all_to_all(x, DP, 0, 0, tiled=True)  59.3 us
    all_to_all x1, waiting for transfers between devices, per_device(): lax.all_to_all(packed, 'own', split_axis=0, concat_axis=2, tiled=True)  55.1 us
    all_gather x1, waiting for transfers between devices, dp_gather(): return lax.all_gather(x, 'z', axis=axis, tiled=True)  30.8 us
    all_to_all x1, starting transfers between devices, per_device(): lax.all_to_all(shares, 'own', split_axis=1, concat_axis=0, tiled=True)  18 us
    psum x1, blocking collectives, per_device(): square_sums = lax.psum(square_sums, 'z')  12.4 us
    all_to_all x1, starting transfers between devices, per_device(): lax.all_to_all(packed, 'own', split_axis=0, concat_axis=2, tiled=True)  11.6 us
    dot_general x1, matrix products, per_device(): jnp.einsum('srk,skn->srn', root_left, product, preferred_element_type=jnp...  7.84 us
    ppermute x1, waiting for transfers between devices, per_device(): partner = lax.ppermute(root_right, 'xlo', [(0, 1), (1, 0)])  5.56 us
  transfers between devices with their start and end apart: 5, of which 4 were waited for; matrix products, arithmetic and copies ran while one was open for 8% of the time, Pallas kernels for 0%

profile of v6, /device:TPU:1, one launch (start us, length us, event | category | flops | bytes accessed | tf_op | source)
XLA Modules:
  0.0 255.8 jit_solution(16374685907940675669)
XLA Ops:
  7.2 2.5 convert_bitcast_fusion
  9.8 59.3 %all_to_all.35 = bf16[16,1,64,1024]{3,2,1,0:T(8,128)(2,1)S(1)} all-to-all(bf16[16,1,64,1024]{3,2,1,0:T(8,128)(2,1)S(1)} %convert_bitcast_fusion), channel_id=1, replica_groups=mesh['z'=8,'xlo'=2,'own'=16] {'z','xlo'}, dimensions={0} | all-to-all | bytes 4194304 | tf_op jit(solution)/shard_map/all_to_all | solution.py:25
  69.2 0.4 reduce_sum.47
  69.5 4.6 %all-gather = bf16[128,1024]{1,0:T(8,128)(2,1)} all-gather(bf16[64,1024]{1,0:T(8,128)(2,1)S(1)} %reduce_sum.47), channel_id=2, replica_groups=mesh['z'=8,'xlo'=2,'own'=16] {'xlo'}, dimensions={0}, use_global_device_ids=true | all-gather | bytes 393216 | tf_op jit(solution)/shard_map/all_gather | solution.py:18
  74.3 5.6 %collective-permute-done = bf16[2,64,1024]{2,1,0:T(8,128)(2,1)S(1)} collective-permute-done((bf16[2,64,1024]{2,1,0:T(8,128)(2,1)S(1)}, bf16[2,64,1024]{2,1,0:T(8,128)(2,1)S(1)}, u32[]{:S(2)}, u32[]{:S(2)}) %collective-permute-start) | collective-permute-done | bytes 262176 | tf_op jit(solution)/shard_map/ppermute | solution.py:49
  79.9 0.8 maximum_select_fusion
  80.7 30.8 %all-gather.4.cloned.1.call-done = bf16[16,64,1024]{2,1,0:T(8,128)(2,1)} async-done(((bf16[2,64,1024]{2,1,0:T(8,128)(2,1)}), bf16[16,64,1024]{2,1,0:T(8,128)(2,1)}) %all-gather.4.cloned.1.call-update) | async-done | bytes 2097168 | tf_op jit(solution)/shard_map/all_gather | solution.py:19
  111.8 4.4 %gather_fusion = bf16[32,64,1024]{2,1,0:T(8,128)(2,1)} fusion(bf16[16,64,1024]{2,1,0:T(8,128)(2,1)} %all-gather.4.cloned.1.call-done, s32[1024]{0:T(1024)S(1)} %pad_clamp_fusion.1), kind=kCustom, calls=%fused_computation | custom fusion | bytes 8388736 | tf_op jit(solution)/shard_map/jit(_take)/gather | solution.py:54
  116.2 4.6 %broadcast_select_fusion = bf16[16,2,64,1024]{3,2,1,0:T(8,128)(2,1)} fusion(bf16[16,2,64,1024]{3,2,1,0:T(8,128)(2,1)} %bitcast.37, pred[16,2]{1,0:T(8,128)(4,1)S(1)} %compare_and_fusion), kind=kLoop, calls=%fused_computation.4 | loop fusion | flops 2097152 | bytes 8388640 | tf_op jit(solution)/shard_map/jit(_take)/select_n | solution.py:54
  120.7 11.6 %all-to-all-start.1 = ((bf16[16,2,64,1024]{3,2,1,0:T(8,128)(2,1)}), bf16[16,2,64,1024]{3,2,1,0:T(8,128)(2,1)}, u32[]{:S(2)}, u32[]{:S(2)}) async-start(bf16[16,2,64,1024]{3,2,1,0:T(8,128)(2,1)} %broadcast_select_fusion), calls=%async_computation.1 | async-start | bytes 8388608 | tf_op jit(solution)/shard_map/all_to_all | solution.py:56
  132.5 55.1 %all-to-all-done.1 = bf16[16,2,64,1024]{3,2,1,0:T(8,128)(2,1)} async-done(((bf16[16,2,64,1024]{3,2,1,0:T(8,128)(2,1)}), bf16[16,2,64,1024]{3,2,1,0:T(8,128)(2,1)}, u32[]{:S(2)}, u32[]{:S(2)}) %all-to-all-start.1) | async-done | bytes 4194336 | tf_op jit(solution)/shard_map/all_to_all | solution.py:56
  187.7 2.7 %copy.23 = bf16[1,2,16,64,1024]{4,3,2,1,0:T(8,128)(2,1)S(1)} copy(bf16[1,2,16,64,1024]{4,3,1,2,0:T(8,128)(2,1)} %bitcast.10) | data formatting | bytes 8388608 | tf_op jit(solution)/shard_map/all_to_all | solution.py:56
  190.4 1.9 fusion.10
  192.7 2.2 fusion.7
  194.9 7.8 %multiply_reduce_fusion = (f32[2]{0:T(128)S(1)}, f32[2,1024,64]{1,2,0:T(8,128)S(1)}) fusion(bf16[2,64,1024]{2,1,0:T(8,128)(2,1)S(1)} %copy-done, bf16[2,1024,1024]{2,1,0:T(8,128)(2,1)} %bitcast.35, bf16[2,1024,1024]{2,1,0:T(8,128)(2,1)} %all-gather.6.cloned.1.call-done), kind=kOutput, calls=%fused_computation.19 | convolution fusion | flops 4565762048 | bytes 9175048 | tf_op jit(solution)/shard_map/srk,skn->srn/dot_general | solution.py:75
  202.7 3.8 %all-reduce.1 = (f32[2]{0:T(128)S(1)}, f32[2]{0:T(128)S(1)}) all-reduce(f32[2]{0:T(128)S(1)} %get-tuple-element.19, f32[2]{0:T(128)S(1)} %get-tuple-element.15), channel_id=1, replica_groups=mesh['z'=8,'xlo'=2,'own'=16] {'xlo'}, use_global_device_ids=true, to_apply=%region_7.8 | all-reduce | flops 4 | bytes 32 | tf_op jit(solution)/shard_map/psum | solution.py:78
  206.5 12.4 %all-reduce = (f32[2]{0:T(128)S(1)}, f32[2]{0:T(128)S(1)}) all-reduce(f32[2]{0:T(128)S(1)} %get-tuple-element.12, f32[2]{0:T(128)S(1)} %get-tuple-element.13), channel_id=1, replica_groups=mesh['z'=8,'xlo'=2,'own'=16] {'z'}, use_global_device_ids=true, to_apply=%region_8.9 | all-reduce | flops 4 | bytes 32 | tf_op jit(solution)/shard_map/psum | solution.py:82
  218.9 1.0 fusion.13
  220.0 0.8 copy.25
  220.8 18.0 %all-to-all-start.2 = ((bf16[2,16,4,1024]{3,2,0,1:T(4,128)(2,1)}), bf16[2,16,4,1024]{3,2,0,1:T(4,128)(2,1)S(1)}, u32[]{:S(2)}, u32[]{:S(2)}) async-start(bf16[2,16,4,1024]{3,2,0,1:T(4,128)(2,1)} %copy.25), calls=%async_computation.2 | async-start | bytes 524288 | tf_op jit(solution)/shard_map/all_to_all | solution.py:96
  238.8 4.3 %fusion.5 = f32[2,64,1024]{2,1,0:T(8,128)} fusion(f32[2,64,1024]{2,1,0:T(8,128)S(1)} %copy-done.2, bf16[2,1024,1024]{2,1,0:T(8,128)(2,1)} %bitcast.36, s32[]{:T(128)S(6)} %select_n.73, pred[2]{0:T(512)(128)(4,1)S(1)} %dynamic_slice.9), kind=kOutput, calls=%fused_computation.9 | convolution fusion | flops 268959744 | bytes 5767174 | tf_op jit(solution)/shard_map/skr,skn->srn/dot_general | solution.py:66
  243.1 4.4 %all-to-all-done.2 = bf16[2,16,4,1024]{3,2,0,1:T(4,128)(2,1)S(1)} async-done(((bf16[2,16,4,1024]{3,2,0,1:T(4,128)(2,1)}), bf16[2,16,4,1024]{3,2,0,1:T(4,128)(2,1)S(1)}, u32[]{:S(2)}, u32[]{:S(2)}) %all-to-all-start.2) | async-done | bytes 262176 | tf_op jit(solution)/shard_map/all_to_all | solution.py:96
  247.5 0.7 gather_fusion.1
  248.2 0.8 broadcast_select_fusion.1
  (36 shorter events, 1.1 us)
Async XLA Ops:
  7.2 187.7 %copy-start = (bf16[2,64,1024]{2,1,0:T(8,128)(2,1)S(1)}, bf16[2,64,1024]{2,1,0:T(8,128)(2,1)}, u32[]{:S(2)}) copy-start(bf16[2,64,1024]{2,1,0:T(8,128)(2,1)} %param.13) | copy-start | bytes 786436
  7.2 104.4 %all-gather.4.cloned.1.call-start = ((), (), s32[]{:S(2)}) async-start(), calls=%async_computation.3 | async-start | bytes 2359296 | tf_op jit(solution)/shard_map/all_gather | solution.py:19
  9.8 64.4 %copy-start.7 = (bf16[2,64,1024]{2,1,0:T(8,128)(2,1)S(1)}, bf16[2,64,1024]{2,1,0:T(8,128)(2,1)}, u32[]{:S(2)}) copy-start(bf16[2,64,1024]{2,1,0:T(8,128)(2,1)} %param.14) | copy-start | bytes 786436
  9.8 101.8 %copy-start.8 = (s32[16]{0:T(128)S(1)}, s32[16]{0:T(128)}, u32[]{:S(2)}) copy-start(s32[16]{0:T(128)} %param.10) | copy-start | bytes 196
  74.2 120.7 %all-gather.6.cloned.1.call-start = ((), (), s32[]{:S(2)}) async-start(), calls=%async_computation.4 | async-start | bytes 4718592 | tf_op jit(solution)/shard_map/all_gather | solution.py:57
  74.2 5.7 %collective-permute-start = (bf16[2,64,1024]{2,1,0:T(8,128)(2,1)S(1)}, bf16[2,64,1024]{2,1,0:T(8,128)(2,1)S(1)}, u32[]{:S(2)}, u32[]{:S(2)}) collective-permute-start(bf16[2,64,1024]{2,1,0:T(8,128)(2,1)S(1)} %copy-done.7), channel_id=1, source_target_pairs={{0,16},{16,0},{1,17},{17,1},{2,18},{18,2},{3,19},{19,3},{4,20},{20... | collective-permute-start | bytes 786440 | tf_op jit(solution)/shard_map/ppermute | solution.py:49
  120.7 66.9 %all-to-all-start.1 = ((bf16[16,2,64,1024]{3,2,1,0:T(8,128)(2,1)}), bf16[16,2,64,1024]{3,2,1,0:T(8,128)(2,1)}, u32[]{:S(2)}, u32[]{:S(2)}) async-start(bf16[16,2,64,1024]{3,2,1,0:T(8,128)(2,1)} %broadcast_select_fusion), calls=%async_computation.1 | async-start | bytes 8388608 | tf_op jit(solution)/shard_map/all_to_all | solution.py:56
  187.7 2.8 %copy-start.3 = (f32[2,64,1024]{2,1,0:T(8,128)S(1)}, f32[2,64,1024]{2,1,0:T(8,128)}, u32[]{:S(2)}) copy-start(f32[2,64,1024]{2,1,0:T(8,128)} %param.17) | copy-start | bytes 1572868
  187.7 2.8 %copy-start.4 = (f32[2,64,1024]{2,1,0:T(8,128)S(1)}, f32[2,64,1024]{2,1,0:T(8,128)}, u32[]{:S(2)}) copy-start(f32[2,64,1024]{2,1,0:T(8,128)} %param.16) | copy-start | bytes 1572868
  187.7 5.0 %copy-start.5 = (f32[2,64,1024]{2,1,0:T(8,128)S(1)}, f32[2,64,1024]{2,1,0:T(8,128)}, u32[]{:S(2)}) copy-start(f32[2,64,1024]{2,1,0:T(8,128)} %param.11) | copy-start | bytes 1572868
  190.4 2.3 copy-start.1
  194.9 24.1 %copy-start.6 = (f32[2,64,1024]{2,1,0:T(8,128)S(1)}, f32[2,64,1024]{2,1,0:T(8,128)}, u32[]{:S(2)}) copy-start(f32[2,64,1024]{2,1,0:T(8,128)} %param.15) | copy-start | bytes 1572868
  194.9 43.9 %copy-start.2 = (f32[2,64,1024]{2,1,0:T(8,128)S(1)}, f32[2,64,1024]{2,1,0:T(8,128)}, u32[]{:S(2)}) copy-start(f32[2,64,1024]{2,1,0:T(8,128)} %param.12) | copy-start | bytes 1572868
  220.8 26.7 %all-to-all-start.2 = ((bf16[2,16,4,1024]{3,2,0,1:T(4,128)(2,1)}), bf16[2,16,4,1024]{3,2,0,1:T(4,128)(2,1)S(1)}, u32[]{:S(2)}, u32[]{:S(2)}) async-start(bf16[2,16,4,1024]{3,2,0,1:T(4,128)(2,1)} %copy.25), calls=%async_computation.2 | async-start | bytes 524288 | tf_op jit(solution)/shard_map/all_to_all | solution.py:96
Sparse Core Ops, SparseCore 0:
  74.3 37.2 all-gather.3
  113.9 57.3 all-gather.5

commit v7 on v6

--- a/solution.py
+++ b/solution.py
@@ -20,9 +20,11 @@
 
 
 def dp_sum(x):
-    sources = lax.axis_size("z") * lax.axis_size("xlo")
-    x = x.reshape(sources, x.shape[0] // sources, *x.shape[1:])
-    x = lax.all_to_all(x, DP, 0, 0, tiled=True)
+    pairs, peers = lax.axis_size("z"), lax.axis_size("xlo")
+    x = x.reshape(pairs, peers, x.shape[0] // (pairs * peers), *x.shape[1:])
+    x = lax.all_to_all(x, "xlo", 1, 1, tiled=True)
+    x = jnp.sum(x.astype(jnp.float32), axis=1).astype(jnp.bfloat16)
+    x = lax.all_to_all(x, "z", 0, 0, tiled=True)
     return jnp.sum(x.astype(jnp.float32), axis=0).astype(jnp.bfloat16)
 
 
@@ -51,7 +53,7 @@
     pair = jnp.swapaxes(pair, 0, 1).reshape(slot_count, 2 * rows_dev, order_size)
     summed = dp_gather(dp_sum(grads[0].astype(jnp.bfloat16)), 0)
     summed, pair = lax.optimization_barrier((summed, pair))
-    packed = jnp.take(summed, block_of, axis=0)
+    packed = jnp.take(summed, block_of, axis=0, mode="clip")
     packed = packed.reshape(owners, slot_count, rows_dev, order_size)
     arrived = lax.all_to_all(packed, "own", split_axis=0, concat_axis=2, tiled=True)
     right_full = lax.all_gather(pair, "z", axis=1, tiled=True)
@@ -95,7 +97,7 @@
     )
     delivered = lax.all_to_all(shares, "own", split_axis=1, concat_axis=0, tiled=True)
     delivered = delivered.reshape(owned_slots, rows_dev // owners, order_size)
-    weights_out = jnp.take(delivered, owner_map, axis=0)
+    weights_out = jnp.take(delivered, owner_map, axis=0, mode="clip")
     return (left_next, right_next, master_next, first_next, second_next, weights_out)
 
 

time: 256 us -> 255 us (level)
  other arithmetic: 12.3 us -> 8.37 us
    select_n x4 -> x0, other arithmetic: 5.39 us -> none  [the longest x2 4.6 us: per_device(): packed = jnp.take(summed, block_of, axis=0)]
    all_to_all x1 -> x2, blocking collectives: 59.3 us -> 61.6 us  [the longest x1 36.2 us: dp_sum(): x = lax.all_to_all(x, 'z', 0, 0, tiled=True)]
  transfers between devices with their start and end apart: 5 -> 5, of which waited for: 4 -> 4; matrix products, arithmetic and copies ran while one was open for 8% -> 7% of each run, Pallas kernels for 0% -> 0%
where the time goes in v7:
time: 255 us
  waiting for transfers between devices  95.2 us (37%)
  blocking collectives  82.4 us (32%)
  starting transfers between devices  30.6 us (12%)
  matrix products  14.4 us (6%)
  between operations  14.1 us (6%)
  local copies, waits for them, and re-layouts  9.96 us (4%)
  other arithmetic  8.37 us (3%)
    all_to_all x1, waiting for transfers between devices, per_device(): lax.all_to_all(packed, 'own', split_axis=0, concat_axis=2, tiled=True)  55.1 us
    all_to_all x1, blocking collectives, dp_sum(): x = lax.all_to_all(x, 'z', 0, 0, tiled=True)  36.2 us
    all_gather x1, waiting for transfers between devices, dp_gather(): return lax.all_gather(x, 'z', axis=axis, tiled=True)  29.8 us
    all_to_all x1, blocking collectives, dp_sum(): x = lax.all_to_all(x, 'xlo', 1, 1, tiled=True)  25.4 us
    all_to_all x1, starting transfers between devices, per_device(): lax.all_to_all(shares, 'own', split_axis=1, concat_axis=0, tiled=True)  18 us
    psum x1, blocking collectives, per_device(): square_sums = lax.psum(square_sums, 'z')  12.4 us
    all_to_all x1, starting transfers between devices, per_device(): lax.all_to_all(packed, 'own', split_axis=0, concat_axis=2, tiled=True)  11.6 us
    dot_general x1, matrix products, per_device(): jnp.einsum('srk,skn->srn', root_left, product, preferred_element_type=jnp...  7.84 us
  transfers between devices with their start and end apart: 5, of which 4 were waited for; matrix products, arithmetic and copies ran while one was open for 7% of the time, Pallas kernels for 0%

profile of v7, /device:TPU:1, one launch (start us, length us, event | category | flops | bytes accessed | tf_op | source)
XLA Modules:
  0.0 255.0 jit_solution(8026204523827009087)
XLA Ops:
  7.2 2.5 convert_element_type.26
  10.0 25.4 %all_to_all.40 = bf16[8,2,1,64,1024]{4,3,0,2,1:T(8,128)(2,1)S(1)} all-to-all(bf16[8,2,1,64,1024]{4,3,0,2,1:T(8,128)(2,1)S(1)} %copy.26), channel_id=1, replica_groups=mesh['z'=8,'xlo'=2,'own'=16] {'xlo'}, dimensions={1} | all-to-all | bytes 4194304 | tf_op jit(solution)/shard_map/all_to_all | solution.py:25
  35.4 0.7 reduce_sum.55
  36.0 36.2 %all_to_all.41 = bf16[8,1,64,1024]{3,2,1,0:T(8,128)(2,1)S(1)} all-to-all(bf16[8,1,64,1024]{3,2,1,0:T(8,128)(2,1)S(1)} %bitcast.35), channel_id=1, replica_groups=mesh['z'=8,'xlo'=2,'own'=16] {'z'}, dimensions={0} | all-to-all | bytes 2097152 | tf_op jit(solution)/shard_map/all_to_all | solution.py:27
  72.4 4.6 %all-gather = bf16[128,1024]{1,0:T(8,128)(2,1)} all-gather(bf16[64,1024]{1,0:T(8,128)(2,1)S(1)} %reduce_sum.57), channel_id=2, replica_groups=mesh['z'=8,'xlo'=2,'own'=16] {'xlo'}, dimensions={0}, use_global_device_ids=true | all-gather | bytes 393216 | tf_op jit(solution)/shard_map/all_gather | solution.py:18
  77.1 0.9 collective-permute-start
  78.0 5.8 %collective-permute-done = bf16[2,64,1024]{2,1,0:T(8,128)(2,1)S(1)} collective-permute-done((bf16[2,64,1024]{2,1,0:T(8,128)(2,1)}, bf16[2,64,1024]{2,1,0:T(8,128)(2,1)S(1)}, u32[]{:S(2)}, u32[]{:S(2)}) %collective-permute-start) | collective-permute-done | bytes 262176 | tf_op jit(solution)/shard_map/ppermute | solution.py:51
  83.8 1.9 maximum_select_fusion
  85.8 29.8 %all-gather.4.cloned.1.call-done = bf16[16,64,1024]{2,1,0:T(8,128)(2,1)} async-done(((bf16[2,64,1024]{2,1,0:T(8,128)(2,1)}), bf16[16,64,1024]{2,1,0:T(8,128)(2,1)}) %all-gather.4.cloned.1.call-update) | async-done | bytes 2097168 | tf_op jit(solution)/shard_map/all_gather | solution.py:19
  115.7 4.4 %gather_fusion = bf16[32,64,1024]{2,1,0:T(8,128)(2,1)} fusion(bf16[16,64,1024]{2,1,0:T(8,128)(2,1)} %all-gather.4.cloned.1.call-done, s32[1024]{0:T(1024)S(1)} %pad_clamp_fusion.1), kind=kCustom, calls=%fused_computation | custom fusion | bytes 8388736 | tf_op jit(solution)/shard_map/jit(_take)/gather | solution.py:56
  120.1 11.6 %all-to-all-start.2 = ((bf16[16,2,64,1024]{3,2,1,0:T(8,128)(2,1)}), bf16[16,2,64,1024]{3,2,1,0:T(8,128)(2,1)}, u32[]{:S(2)}, u32[]{:S(2)}) async-start(bf16[16,2,64,1024]{3,2,1,0:T(8,128)(2,1)} %bitcast.33), calls=%async_computation.2 | async-start | bytes 8388608 | tf_op jit(solution)/shard_map/all_to_all | solution.py:58
  131.8 55.1 %all-to-all-done.2 = bf16[16,2,64,1024]{3,2,1,0:T(8,128)(2,1)} async-done(((bf16[16,2,64,1024]{3,2,1,0:T(8,128)(2,1)}), bf16[16,2,64,1024]{3,2,1,0:T(8,128)(2,1)}, u32[]{:S(2)}, u32[]{:S(2)}) %all-to-all-start.2) | async-done | bytes 4194336 | tf_op jit(solution)/shard_map/all_to_all | solution.py:58
  187.0 2.7 %copy.27 = bf16[1,2,16,64,1024]{4,3,2,1,0:T(8,128)(2,1)S(1)} copy(bf16[1,2,16,64,1024]{4,3,1,2,0:T(8,128)(2,1)} %bitcast.9) | data formatting | bytes 8388608 | tf_op jit(solution)/shard_map/all_to_all | solution.py:58
  189.8 1.9 fusion.10
  192.0 2.2 fusion.7
  194.2 7.8 %multiply_reduce_fusion = (f32[2]{0:T(128)S(1)}, f32[2,1024,64]{1,2,0:T(8,128)S(1)}) fusion(bf16[2,64,1024]{2,1,0:T(8,128)(2,1)S(1)} %copy-done, bf16[2,1024,1024]{2,1,0:T(8,128)(2,1)} %bitcast.31, bf16[2,1024,1024]{2,1,0:T(8,128)(2,1)} %all-gather.6.cloned.1.call-done), kind=kOutput, calls=%fused_computation.17 | convolution fusion | flops 4565762048 | bytes 9175048 | tf_op jit(solution)/shard_map/srk,skn->srn/dot_general | solution.py:77
  202.0 3.8 %all-reduce.1 = (f32[2]{0:T(128)S(1)}, f32[2]{0:T(128)S(1)}) all-reduce(f32[2]{0:T(128)S(1)} %get-tuple-element.19, f32[2]{0:T(128)S(1)} %get-tuple-element.15), channel_id=1, replica_groups=mesh['z'=8,'xlo'=2,'own'=16] {'xlo'}, use_global_device_ids=true, to_apply=%region_8.9 | all-reduce | flops 4 | bytes 32 | tf_op jit(solution)/shard_map/psum | solution.py:80
  205.8 12.4 %all-reduce = (f32[2]{0:T(128)S(1)}, f32[2]{0:T(128)S(1)}) all-reduce(f32[2]{0:T(128)S(1)} %get-tuple-element.12, f32[2]{0:T(128)S(1)} %get-tuple-element.13), channel_id=1, replica_groups=mesh['z'=8,'xlo'=2,'own'=16] {'z'}, use_global_device_ids=true, to_apply=%region_9.10 | all-reduce | flops 4 | bytes 32 | tf_op jit(solution)/shard_map/psum | solution.py:84
  218.3 1.0 fusion.13
  219.3 0.8 copy.29
  220.2 18.0 %all-to-all-start.3 = ((bf16[2,16,4,1024]{3,2,0,1:T(4,128)(2,1)}), bf16[2,16,4,1024]{3,2,0,1:T(4,128)(2,1)S(1)}, u32[]{:S(2)}, u32[]{:S(2)}) async-start(bf16[2,16,4,1024]{3,2,0,1:T(4,128)(2,1)} %copy.29), calls=%async_computation.3 | async-start | bytes 524288 | tf_op jit(solution)/shard_map/all_to_all | solution.py:98
  238.1 4.3 %fusion.5 = f32[2,64,1024]{2,1,0:T(8,128)} fusion(f32[2,64,1024]{2,1,0:T(8,128)S(1)} %copy-done.2, bf16[2,1024,1024]{2,1,0:T(8,128)(2,1)} %bitcast.32, s32[]{:T(128)S(6)} %select_n.39, pred[2]{0:T(512)(128)(4,1)S(1)} %dynamic_slice.9), kind=kOutput, calls=%fused_computation.7 | convolution fusion | flops 268959744 | bytes 5767174 | tf_op jit(solution)/shard_map/skr,skn->srn/dot_general | solution.py:68
  242.5 4.4 %all-to-all-done.3 = bf16[2,16,4,1024]{3,2,0,1:T(4,128)(2,1)S(1)} async-done(((bf16[2,16,4,1024]{3,2,0,1:T(4,128)(2,1)}), bf16[2,16,4,1024]{3,2,0,1:T(4,128)(2,1)S(1)}, u32[]{:S(2)}, u32[]{:S(2)}) %all-to-all-start.3) | async-done | bytes 262176 | tf_op jit(solution)/shard_map/all_to_all | solution.py:98
  246.8 1.3 gather_fusion.1
  (30 shorter events, 1.2 us)
Async XLA Ops:
  7.2 187.0 %copy-start = (bf16[2,64,1024]{2,1,0:T(8,128)(2,1)S(1)}, bf16[2,64,1024]{2,1,0:T(8,128)(2,1)}, u32[]{:S(2)}) copy-start(bf16[2,64,1024]{2,1,0:T(8,128)(2,1)} %param.13) | copy-start | bytes 786436
  7.2 108.4 %all-gather.4.cloned.1.call-start = ((), (), s32[]{:S(2)}) async-start(), calls=%async_computation.4 | async-start | bytes 2359296 | tf_op jit(solution)/shard_map/all_gather | solution.py:19
  35.4 80.2 %copy-start.7 = (s32[16]{0:T(128)S(1)}, s32[16]{0:T(128)}, u32[]{:S(2)}) copy-start(s32[16]{0:T(128)} %param.10) | copy-start | bytes 196
  77.1 117.2 %all-gather.6.cloned.1.call-start = ((), (), s32[]{:S(2)}) async-start(), calls=%async_computation.5 | async-start | bytes 4718592 | tf_op jit(solution)/shard_map/all_gather | solution.py:59
  77.1 6.7 %collective-permute-start = (bf16[2,64,1024]{2,1,0:T(8,128)(2,1)}, bf16[2,64,1024]{2,1,0:T(8,128)(2,1)S(1)}, u32[]{:S(2)}, u32[]{:S(2)}) collective-permute-start(bf16[2,64,1024]{2,1,0:T(8,128)(2,1)} %param.14), channel_id=1, source_target_pairs={{0,16},{16,0},{1,17},{17,1},{2,18},{18,2},{3,19},{19,3},{4,20},{20... | collective-permute-start | bytes 786440 | tf_op jit(solution)/shard_map/ppermute | solution.py:51
  120.1 66.9 %all-to-all-start.2 = ((bf16[16,2,64,1024]{3,2,1,0:T(8,128)(2,1)}), bf16[16,2,64,1024]{3,2,1,0:T(8,128)(2,1)}, u32[]{:S(2)}, u32[]{:S(2)}) async-start(bf16[16,2,64,1024]{3,2,1,0:T(8,128)(2,1)} %bitcast.33), calls=%async_computation.2 | async-start | bytes 8388608 | tf_op jit(solution)/shard_map/all_to_all | solution.py:58
  187.0 2.8 %copy-start.3 = (f32[2,64,1024]{2,1,0:T(8,128)S(1)}, f32[2,64,1024]{2,1,0:T(8,128)}, u32[]{:S(2)}) copy-start(f32[2,64,1024]{2,1,0:T(8,128)} %param.17) | copy-start | bytes 1572868
  187.0 2.8 %copy-start.4 = (f32[2,64,1024]{2,1,0:T(8,128)S(1)}, f32[2,64,1024]{2,1,0:T(8,128)}, u32[]{:S(2)}) copy-start(f32[2,64,1024]{2,1,0:T(8,128)} %param.16) | copy-start | bytes 1572868
  187.0 5.0 %copy-start.5 = (f32[2,64,1024]{2,1,0:T(8,128)S(1)}, f32[2,64,1024]{2,1,0:T(8,128)}, u32[]{:S(2)}) copy-start(f32[2,64,1024]{2,1,0:T(8,128)} %param.11) | copy-start | bytes 1572868
  189.7 2.3 copy-start.1
  194.2 24.1 %copy-start.6 = (f32[2,64,1024]{2,1,0:T(8,128)S(1)}, f32[2,64,1024]{2,1,0:T(8,128)}, u32[]{:S(2)}) copy-start(f32[2,64,1024]{2,1,0:T(8,128)} %param.15) | copy-start | bytes 1572868
  194.2 43.9 %copy-start.2 = (f32[2,64,1024]{2,1,0:T(8,128)S(1)}, f32[2,64,1024]{2,1,0:T(8,128)}, u32[]{:S(2)}) copy-start(f32[2,64,1024]{2,1,0:T(8,128)} %param.12) | copy-start | bytes 1572868
  220.2 26.7 %all-to-all-start.3 = ((bf16[2,16,4,1024]{3,2,0,1:T(4,128)(2,1)}), bf16[2,16,4,1024]{3,2,0,1:T(4,128)(2,1)S(1)}, u32[]{:S(2)}, u32[]{:S(2)}) async-start(bf16[2,16,4,1024]{3,2,0,1:T(4,128)(2,1)} %copy.29), calls=%async_computation.3 | async-start | bytes 524288 | tf_op jit(solution)/shard_map/all_to_all | solution.py:98
Sparse Core Ops, SparseCore 0:
  77.2 38.3 all-gather.3
  117.9 57.3 all-gather.5

commit v8 on v6

--- a/solution.py
+++ b/solution.py
@@ -51,7 +51,7 @@
     pair = jnp.swapaxes(pair, 0, 1).reshape(slot_count, 2 * rows_dev, order_size)
     summed = dp_gather(dp_sum(grads[0].astype(jnp.bfloat16)), 0)
     summed, pair = lax.optimization_barrier((summed, pair))
-    packed = jnp.take(summed, block_of, axis=0)
+    packed = jnp.take(summed, block_of, axis=0, mode="clip")
     packed = packed.reshape(owners, slot_count, rows_dev, order_size)
     arrived = lax.all_to_all(packed, "own", split_axis=0, concat_axis=2, tiled=True)
     right_full = lax.all_gather(pair, "z", axis=1, tiled=True)
@@ -95,7 +95,7 @@
     )
     delivered = lax.all_to_all(shares, "own", split_axis=1, concat_axis=0, tiled=True)
     delivered = delivered.reshape(owned_slots, rows_dev // owners, order_size)
-    weights_out = jnp.take(delivered, owner_map, axis=0)
+    weights_out = jnp.take(delivered, owner_map, axis=0, mode="clip")
     return (left_next, right_next, master_next, first_next, second_next, weights_out)
 
 

time: 256 us -> 251 us (0.980)
  other arithmetic: 12.3 us -> 6.86 us
    select_n x4 -> x0, other arithmetic: 5.39 us -> none  [the longest x2 4.6 us: per_device(): packed = jnp.take(summed, block_of, axis=0)]
  transfers between devices with their start and end apart: 5 -> 5, of which waited for: 4 -> 4; matrix products, arithmetic and copies ran while one was open for 8% -> 7% of each run, Pallas kernels for 0% -> 0%
where the time goes in v8:
time: 251 us
  waiting for transfers between devices  95.9 us (38%)
  blocking collectives  80.1 us (32%)
  starting transfers between devices  29.7 us (12%)
  matrix products  14.4 us (6%)
  between operations  14.2 us (6%)
  local copies, waits for them, and re-layouts  9.79 us (4%)
  other arithmetic  6.86 us (3%)
    all_to_all x1, blocking collectives, dp_sum(): x = lax.all_to_all(x, DP, 0, 0, tiled=True)  59.3 us
    all_to_all x1, waiting for transfers between devices, per_device(): lax.all_to_all(packed, 'own', split_axis=0, concat_axis=2, tiled=True)  55.1 us
    all_gather x1, waiting for transfers between devices, dp_gather(): return lax.all_gather(x, 'z', axis=axis, tiled=True)  30.8 us
    all_to_all x1, starting transfers between devices, per_device(): lax.all_to_all(shares, 'own', split_axis=1, concat_axis=0, tiled=True)  18 us
    psum x1, blocking collectives, per_device(): square_sums = lax.psum(square_sums, 'z')  12.4 us
    all_to_all x1, starting transfers between devices, per_device(): lax.all_to_all(packed, 'own', split_axis=0, concat_axis=2, tiled=True)  11.6 us
    dot_general x1, matrix products, per_device(): jnp.einsum('srk,skn->srn', root_left, product, preferred_element_type=jnp...  7.84 us
    ppermute x1, waiting for transfers between devices, per_device(): partner = lax.ppermute(root_right, 'xlo', [(0, 1), (1, 0)])  5.56 us
  transfers between devices with their start and end apart: 5, of which 4 were waited for; matrix products, arithmetic and copies ran while one was open for 7% of the time, Pallas kernels for 0%

profile of v8, /device:TPU:1, one launch (start us, length us, event | category | flops | bytes accessed | tf_op | source)
XLA Modules:
  0.0 250.9 jit_solution(8889065107897612957)
XLA Ops:
  7.2 2.5 %convert_bitcast_fusion = bf16[16,1,64,1024]{3,2,1,0:T(8,128)(2,1)S(1)} fusion(f32[1,16,64,1024]{3,2,1,0:T(8,128)} %param.9), kind=kLoop, calls=%fused_computation.4 | loop fusion | flops 1048576 | bytes 6291456 | tf_op jit(solution)/shard_map/convert_element_type | solution.py:52
  9.8 59.3 %all_to_all.35 = bf16[16,1,64,1024]{3,2,1,0:T(8,128)(2,1)S(1)} all-to-all(bf16[16,1,64,1024]{3,2,1,0:T(8,128)(2,1)S(1)} %convert_bitcast_fusion), channel_id=1, replica_groups=mesh['z'=8,'xlo'=2,'own'=16] {'z','xlo'}, dimensions={0} | all-to-all | bytes 4194304 | tf_op jit(solution)/shard_map/all_to_all | solution.py:25
  69.2 0.4 reduce_sum.41
  69.6 4.6 %all-gather = bf16[128,1024]{1,0:T(8,128)(2,1)} all-gather(bf16[64,1024]{1,0:T(8,128)(2,1)S(1)} %reduce_sum.41), channel_id=2, replica_groups=mesh['z'=8,'xlo'=2,'own'=16] {'xlo'}, dimensions={0}, use_global_device_ids=true | all-gather | bytes 393216 | tf_op jit(solution)/shard_map/all_gather | solution.py:18
  74.3 5.6 %collective-permute-done = bf16[2,64,1024]{2,1,0:T(8,128)(2,1)S(1)} collective-permute-done((bf16[2,64,1024]{2,1,0:T(8,128)(2,1)S(1)}, bf16[2,64,1024]{2,1,0:T(8,128)(2,1)S(1)}, u32[]{:S(2)}, u32[]{:S(2)}) %collective-permute-start) | collective-permute-done | bytes 262176 | tf_op jit(solution)/shard_map/ppermute | solution.py:49
  79.9 0.8 maximum_select_fusion
  80.7 30.8 %all-gather.4.cloned.1.call-done = bf16[16,64,1024]{2,1,0:T(8,128)(2,1)} async-done(((bf16[2,64,1024]{2,1,0:T(8,128)(2,1)}), bf16[16,64,1024]{2,1,0:T(8,128)(2,1)}) %all-gather.4.cloned.1.call-update) | async-done | bytes 2097168 | tf_op jit(solution)/shard_map/all_gather | solution.py:19
  111.7 4.4 %gather_fusion = bf16[32,64,1024]{2,1,0:T(8,128)(2,1)} fusion(bf16[16,64,1024]{2,1,0:T(8,128)(2,1)} %all-gather.4.cloned.1.call-done, s32[1024]{0:T(1024)S(1)} %pad_clamp_fusion.1), kind=kCustom, calls=%fused_computation | custom fusion | bytes 8388736 | tf_op jit(solution)/shard_map/jit(_take)/gather | solution.py:54
  116.0 11.6 %all-to-all-start.1 = ((bf16[16,2,64,1024]{3,2,1,0:T(8,128)(2,1)}), bf16[16,2,64,1024]{3,2,1,0:T(8,128)(2,1)}, u32[]{:S(2)}, u32[]{:S(2)}) async-start(bf16[16,2,64,1024]{3,2,1,0:T(8,128)(2,1)} %bitcast.33), calls=%async_computation.1 | async-start | bytes 8388608 | tf_op jit(solution)/shard_map/all_to_all | solution.py:56
  127.8 55.1 %all-to-all-done.1 = bf16[16,2,64,1024]{3,2,1,0:T(8,128)(2,1)} async-done(((bf16[16,2,64,1024]{3,2,1,0:T(8,128)(2,1)}), bf16[16,2,64,1024]{3,2,1,0:T(8,128)(2,1)}, u32[]{:S(2)}, u32[]{:S(2)}) %all-to-all-start.1) | async-done | bytes 4194336 | tf_op jit(solution)/shard_map/all_to_all | solution.py:56
  183.0 2.7 %copy.22 = bf16[1,2,16,64,1024]{4,3,2,1,0:T(8,128)(2,1)S(1)} copy(bf16[1,2,16,64,1024]{4,3,1,2,0:T(8,128)(2,1)} %bitcast.8) | data formatting | bytes 8388608 | tf_op jit(solution)/shard_map/all_to_all | solution.py:56
  185.7 1.9 fusion.10
  187.6 0.3 copy-done.1
  188.0 2.2 fusion.7
  190.2 7.8 %multiply_reduce_fusion = (f32[2]{0:T(128)S(1)}, f32[2,1024,64]{1,2,0:T(8,128)S(1)}) fusion(bf16[2,64,1024]{2,1,0:T(8,128)(2,1)S(1)} %copy-done, bf16[2,1024,1024]{2,1,0:T(8,128)(2,1)} %bitcast.31, bf16[2,1024,1024]{2,1,0:T(8,128)(2,1)} %all-gather.6.cloned.1.call-done), kind=kOutput, calls=%fused_computation.18 | convolution fusion | flops 4565762048 | bytes 9175048 | tf_op jit(solution)/shard_map/srk,skn->srn/dot_general | solution.py:75
  198.0 3.8 %all-reduce.1 = (f32[2]{0:T(128)S(1)}, f32[2]{0:T(128)S(1)}) all-reduce(f32[2]{0:T(128)S(1)} %get-tuple-element.19, f32[2]{0:T(128)S(1)} %get-tuple-element.15), channel_id=1, replica_groups=mesh['z'=8,'xlo'=2,'own'=16] {'xlo'}, use_global_device_ids=true, to_apply=%region_7.8 | all-reduce | flops 4 | bytes 32 | tf_op jit(solution)/shard_map/psum | solution.py:78
  201.8 12.4 %all-reduce = (f32[2]{0:T(128)S(1)}, f32[2]{0:T(128)S(1)}) all-reduce(f32[2]{0:T(128)S(1)} %get-tuple-element.12, f32[2]{0:T(128)S(1)} %get-tuple-element.13), channel_id=1, replica_groups=mesh['z'=8,'xlo'=2,'own'=16] {'z'}, use_global_device_ids=true, to_apply=%region_8.9 | all-reduce | flops 4 | bytes 32 | tf_op jit(solution)/shard_map/psum | solution.py:82
  214.2 1.0 fusion.13
  215.2 0.1 reshape.49
  215.3 0.8 copy.24
  216.1 18.0 %all-to-all-start.2 = ((bf16[2,16,4,1024]{3,2,0,1:T(4,128)(2,1)}), bf16[2,16,4,1024]{3,2,0,1:T(4,128)(2,1)S(1)}, u32[]{:S(2)}, u32[]{:S(2)}) async-start(bf16[2,16,4,1024]{3,2,0,1:T(4,128)(2,1)} %copy.24), calls=%async_computation.2 | async-start | bytes 524288 | tf_op jit(solution)/shard_map/all_to_all | solution.py:96
  234.1 4.3 %fusion.5 = f32[2,64,1024]{2,1,0:T(8,128)} fusion(f32[2,64,1024]{2,1,0:T(8,128)S(1)} %copy-done.2, bf16[2,1024,1024]{2,1,0:T(8,128)(2,1)} %bitcast.32, s32[]{:T(128)S(6)} %select_n.39, pred[2]{0:T(512)(128)(4,1)S(1)} %dynamic_slice.9), kind=kOutput, calls=%fused_computation.8 | convolution fusion | flops 268959744 | bytes 5767174 | tf_op jit(solution)/shard_map/skr,skn->srn/dot_general | solution.py:66
  238.4 4.4 %all-to-all-done.2 = bf16[2,16,4,1024]{3,2,0,1:T(4,128)(2,1)S(1)} async-done(((bf16[2,16,4,1024]{3,2,0,1:T(4,128)(2,1)}), bf16[2,16,4,1024]{3,2,0,1:T(4,128)(2,1)S(1)}, u32[]{:S(2)}, u32[]{:S(2)}) %all-to-all-start.2) | async-done | bytes 262176 | tf_op jit(solution)/shard_map/all_to_all | solution.py:96
  242.8 1.3 gather_fusion.1
  (29 shorter events, 0.5 us)
Async XLA Ops:
  7.2 183.0 %copy-start = (bf16[2,64,1024]{2,1,0:T(8,128)(2,1)S(1)}, bf16[2,64,1024]{2,1,0:T(8,128)(2,1)}, u32[]{:S(2)}) copy-start(bf16[2,64,1024]{2,1,0:T(8,128)(2,1)} %param.13) | copy-start | bytes 786436
  7.2 104.4 %all-gather.4.cloned.1.call-start = ((), (), s32[]{:S(2)}) async-start(), calls=%async_computation.3 | async-start | bytes 2359296 | tf_op jit(solution)/shard_map/all_gather | solution.py:19
  9.8 64.4 %copy-start.7 = (bf16[2,64,1024]{2,1,0:T(8,128)(2,1)S(1)}, bf16[2,64,1024]{2,1,0:T(8,128)(2,1)}, u32[]{:S(2)}) copy-start(bf16[2,64,1024]{2,1,0:T(8,128)(2,1)} %param.14) | copy-start | bytes 786436
  9.8 101.8 %copy-start.8 = (s32[16]{0:T(128)S(1)}, s32[16]{0:T(128)}, u32[]{:S(2)}) copy-start(s32[16]{0:T(128)} %param.10) | copy-start | bytes 196
  74.2 116.0 %all-gather.6.cloned.1.call-start = ((), (), s32[]{:S(2)}) async-start(), calls=%async_computation.4 | async-start | bytes 4718592 | tf_op jit(solution)/shard_map/all_gather | solution.py:57
  74.2 5.7 %collective-permute-start = (bf16[2,64,1024]{2,1,0:T(8,128)(2,1)S(1)}, bf16[2,64,1024]{2,1,0:T(8,128)(2,1)S(1)}, u32[]{:S(2)}, u32[]{:S(2)}) collective-permute-start(bf16[2,64,1024]{2,1,0:T(8,128)(2,1)S(1)} %copy-done.7), channel_id=1, source_target_pairs={{0,16},{16,0},{1,17},{17,1},{2,18},{18,2},{3,19},{19,3},{4,20},{20... | collective-permute-start | bytes 786440 | tf_op jit(solution)/shard_map/ppermute | solution.py:49
  116.0 66.9 %all-to-all-start.1 = ((bf16[16,2,64,1024]{3,2,1,0:T(8,128)(2,1)}), bf16[16,2,64,1024]{3,2,1,0:T(8,128)(2,1)}, u32[]{:S(2)}, u32[]{:S(2)}) async-start(bf16[16,2,64,1024]{3,2,1,0:T(8,128)(2,1)} %bitcast.33), calls=%async_computation.1 | async-start | bytes 8388608 | tf_op jit(solution)/shard_map/all_to_all | solution.py:56
  182.9 2.8 %copy-start.3 = (f32[2,64,1024]{2,1,0:T(8,128)S(1)}, f32[2,64,1024]{2,1,0:T(8,128)}, u32[]{:S(2)}) copy-start(f32[2,64,1024]{2,1,0:T(8,128)} %param.17) | copy-start | bytes 1572868
  183.0 2.8 %copy-start.4 = (f32[2,64,1024]{2,1,0:T(8,128)S(1)}, f32[2,64,1024]{2,1,0:T(8,128)}, u32[]{:S(2)}) copy-start(f32[2,64,1024]{2,1,0:T(8,128)} %param.16) | copy-start | bytes 1572868
  183.0 5.0 %copy-start.5 = (f32[2,64,1024]{2,1,0:T(8,128)S(1)}, f32[2,64,1024]{2,1,0:T(8,128)}, u32[]{:S(2)}) copy-start(f32[2,64,1024]{2,1,0:T(8,128)} %param.11) | copy-start | bytes 1572868
  185.7 2.3 copy-start.1
  190.2 24.1 %copy-start.6 = (f32[2,64,1024]{2,1,0:T(8,128)S(1)}, f32[2,64,1024]{2,1,0:T(8,128)}, u32[]{:S(2)}) copy-start(f32[2,64,1024]{2,1,0:T(8,128)} %param.15) | copy-start | bytes 1572868
  190.2 43.9 %copy-start.2 = (f32[2,64,1024]{2,1,0:T(8,128)S(1)}, f32[2,64,1024]{2,1,0:T(8,128)}, u32[]{:S(2)}) copy-start(f32[2,64,1024]{2,1,0:T(8,128)} %param.12) | copy-start | bytes 1572868
  216.1 26.7 %all-to-all-start.2 = ((bf16[2,16,4,1024]{3,2,0,1:T(4,128)(2,1)}), bf16[2,16,4,1024]{3,2,0,1:T(4,128)(2,1)S(1)}, u32[]{:S(2)}, u32[]{:S(2)}) async-start(bf16[2,16,4,1024]{3,2,0,1:T(4,128)(2,1)} %copy.24), calls=%async_computation.2 | async-start | bytes 524288 | tf_op jit(solution)/shard_map/all_to_all | solution.py:96
Sparse Core Ops, SparseCore 0:
  74.3 37.2 all-gather.3
  113.9 57.3 all-gather.5

commit v9 on v8

--- a/solution.py
+++ b/solution.py
@@ -24,6 +24,16 @@
     x = x.reshape(sources, x.shape[0] // sources, *x.shape[1:])
     x = lax.all_to_all(x, DP, 0, 0, tiled=True)
     return jnp.sum(x.astype(jnp.float32), axis=0).astype(jnp.bfloat16)
+
+
+def dp_total(x):
+    x = x + lax.ppermute(x, "xlo", [(0, 1), (1, 0)])
+    ring = lax.axis_size("z")
+    step = 1
+    while step < ring:
+        x = x + lax.ppermute(x, "z", [(i, i ^ step) for i in range(ring)])
+        step *= 2
+    return x
 
 
 def per_device(
@@ -75,11 +85,9 @@
     direction = jnp.einsum(
         "srk,skn->srn", root_left, product, preferred_element_type=jnp.float32
     )
-    square_sums = lax.psum(
-        (jnp.sum(adam_step * adam_step, axis=(1, 2)), jnp.sum(direction * direction, axis=(1, 2))),
-        "xlo",
+    square_sums = dp_total(
+        jnp.stack([jnp.sum(adam_step * adam_step, axis=(1, 2)), jnp.sum(direction * direction, axis=(1, 2))])
     )
-    square_sums = lax.psum(square_sums, "z")
     graft = jnp.sqrt(square_sums[0]) / (jnp.sqrt(square_sums[1]) + 1e-06)
     master_new = master - learn_rate * graft[:, None, None] * direction
     occupied_mine = lax.dynamic_slice_in_dim(

time: 251 us -> 250 us (level)
  blocking collectives: 80.1 us -> 63.9 us
  waiting for transfers between devices: 95.9 us -> 105 us
  starting transfers between devices: 29.7 us -> 34.8 us
    psum x2 -> x0, blocking collectives: 16.2 us -> none  [the longest x1 12.4 us: per_device(): square_sums = lax.psum(square_sums, 'z')]
    ppermute x0 -> x4, waiting for transfers between devices: none -> 9.39 us  [the longest x3 6.98 us: dp_total(): x = x + lax.ppermute(x, 'z', [(i, i ^ step) for i in range(ring)])]
    ppermute x0 -> x4, starting transfers between devices: none -> 5.37 us  [the longest x3 5.28 us: dp_total(): x = x + lax.ppermute(x, 'z', [(i, i ^ step) for i in range(ring)])]
  transfers between devices with their start and end apart: 5 -> 9, of which waited for: 4 -> 8; matrix products, arithmetic and copies ran while one was open for 7% -> 7% of each run, Pallas kernels for 0% -> 0%
where the time goes in v9:
time: 250 us; the launch traced here: 249 us
  waiting for transfers between devices  105 us (42%)
  blocking collectives  63.9 us (26%)
  starting transfers between devices  34.8 us (14%)
  matrix products  14.4 us (6%)
  between operations  14.2 us (6%)
  local copies, waits for them, and re-layouts  9.83 us (4%)
  other arithmetic  6.89 us (3%)
    all_to_all x1, blocking collectives, dp_sum(): x = lax.all_to_all(x, DP, 0, 0, tiled=True)  59.3 us
    all_to_all x1, waiting for transfers between devices, per_device(): lax.all_to_all(packed, 'own', split_axis=0, concat_axis=2, tiled=True)  55.1 us
    all_gather x1, waiting for transfers between devices, dp_gather(): return lax.all_gather(x, 'z', axis=axis, tiled=True)  30.8 us
    all_to_all x1, starting transfers between devices, per_device(): lax.all_to_all(shares, 'own', split_axis=1, concat_axis=0, tiled=True)  17.7 us
    all_to_all x1, starting transfers between devices, per_device(): lax.all_to_all(packed, 'own', split_axis=0, concat_axis=2, tiled=True)  11.6 us
    dot_general x1, matrix products, per_device(): jnp.einsum('srk,skn->srn', root_left, product, preferred_element_type=jnp...  7.84 us
    ppermute x3, waiting for transfers between devices, dp_total(): x = x + lax.ppermute(x, 'z', [(i, i ^ step) for i in range(ring)])  6.98 us
    ppermute x1, waiting for transfers between devices, per_device(): partner = lax.ppermute(root_right, 'xlo', [(0, 1), (1, 0)])  5.56 us
  transfers between devices with their start and end apart: 9, of which 8 were waited for; matrix products, arithmetic and copies ran while one was open for 7% of the time, Pallas kernels for 0%

profile of v9, /device:TPU:1, one launch (start us, length us, event | category | flops | bytes accessed | tf_op | source)
XLA Modules:
  0.0 249.3 jit_solution(4979138911070288747)
XLA Ops:
  7.2 2.5 %convert_bitcast_fusion = bf16[16,1,64,1024]{3,2,1,0:T(8,128)(2,1)S(1)} fusion(f32[1,16,64,1024]{3,2,1,0:T(8,128)} %param.9), kind=kLoop, calls=%fused_computation.4 | loop fusion | flops 1048576 | bytes 6291456 | tf_op jit(solution)/shard_map/convert_element_type | solution.py:62
  9.8 59.3 %all_to_all.35 = bf16[16,1,64,1024]{3,2,1,0:T(8,128)(2,1)S(1)} all-to-all(bf16[16,1,64,1024]{3,2,1,0:T(8,128)(2,1)S(1)} %convert_bitcast_fusion), channel_id=1, replica_groups=mesh['z'=8,'xlo'=2,'own'=16] {'z','xlo'}, dimensions={0} | all-to-all | bytes 4194304 | tf_op jit(solution)/shard_map/all_to_all | solution.py:25
  69.6 4.6 %all-gather = bf16[128,1024]{1,0:T(8,128)(2,1)} all-gather(bf16[64,1024]{1,0:T(8,128)(2,1)S(1)} %reduce_sum.41), channel_id=2, replica_groups=mesh['z'=8,'xlo'=2,'own'=16] {'xlo'}, dimensions={0}, use_global_device_ids=true | all-gather | bytes 393216 | tf_op jit(solution)/shard_map/all_gather | solution.py:18
  74.3 5.6 %collective-permute-done = bf16[2,64,1024]{2,1,0:T(8,128)(2,1)S(1)} collective-permute-done((bf16[2,64,1024]{2,1,0:T(8,128)(2,1)S(1)}, bf16[2,64,1024]{2,1,0:T(8,128)(2,1)S(1)}, u32[]{:S(2)}, u32[]{:S(2)}) %collective-permute-start) | collective-permute-done | bytes 262176 | tf_op jit(solution)/shard_map/ppermute | solution.py:59
  80.7 30.8 %all-gather.4.cloned.1.call-done = bf16[16,64,1024]{2,1,0:T(8,128)(2,1)} async-done(((bf16[2,64,1024]{2,1,0:T(8,128)(2,1)}), bf16[16,64,1024]{2,1,0:T(8,128)(2,1)}) %all-gather.4.cloned.1.call-update) | async-done | bytes 2097168 | tf_op jit(solution)/shard_map/all_gather | solution.py:19
  111.7 4.4 %gather_fusion = bf16[32,64,1024]{2,1,0:T(8,128)(2,1)} fusion(bf16[16,64,1024]{2,1,0:T(8,128)(2,1)} %all-gather.4.cloned.1.call-done, s32[1024]{0:T(1024)S(1)} %pad_clamp_fusion.1), kind=kCustom, calls=%fused_computation | custom fusion | bytes 8388736 | tf_op jit(solution)/shard_map/jit(_take)/gather | solution.py:64
  116.0 11.6 %all-to-all-start.1 = ((bf16[16,2,64,1024]{3,2,1,0:T(8,128)(2,1)}), bf16[16,2,64,1024]{3,2,1,0:T(8,128)(2,1)}, u32[]{:S(2)}, u32[]{:S(2)}) async-start(bf16[16,2,64,1024]{3,2,1,0:T(8,128)(2,1)} %bitcast.37), calls=%async_computation.1 | async-start | bytes 8388608 | tf_op jit(solution)/shard_map/all_to_all | solution.py:66
  127.8 55.1 %all-to-all-done.1 = bf16[16,2,64,1024]{3,2,1,0:T(8,128)(2,1)} async-done(((bf16[16,2,64,1024]{3,2,1,0:T(8,128)(2,1)}), bf16[16,2,64,1024]{3,2,1,0:T(8,128)(2,1)}, u32[]{:S(2)}, u32[]{:S(2)}) %all-to-all-start.1) | async-done | bytes 4194336 | tf_op jit(solution)/shard_map/all_to_all | solution.py:66
  183.0 2.7 %copy.22 = bf16[1,2,16,64,1024]{4,3,2,1,0:T(8,128)(2,1)S(1)} copy(bf16[1,2,16,64,1024]{4,3,1,2,0:T(8,128)(2,1)} %bitcast.8) | data formatting | bytes 8388608 | tf_op jit(solution)/shard_map/all_to_all | solution.py:66
  185.7 1.9 fusion.10
  188.0 2.2 fusion.7
  190.2 7.8 %multiply_reduce_fusion = (f32[2]{0:T(128)S(1)}, f32[2,1024,64]{1,2,0:T(8,128)S(1)}) fusion(bf16[2,64,1024]{2,1,0:T(8,128)(2,1)S(1)} %copy-done, bf16[2,1024,1024]{2,1,0:T(8,128)(2,1)} %bitcast.35, bf16[2,1024,1024]{2,1,0:T(8,128)(2,1)} %all-gather.6.cloned.1.call-done), kind=kOutput, calls=%fused_computation.18 | convolution fusion | flops 4565762048 | bytes 9175048 | tf_op jit(solution)/shard_map/srk,skn->srn/dot_general | solution.py:85
  198.2 2.4 collective-permute-done.1
  200.6 1.1 collective-permute-start.2
  201.7 1.4 collective-permute-done.2
  203.1 1.5 collective-permute-start.3
  204.6 2.0 collective-permute-done.3
  206.5 2.7 %collective-permute-start.4 = (f32[2,2]{1,0:T(2,128)S(1)}, f32[2,2]{1,0:T(2,128)S(1)}, u32[]{:S(2)}, u32[]{:S(2)}) collective-permute-start(f32[2,2]{1,0:T(2,128)S(1)} %add.59), channel_id=1, source_target_pairs={{0,128},{32,160},{64,192},{96,224},{128,0},{160,32},{192,64},{224,... | collective-permute-start | bytes 56 | tf_op jit(solution)/shard_map/ppermute | solution.py:34
  209.2 3.6 %collective-permute-done.4 = f32[2,2]{1,0:T(2,128)S(1)} collective-permute-done((f32[2,2]{1,0:T(2,128)S(1)}, f32[2,2]{1,0:T(2,128)S(1)}, u32[]{:S(2)}, u32[]{:S(2)}) %collective-permute-start.4) | collective-permute-done | bytes 48 | tf_op jit(solution)/shard_map/ppermute | solution.py:34
  212.9 1.0 fusion.13
  214.8 17.7 %all-to-all-start.2 = ((bf16[2,16,4,1024]{3,2,0,1:T(4,128)(2,1)}), bf16[2,16,4,1024]{3,2,0,1:T(4,128)(2,1)S(1)}, u32[]{:S(2)}, u32[]{:S(2)}) async-start(bf16[2,16,4,1024]{3,2,0,1:T(4,128)(2,1)} %copy.24), calls=%async_computation.2 | async-start | bytes 524288 | tf_op jit(solution)/shard_map/all_to_all | solution.py:104
  232.4 4.3 %fusion.5 = f32[2,64,1024]{2,1,0:T(8,128)} fusion(f32[2,64,1024]{2,1,0:T(8,128)S(1)} %copy-done.2, bf16[2,1024,1024]{2,1,0:T(8,128)(2,1)} %bitcast.36, s32[]{:T(128)S(6)} %select_n.39, pred[2]{0:T(512)(128)(4,1)S(1)} %dynamic_slice.9), kind=kOutput, calls=%fused_computation.8 | convolution fusion | flops 268959744 | bytes 5767174 | tf_op jit(solution)/shard_map/skr,skn->srn/dot_general | solution.py:76
  236.8 4.4 %all-to-all-done.2 = bf16[2,16,4,1024]{3,2,0,1:T(4,128)(2,1)S(1)} async-done(((bf16[2,16,4,1024]{3,2,0,1:T(4,128)(2,1)}), bf16[2,16,4,1024]{3,2,0,1:T(4,128)(2,1)S(1)}, u32[]{:S(2)}, u32[]{:S(2)}) %all-to-all-start.2) | async-done | bytes 262176 | tf_op jit(solution)/shard_map/all_to_all | solution.py:104
  241.1 1.3 gather_fusion.1
  (40 shorter events, 3.2 us)
Async XLA Ops:
  7.2 183.0 %copy-start = (bf16[2,64,1024]{2,1,0:T(8,128)(2,1)S(1)}, bf16[2,64,1024]{2,1,0:T(8,128)(2,1)}, u32[]{:S(2)}) copy-start(bf16[2,64,1024]{2,1,0:T(8,128)(2,1)} %param.13) | copy-start | bytes 786436
  7.2 104.4 %all-gather.4.cloned.1.call-start = ((), (), s32[]{:S(2)}) async-start(), calls=%async_computation.3 | async-start | bytes 2359296 | tf_op jit(solution)/shard_map/all_gather | solution.py:19
  9.8 64.4 %copy-start.7 = (bf16[2,64,1024]{2,1,0:T(8,128)(2,1)S(1)}, bf16[2,64,1024]{2,1,0:T(8,128)(2,1)}, u32[]{:S(2)}) copy-start(bf16[2,64,1024]{2,1,0:T(8,128)(2,1)} %param.14) | copy-start | bytes 786436
  9.8 101.8 %copy-start.8 = (s32[16]{0:T(128)S(1)}, s32[16]{0:T(128)}, u32[]{:S(2)}) copy-start(s32[16]{0:T(128)} %param.10) | copy-start | bytes 196
  74.2 116.0 %all-gather.6.cloned.1.call-start = ((), (), s32[]{:S(2)}) async-start(), calls=%async_computation.4 | async-start | bytes 4718592 | tf_op jit(solution)/shard_map/all_gather | solution.py:67
  74.2 5.7 %collective-permute-start = (bf16[2,64,1024]{2,1,0:T(8,128)(2,1)S(1)}, bf16[2,64,1024]{2,1,0:T(8,128)(2,1)S(1)}, u32[]{:S(2)}, u32[]{:S(2)}) collective-permute-start(bf16[2,64,1024]{2,1,0:T(8,128)(2,1)S(1)} %copy-done.7), channel_id=1, source_target_pairs={{0,16},{16,0},{1,17},{17,1},{2,18},{18,2},{3,19},{19,3},{4,20},{20... | collective-permute-start | bytes 786440 | tf_op jit(solution)/shard_map/ppermute | solution.py:59
  116.0 66.9 %all-to-all-start.1 = ((bf16[16,2,64,1024]{3,2,1,0:T(8,128)(2,1)}), bf16[16,2,64,1024]{3,2,1,0:T(8,128)(2,1)}, u32[]{:S(2)}, u32[]{:S(2)}) async-start(bf16[16,2,64,1024]{3,2,1,0:T(8,128)(2,1)} %bitcast.37), calls=%async_computation.1 | async-start | bytes 8388608 | tf_op jit(solution)/shard_map/all_to_all | solution.py:66
  182.9 2.8 %copy-start.3 = (f32[2,64,1024]{2,1,0:T(8,128)S(1)}, f32[2,64,1024]{2,1,0:T(8,128)}, u32[]{:S(2)}) copy-start(f32[2,64,1024]{2,1,0:T(8,128)} %param.17) | copy-start | bytes 1572868
  182.9 2.8 %copy-start.4 = (f32[2,64,1024]{2,1,0:T(8,128)S(1)}, f32[2,64,1024]{2,1,0:T(8,128)}, u32[]{:S(2)}) copy-start(f32[2,64,1024]{2,1,0:T(8,128)} %param.16) | copy-start | bytes 1572868
  182.9 5.0 %copy-start.5 = (f32[2,64,1024]{2,1,0:T(8,128)S(1)}, f32[2,64,1024]{2,1,0:T(8,128)}, u32[]{:S(2)}) copy-start(f32[2,64,1024]{2,1,0:T(8,128)} %param.11) | copy-start | bytes 1572868
  185.7 2.3 copy-start.1
  190.2 22.7 %copy-start.6 = (f32[2,64,1024]{2,1,0:T(8,128)S(1)}, f32[2,64,1024]{2,1,0:T(8,128)}, u32[]{:S(2)}) copy-start(f32[2,64,1024]{2,1,0:T(8,128)} %param.15) | copy-start | bytes 1572868
  190.2 42.3 %copy-start.2 = (f32[2,64,1024]{2,1,0:T(8,128)S(1)}, f32[2,64,1024]{2,1,0:T(8,128)}, u32[]{:S(2)}) copy-start(f32[2,64,1024]{2,1,0:T(8,128)} %param.12) | copy-start | bytes 1572868
  198.1 2.5 %collective-permute-start.1 = (f32[2,2]{1,0:T(2,128)S(1)}, f32[2,2]{1,0:T(2,128)S(1)}, u32[]{:S(2)}, u32[]{:S(2)}) collective-permute-start(f32[2,2]{1,0:T(2,128)S(1)} %pad_maximum_fusion), channel_id=1, source_target_pairs={{0,16},{16,0},{1,17},{17,1},{2,18},{18,2},{3,19},{19,3},{4,20},{20... | collective-permute-start | bytes 56 | tf_op jit(solution)/shard_map/ppermute | solution.py:30
  200.6 2.5 %collective-permute-start.2 = (f32[2,2]{1,0:T(2,128)S(1)}, f32[2,2]{1,0:T(2,128)S(1)}, u32[]{:S(2)}, u32[]{:S(2)}) collective-permute-start(f32[2,2]{1,0:T(2,128)S(1)} %fusion.19), channel_id=1, source_target_pairs={{0,32},{32,0},{64,96},{96,64},{128,160},{160,128},{192,224},{224,1... | collective-permute-start | bytes 56 | tf_op jit(solution)/shard_map/ppermute | solution.py:34
  203.1 3.4 %collective-permute-start.3 = (f32[2,2]{1,0:T(2,128)S(1)}, f32[2,2]{1,0:T(2,128)S(1)}, u32[]{:S(2)}, u32[]{:S(2)}) collective-permute-start(f32[2,2]{1,0:T(2,128)S(1)} %fusion.25), channel_id=1, source_target_pairs={{0,64},{32,96},{64,0},{96,32},{128,192},{160,224},{192,128},{224,1... | collective-permute-start | bytes 56 | tf_op jit(solution)/shard_map/ppermute | solution.py:34
  206.5 6.3 %collective-permute-start.4 = (f32[2,2]{1,0:T(2,128)S(1)}, f32[2,2]{1,0:T(2,128)S(1)}, u32[]{:S(2)}, u32[]{:S(2)}) collective-permute-start(f32[2,2]{1,0:T(2,128)S(1)} %add.59), channel_id=1, source_target_pairs={{0,128},{32,160},{64,192},{96,224},{128,0},{160,32},{192,64},{224,... | collective-permute-start | bytes 56 | tf_op jit(solution)/shard_map/ppermute | solution.py:34
  214.8 26.4 %all-to-all-start.2 = ((bf16[2,16,4,1024]{3,2,0,1:T(4,128)(2,1)}), bf16[2,16,4,1024]{3,2,0,1:T(4,128)(2,1)S(1)}, u32[]{:S(2)}, u32[]{:S(2)}) async-start(bf16[2,16,4,1024]{3,2,0,1:T(4,128)(2,1)} %copy.24), calls=%async_computation.2 | async-start | bytes 524288 | tf_op jit(solution)/shard_map/all_to_all | solution.py:104
Sparse Core Ops, SparseCore 0:
  74.3 37.2 all-gather.3
  113.9 57.3 all-gather.5

commit v10 on v9

--- a/solution.py
+++ b/solution.py
@@ -26,14 +26,15 @@
     return jnp.sum(x.astype(jnp.float32), axis=0).astype(jnp.bfloat16)
 
 
-def dp_total(x):
+def dp_total(x, later):
     x = x + lax.ppermute(x, "xlo", [(0, 1), (1, 0)])
+    x, later = lax.optimization_barrier((x, later))
     ring = lax.axis_size("z")
     step = 1
     while step < ring:
         x = x + lax.ppermute(x, "z", [(i, i ^ step) for i in range(ring)])
         step *= 2
-    return x
+    return x, later
 
 
 def per_device(
@@ -70,12 +71,6 @@
     row_part = lax.dynamic_slice_in_dim(rounded, first_row, rows_dev, 1)
     col_part = lax.dynamic_slice_in_dim(rounded, first_row, rows_dev, 2)
     own_rows = row_part.astype(jnp.float32)
-    left_new = stat_decay * stat_left + (1.0 - stat_decay) * jnp.einsum(
-        "srk,snk->srn", row_part, rounded, preferred_element_type=jnp.float32
-    )
-    right_new = stat_decay * stat_right + (1.0 - stat_decay) * jnp.einsum(
-        "skr,skn->srn", col_part, rounded, preferred_element_type=jnp.float32
-    )
     first_new = first_decay * moment_first + (1.0 - first_decay) * own_rows
     second_new = second_decay * moment_second + (1.0 - second_decay) * own_rows * own_rows
     adam_step = first_new / (jnp.sqrt(second_new) + 1e-08)
@@ -85,8 +80,15 @@
     direction = jnp.einsum(
         "srk,skn->srn", root_left, product, preferred_element_type=jnp.float32
     )
-    square_sums = dp_total(
-        jnp.stack([jnp.sum(adam_step * adam_step, axis=(1, 2)), jnp.sum(direction * direction, axis=(1, 2))])
+    square_sums, (row_late, col_late, rounded_late) = dp_total(
+        jnp.stack([jnp.sum(adam_step * adam_step, axis=(1, 2)), jnp.sum(direction * direction, axis=(1, 2))]),
+        (row_part, col_part, rounded),
+    )
+    left_new = stat_decay * stat_left + (1.0 - stat_decay) * jnp.einsum(
+        "srk,snk->srn", row_late, rounded_late, preferred_element_type=jnp.float32
+    )
+    right_new = stat_decay * stat_right + (1.0 - stat_decay) * jnp.einsum(
+        "skr,skn->srn", col_late, rounded_late, preferred_element_type=jnp.float32
     )
     graft = jnp.sqrt(square_sums[0]) / (jnp.sqrt(square_sums[1]) + 1e-06)
     master_new = master - learn_rate * graft[:, None, None] * direction

time: 250 us -> 251 us (level)
  transfers between devices with their start and end apart: 9 -> 9, of which waited for: 8 -> 7; matrix products, arithmetic and copies ran while one was open for 7% -> 8% of each run, Pallas kernels for 0% -> 0%
where the time goes in v10:
time: 251 us; the launch traced here: 250 us
  waiting for transfers between devices  103 us (41%)
  blocking collectives  63.9 us (25%)
  starting transfers between devices  34.3 us (14%)
  matrix products  16.1 us (6%)
  between operations  14.2 us (6%)
  local copies, waits for them, and re-layouts  11.4 us (5%)
  other arithmetic  7.18 us (3%)
    all_to_all x1, blocking collectives, dp_sum(): x = lax.all_to_all(x, DP, 0, 0, tiled=True)  59.3 us
    all_to_all x1, waiting for transfers between devices, per_device(): lax.all_to_all(packed, 'own', split_axis=0, concat_axis=2, tiled=True)  55.1 us
    all_gather x1, waiting for transfers between devices, dp_gather(): return lax.all_gather(x, 'z', axis=axis, tiled=True)  30.8 us
    all_to_all x1, starting transfers between devices, per_device(): lax.all_to_all(shares, 'own', split_axis=1, concat_axis=0, tiled=True)  16.8 us
    all_to_all x1, starting transfers between devices, per_device(): lax.all_to_all(packed, 'own', split_axis=0, concat_axis=2, tiled=True)  11.6 us
    dot_general x1, matrix products, per_device(): jnp.einsum('srk,skn->srn', root_left, product, preferred_element_type=jnp...  7.8 us
    ppermute x3, starting transfers between devices, dp_total(): x = x + lax.ppermute(x, 'z', [(i, i ^ step) for i in range(ring)])  5.62 us
    ppermute x1, waiting for transfers between devices, per_device(): partner = lax.ppermute(root_right, 'xlo', [(0, 1), (1, 0)])  5.56 us
  transfers between devices with their start and end apart: 9, of which 7 were waited for; matrix products, arithmetic and copies ran while one was open for 8% of the time, Pallas kernels for 0%

profile of v10, /device:TPU:1, one launch (start us, length us, event | category | flops | bytes accessed | tf_op | source)
XLA Modules:
  0.0 250.5 jit_solution(15866163680706242155)
XLA Ops:
  7.2 2.5 %convert_bitcast_fusion = bf16[16,1,64,1024]{3,2,1,0:T(8,128)(2,1)S(1)} fusion(f32[1,16,64,1024]{3,2,1,0:T(8,128)} %param.9), kind=kLoop, calls=%fused_computation.4 | loop fusion | flops 1048576 | bytes 6291456 | tf_op jit(solution)/shard_map/convert_element_type | solution.py:63
  9.8 59.3 %all_to_all.35 = bf16[16,1,64,1024]{3,2,1,0:T(8,128)(2,1)S(1)} all-to-all(bf16[16,1,64,1024]{3,2,1,0:T(8,128)(2,1)S(1)} %convert_bitcast_fusion), channel_id=1, replica_groups=mesh['z'=8,'xlo'=2,'own'=16] {'z','xlo'}, dimensions={0} | all-to-all | bytes 4194304 | tf_op jit(solution)/shard_map/all_to_all | solution.py:25
  69.6 4.6 %all-gather = bf16[128,1024]{1,0:T(8,128)(2,1)} all-gather(bf16[64,1024]{1,0:T(8,128)(2,1)S(1)} %reduce_sum.41), channel_id=2, replica_groups=mesh['z'=8,'xlo'=2,'own'=16] {'xlo'}, dimensions={0}, use_global_device_ids=true | all-gather | bytes 393216 | tf_op jit(solution)/shard_map/all_gather | solution.py:18
  74.3 5.6 %collective-permute-done = bf16[2,64,1024]{2,1,0:T(8,128)(2,1)S(1)} collective-permute-done((bf16[2,64,1024]{2,1,0:T(8,128)(2,1)S(1)}, bf16[2,64,1024]{2,1,0:T(8,128)(2,1)S(1)}, u32[]{:S(2)}, u32[]{:S(2)}) %collective-permute-start) | collective-permute-done | bytes 262176 | tf_op jit(solution)/shard_map/ppermute | solution.py:60
  80.7 30.8 %all-gather.4.cloned.1.call-done = bf16[16,64,1024]{2,1,0:T(8,128)(2,1)} async-done(((bf16[2,64,1024]{2,1,0:T(8,128)(2,1)}), bf16[16,64,1024]{2,1,0:T(8,128)(2,1)}) %all-gather.4.cloned.1.call-update) | async-done | bytes 2097168 | tf_op jit(solution)/shard_map/all_gather | solution.py:19
  111.7 4.4 %gather_fusion = bf16[32,64,1024]{2,1,0:T(8,128)(2,1)} fusion(bf16[16,64,1024]{2,1,0:T(8,128)(2,1)} %all-gather.4.cloned.1.call-done, s32[1024]{0:T(1024)S(1)} %pad_clamp_fusion.1), kind=kCustom, calls=%fused_computation | custom fusion | bytes 8388736 | tf_op jit(solution)/shard_map/jit(_take)/gather | solution.py:65
  116.1 11.6 %all-to-all-start.1 = ((bf16[16,2,64,1024]{3,2,1,0:T(8,128)(2,1)}), bf16[16,2,64,1024]{3,2,1,0:T(8,128)(2,1)}, u32[]{:S(2)}, u32[]{:S(2)}) async-start(bf16[16,2,64,1024]{3,2,1,0:T(8,128)(2,1)} %bitcast.40), calls=%async_computation.1 | async-start | bytes 8388608 | tf_op jit(solution)/shard_map/all_to_all | solution.py:67
  127.8 55.1 %all-to-all-done.1 = bf16[16,2,64,1024]{3,2,1,0:T(8,128)(2,1)} async-done(((bf16[16,2,64,1024]{3,2,1,0:T(8,128)(2,1)}), bf16[16,2,64,1024]{3,2,1,0:T(8,128)(2,1)}, u32[]{:S(2)}, u32[]{:S(2)}) %all-to-all-start.1) | async-done | bytes 4194336 | tf_op jit(solution)/shard_map/all_to_all | solution.py:67
  183.0 2.7 %copy.22 = bf16[1,2,16,64,1024]{4,3,2,1,0:T(8,128)(2,1)S(1)} copy(bf16[1,2,16,64,1024]{4,3,1,2,0:T(8,128)(2,1)} %bitcast.8) | data formatting | bytes 8388608 | tf_op jit(solution)/shard_map/all_to_all | solution.py:67
  185.9 1.7 copy-done.1
  188.6 1.3 fusion.11
  189.9 7.8 %multiply_reduce_fusion = (f32[2]{0:T(128)S(1)}, f32[2,1024,64]{1,2,0:T(8,128)S(1)}) fusion(bf16[2,64,1024]{2,1,0:T(8,128)(2,1)S(1)} %copy-done, bf16[2,1024,1024]{2,1,0:T(8,128)(2,1)} %bitcast.37, bf16[2,1024,1024]{2,1,0:T(8,128)(2,1)} %all-gather.6.cloned.1.call-done), kind=kOutput, calls=%fused_computation.18 | convolution fusion | flops 4565762048 | bytes 9175048 | tf_op jit(solution)/shard_map/srk,skn->srn/dot_general | solution.py:80
  197.8 2.4 collective-permute-done.1
  200.2 1.1 collective-permute-start.2
  201.4 3.9 %fusion.5 = f32[2,64,1024]{2,1,0:T(8,128)} fusion(f32[2,64,1024]{2,1,0:T(8,128)S(1)} %copy-done.3, bf16[2,1024,64]{2,1,0:T(8,128)(2,1)S(1)} %constant_dynamic-slice_fusion.1, bf16[2,1024,1024]{2,1,0:T(8,128)(2,1)} %bitcast.38, pred[2]{0:T(512)(128)(4,1)S(1)} %dynamic_slice.9), kind=kOutput, calls=%fused_computation.8 | convolution fusion | flops 268959744 | bytes 5505026 | tf_op jit(solution)/shard_map/skr,skn->srn/dot_general | solution.py:90
  205.3 1.8 collective-permute-start.3
  207.1 1.5 collective-permute-done.3
  208.6 2.7 %collective-permute-start.4 = (f32[2,2]{1,0:T(2,128)S(1)}, f32[2,2]{1,0:T(2,128)S(1)}, u32[]{:S(2)}, u32[]{:S(2)}) collective-permute-start(f32[2,2]{1,0:T(2,128)S(1)} %add.59), channel_id=1, source_target_pairs={{0,128},{32,160},{64,192},{96,224},{128,0},{160,32},{192,64},{224,... | collective-permute-start | bytes 56 | tf_op jit(solution)/shard_map/ppermute | solution.py:35
  211.3 3.6 %collective-permute-done.4 = f32[2,2]{1,0:T(2,128)S(1)} collective-permute-done((f32[2,2]{1,0:T(2,128)S(1)}, f32[2,2]{1,0:T(2,128)S(1)}, u32[]{:S(2)}, u32[]{:S(2)}) %collective-permute-start.4) | collective-permute-done | bytes 48 | tf_op jit(solution)/shard_map/ppermute | solution.py:35
  215.0 1.0 fusion.12
  216.9 16.8 %all-to-all-start.2 = ((bf16[2,16,4,1024]{3,2,0,1:T(4,128)(2,1)}), bf16[2,16,4,1024]{3,2,0,1:T(4,128)(2,1)S(1)}, u32[]{:S(2)}, u32[]{:S(2)}) async-start(bf16[2,16,4,1024]{3,2,0,1:T(4,128)(2,1)} %copy.24), calls=%async_computation.2 | async-start | bytes 524288 | tf_op jit(solution)/shard_map/all_to_all | solution.py:106
  233.7 4.4 %fusion.7 = f32[2,64,1024]{2,1,0:T(8,128)} fusion(f32[2,64,1024]{2,1,0:T(8,128)S(1)} %copy-done.6, bf16[2,64,1024]{2,1,0:T(8,128)(2,1)S(1)} %get-tuple-element.14, bf16[2,1024,1024]{2,1,0:T(8,128)(2,1)} %bitcast.39, pred[2]{0:T(512)(128)(4,1)S(1)} %dynamic_slice.9), kind=kOutput, calls=%fused_computation.11 | convolution fusion | flops 268959744 | bytes 5505026 | tf_op jit(solution)/shard_map/srk,snk->srn/dot_general | solution.py:87
  238.1 4.3 %all-to-all-done.2 = bf16[2,16,4,1024]{3,2,0,1:T(4,128)(2,1)S(1)} async-done(((bf16[2,16,4,1024]{3,2,0,1:T(4,128)(2,1)}), bf16[2,16,4,1024]{3,2,0,1:T(4,128)(2,1)S(1)}, u32[]{:S(2)}, u32[]{:S(2)}) %all-to-all-start.2) | async-done | bytes 262176 | tf_op jit(solution)/shard_map/all_to_all | solution.py:106
  242.4 1.3 gather_fusion.1
  (42 shorter events, 4.0 us)
Async XLA Ops:
  7.2 182.7 %copy-start = (bf16[2,64,1024]{2,1,0:T(8,128)(2,1)S(1)}, bf16[2,64,1024]{2,1,0:T(8,128)(2,1)}, u32[]{:S(2)}) copy-start(bf16[2,64,1024]{2,1,0:T(8,128)(2,1)} %param.13) | copy-start | bytes 786436
  7.2 104.4 %all-gather.4.cloned.1.call-start = ((), (), s32[]{:S(2)}) async-start(), calls=%async_computation.3 | async-start | bytes 2359296 | tf_op jit(solution)/shard_map/all_gather | solution.py:19
  9.8 64.4 %copy-start.7 = (bf16[2,64,1024]{2,1,0:T(8,128)(2,1)S(1)}, bf16[2,64,1024]{2,1,0:T(8,128)(2,1)}, u32[]{:S(2)}) copy-start(bf16[2,64,1024]{2,1,0:T(8,128)(2,1)} %param.14) | copy-start | bytes 786436
  9.8 101.8 %copy-start.8 = (s32[16]{0:T(128)S(1)}, s32[16]{0:T(128)}, u32[]{:S(2)}) copy-start(s32[16]{0:T(128)} %param.10) | copy-start | bytes 196
  74.2 115.7 %all-gather.6.cloned.1.call-start = ((), (), s32[]{:S(2)}) async-start(), calls=%async_computation.4 | async-start | bytes 4718592 | tf_op jit(solution)/shard_map/all_gather | solution.py:68
  74.2 5.7 %collective-permute-start = (bf16[2,64,1024]{2,1,0:T(8,128)(2,1)S(1)}, bf16[2,64,1024]{2,1,0:T(8,128)(2,1)S(1)}, u32[]{:S(2)}, u32[]{:S(2)}) collective-permute-start(bf16[2,64,1024]{2,1,0:T(8,128)(2,1)S(1)} %copy-done.7), channel_id=1, source_target_pairs={{0,16},{16,0},{1,17},{17,1},{2,18},{18,2},{3,19},{19,3},{4,20},{20... | collective-permute-start | bytes 786440 | tf_op jit(solution)/shard_map/ppermute | solution.py:60
  116.1 66.9 %all-to-all-start.1 = ((bf16[16,2,64,1024]{3,2,1,0:T(8,128)(2,1)}), bf16[16,2,64,1024]{3,2,1,0:T(8,128)(2,1)}, u32[]{:S(2)}, u32[]{:S(2)}) async-start(bf16[16,2,64,1024]{3,2,1,0:T(8,128)(2,1)} %bitcast.40), calls=%async_computation.1 | async-start | bytes 8388608 | tf_op jit(solution)/shard_map/all_to_all | solution.py:67
  183.0 4.7 %copy-start.2 = (f32[2,64,1024]{2,1,0:T(8,128)S(1)}, f32[2,64,1024]{2,1,0:T(8,128)}, u32[]{:S(2)}) copy-start(f32[2,64,1024]{2,1,0:T(8,128)} %param.17) | copy-start | bytes 1572868
  183.0 5.7 %copy-start.4 = (f32[2,64,1024]{2,1,0:T(8,128)S(1)}, f32[2,64,1024]{2,1,0:T(8,128)}, u32[]{:S(2)}) copy-start(f32[2,64,1024]{2,1,0:T(8,128)} %param.16) | copy-start | bytes 1572868
  185.7 2.0 copy-start.1
  189.9 11.5 %copy-start.3 = (f32[2,64,1024]{2,1,0:T(8,128)S(1)}, f32[2,64,1024]{2,1,0:T(8,128)}, u32[]{:S(2)}) copy-start(f32[2,64,1024]{2,1,0:T(8,128)} %param.12) | copy-start | bytes 1572868
  197.7 17.3 %copy-start.5 = (f32[2,64,1024]{2,1,0:T(8,128)S(1)}, f32[2,64,1024]{2,1,0:T(8,128)}, u32[]{:S(2)}) copy-start(f32[2,64,1024]{2,1,0:T(8,128)} %param.15) | copy-start | bytes 1572868
  197.7 2.5 %collective-permute-start.1 = (f32[2,2]{1,0:T(2,128)S(1)}, f32[2,2]{1,0:T(2,128)S(1)}, u32[]{:S(2)}, u32[]{:S(2)}) collective-permute-start(f32[2,2]{1,0:T(2,128)S(1)} %pad_maximum_fusion), channel_id=1, source_target_pairs={{0,16},{16,0},{1,17},{17,1},{2,18},{18,2},{3,19},{19,3},{4,20},{20... | collective-permute-start | bytes 56 | tf_op jit(solution)/shard_map/ppermute | solution.py:30
  200.2 33.4 %copy-start.6 = (f32[2,64,1024]{2,1,0:T(8,128)S(1)}, f32[2,64,1024]{2,1,0:T(8,128)}, u32[]{:S(2)}) copy-start(f32[2,64,1024]{2,1,0:T(8,128)} %param.11) | copy-start | bytes 1572868
  200.2 5.0 %collective-permute-start.2 = (f32[2,2]{1,0:T(2,128)S(1)}, f32[2,2]{1,0:T(2,128)S(1)}, u32[]{:S(2)}, u32[]{:S(2)}) collective-permute-start(f32[2,2]{1,0:T(2,128)S(1)} %fusion.15), channel_id=1, source_target_pairs={{0,32},{32,0},{64,96},{96,64},{128,160},{160,128},{192,224},{224,1... | collective-permute-start | bytes 56 | tf_op jit(solution)/shard_map/ppermute | solution.py:35
  205.3 3.3 %collective-permute-start.3 = (f32[2,2]{1,0:T(2,128)S(1)}, f32[2,2]{1,0:T(2,128)S(1)}, u32[]{:S(2)}, u32[]{:S(2)}) collective-permute-start(f32[2,2]{1,0:T(2,128)S(1)} %add.58), channel_id=1, source_target_pairs={{0,64},{32,96},{64,0},{96,32},{128,192},{160,224},{192,128},{224,1... | collective-permute-start | bytes 56 | tf_op jit(solution)/shard_map/ppermute | solution.py:35
  208.6 6.3 %collective-permute-start.4 = (f32[2,2]{1,0:T(2,128)S(1)}, f32[2,2]{1,0:T(2,128)S(1)}, u32[]{:S(2)}, u32[]{:S(2)}) collective-permute-start(f32[2,2]{1,0:T(2,128)S(1)} %add.59), channel_id=1, source_target_pairs={{0,128},{32,160},{64,192},{96,224},{128,0},{160,32},{192,64},{224,... | collective-permute-start | bytes 56 | tf_op jit(solution)/shard_map/ppermute | solution.py:35
  216.9 25.5 %all-to-all-start.2 = ((bf16[2,16,4,1024]{3,2,0,1:T(4,128)(2,1)}), bf16[2,16,4,1024]{3,2,0,1:T(4,128)(2,1)S(1)}, u32[]{:S(2)}, u32[]{:S(2)}) async-start(bf16[2,16,4,1024]{3,2,0,1:T(4,128)(2,1)} %copy.24), calls=%async_computation.2 | async-start | bytes 524288 | tf_op jit(solution)/shard_map/all_to_all | solution.py:106
Sparse Core Ops, SparseCore 0:
  74.3 37.2 all-gather.3
  113.9 57.3 all-gather.5

commit v11 on v9

--- a/solution.py
+++ b/solution.py
@@ -20,10 +20,16 @@
 
 
 def dp_sum(x):
-    sources = lax.axis_size("z") * lax.axis_size("xlo")
-    x = x.reshape(sources, x.shape[0] // sources, *x.shape[1:])
+    pairs, peers = lax.axis_size("z"), lax.axis_size("xlo")
+    x = x.reshape(peers, pairs, x.shape[0] // (pairs * peers), *x.shape[1:])
+    x = jnp.swapaxes(x, 0, 1).reshape(pairs * peers, -1, *x.shape[3:])
     x = lax.all_to_all(x, DP, 0, 0, tiled=True)
     return jnp.sum(x.astype(jnp.float32), axis=0).astype(jnp.bfloat16)
+
+
+def block_gather(x):
+    x = lax.all_gather(x, "z", axis=0, tiled=True)
+    return lax.all_gather(x, "xlo", axis=0, tiled=True)
 
 
 def dp_total(x):
@@ -59,7 +65,7 @@
     partner = lax.ppermute(root_right, "xlo", [(0, 1), (1, 0)])
     pair = jnp.where(lax.axis_index("xlo") == 0, jnp.stack([root_right, partner]), jnp.stack([partner, root_right]))
     pair = jnp.swapaxes(pair, 0, 1).reshape(slot_count, 2 * rows_dev, order_size)
-    summed = dp_gather(dp_sum(grads[0].astype(jnp.bfloat16)), 0)
+    summed = block_gather(dp_sum(grads[0].astype(jnp.bfloat16)))
     summed, pair = lax.optimization_barrier((summed, pair))
     packed = jnp.take(summed, block_of, axis=0, mode="clip")
     packed = packed.reshape(owners, slot_count, rows_dev, order_size)

time: 250 us -> 280 us (1.12)
  waiting for transfers between devices: 105 us -> 139 us
  blocking collectives: 63.9 us -> 59.3 us
    all_gather x1 -> x2, waiting for transfers between devices: 30.8 us -> 69.5 us  [the longest x1 37 us: block_gather(): return lax.all_gather(x, 'xlo', axis=0, tiled=True)]
    all_gather x1 -> x0, blocking collectives: 4.59 us -> none  [dp_gather(): x = lax.all_gather(x, 'xlo', axis=axis, tiled=True)]
    all_to_all x1, starting transfers between devices: 11.6 us -> 7.26 us  [per_device(): lax.all_to_all(packed, 'own', split_axis=0, concat_axis=2, tiled=True)]
    ppermute x3, starting transfers between devices: 5.28 us -> 9.18 us  [dp_total(): x = x + lax.ppermute(x, 'z', [(i, i ^ step) for i in range(ring)])]
    ppermute x3, waiting for transfers between devices: 6.98 us -> 3.16 us  [dp_total(): x = x + lax.ppermute(x, 'z', [(i, i ^ step) for i in range(ring)])]
  transfers between devices with their start and end apart: 9 -> 10, of which waited for: 8 -> 9; matrix products, arithmetic and copies ran while one was open for 7% -> 6% of each run, Pallas kernels for 0% -> 0%
where the time goes in v11:
time: 280 us; the launch traced here: 279 us
  waiting for transfers between devices  139 us (50%)
  blocking collectives  59.3 us (21%)
  starting transfers between devices  35.5 us (13%)
  matrix products  14.4 us (5%)
  between operations  13.9 us (5%)
  local copies, waits for them, and re-layouts  10 us (4%)
  other arithmetic  7.54 us (3%)
    all_to_all x1, blocking collectives, dp_sum(): x = lax.all_to_all(x, DP, 0, 0, tiled=True)  59.3 us
    all_to_all x1, waiting for transfers between devices, per_device(): lax.all_to_all(packed, 'own', split_axis=0, concat_axis=2, tiled=True)  55.1 us
    all_gather x1, waiting for transfers between devices, block_gather(): return lax.all_gather(x, 'xlo', axis=0, tiled=True)  37 us
    all_gather x1, waiting for transfers between devices, block_gather(): x = lax.all_gather(x, 'z', axis=0, tiled=True)  32.4 us
    all_to_all x1, starting transfers between devices, per_device(): lax.all_to_all(shares, 'own', split_axis=1, concat_axis=0, tiled=True)  17.6 us
    ppermute x3, starting transfers between devices, dp_total(): x = x + lax.ppermute(x, 'z', [(i, i ^ step) for i in range(ring)])  9.18 us
    dot_general x1, matrix products, per_device(): jnp.einsum('srk,skn->srn', root_left, product, preferred_element_type=jnp...  7.84 us
    all_to_all x1, starting transfers between devices, per_device(): lax.all_to_all(packed, 'own', split_axis=0, concat_axis=2, tiled=True)  7.26 us
  transfers between devices with their start and end apart: 10, of which 9 were waited for; matrix products, arithmetic and copies ran while one was open for 6% of the time, Pallas kernels for 0%

profile of v11, /device:TPU:1, one launch (start us, length us, event | category | flops | bytes accessed | tf_op | source)
XLA Modules:
  0.0 279.3 jit_solution(11078987627856453370)
XLA Ops:
  7.2 2.5 convert_element_type.24
  10.0 59.3 %all_to_all.35 = bf16[16,1,64,1024]{3,2,1,0:T(8,128)(2,1)S(1)} all-to-all(bf16[16,1,64,1024]{3,2,1,0:T(8,128)(2,1)S(1)} %bitcast.43), channel_id=1, replica_groups=mesh['z'=8,'xlo'=2,'own'=16] {'z','xlo'}, dimensions={0} | all-to-all | bytes 4194304 | tf_op jit(solution)/shard_map/all_to_all | solution.py:26
  69.3 1.1 reduce_sum.41
  70.5 32.4 %all-gather.9.cloned.1.call-done = bf16[512,1024]{1,0:T(8,128)(2,1)} async-done(((bf16[64,1024]{1,0:T(8,128)(2,1)}), bf16[512,1024]{1,0:T(8,128)(2,1)}) %all-gather.9.cloned.1.call-update) | async-done | bytes 1048592 | tf_op jit(solution)/shard_map/all_gather | solution.py:31
  103.0 1.3 collective-permute-start
  104.3 4.0 %collective-permute-done = bf16[2,64,1024]{2,1,0:T(8,128)(2,1)S(1)} collective-permute-done((bf16[2,64,1024]{2,1,0:T(8,128)(2,1)S(1)}, bf16[2,64,1024]{2,1,0:T(8,128)(2,1)S(1)}, u32[]{:S(2)}, u32[]{:S(2)}) %collective-permute-start) | collective-permute-done | bytes 262176 | tf_op jit(solution)/shard_map/ppermute | solution.py:65
  109.2 37.0 %all-gather.5.cloned.1.call-done = bf16[16,64,1024]{2,1,0:T(8,128)(2,1)} async-done(((bf16[8,64,1024]{2,1,0:T(8,128)(2,1)}), bf16[16,64,1024]{2,1,0:T(8,128)(2,1)}) %all-gather.5.cloned.1.call-update) | async-done | bytes 2097168 | tf_op jit(solution)/shard_map/all_gather | solution.py:32
  146.3 4.4 %gather_fusion = bf16[32,64,1024]{2,1,0:T(8,128)(2,1)} fusion(bf16[16,64,1024]{2,1,0:T(8,128)(2,1)} %all-gather.5.cloned.1.call-done, s32[1024]{0:T(1024)S(1)} %pad_clamp_fusion.1), kind=kCustom, calls=%fused_computation | custom fusion | bytes 8388736 | tf_op jit(solution)/shard_map/jit(_take)/gather | solution.py:70
  150.7 7.3 %all-to-all-start.1 = ((bf16[16,2,64,1024]{3,2,1,0:T(8,128)(2,1)}), bf16[16,2,64,1024]{3,2,1,0:T(8,128)(2,1)}, u32[]{:S(2)}, u32[]{:S(2)}) async-start(bf16[16,2,64,1024]{3,2,1,0:T(8,128)(2,1)} %bitcast.41), calls=%async_computation.1 | async-start | bytes 8388608 | tf_op jit(solution)/shard_map/all_to_all | solution.py:72
  158.1 55.1 %all-to-all-done.1 = bf16[16,2,64,1024]{3,2,1,0:T(8,128)(2,1)} async-done(((bf16[16,2,64,1024]{3,2,1,0:T(8,128)(2,1)}), bf16[16,2,64,1024]{3,2,1,0:T(8,128)(2,1)}, u32[]{:S(2)}, u32[]{:S(2)}) %all-to-all-start.1) | async-done | bytes 4194336 | tf_op jit(solution)/shard_map/all_to_all | solution.py:72
  213.3 2.7 copy.30
  216.0 1.9 fusion.10
  218.3 2.2 fusion.7
  220.5 7.8 %multiply_reduce_fusion = (f32[2]{0:T(128)S(1)}, f32[2,1024,64]{1,2,0:T(8,128)S(1)}) fusion(bf16[2,64,1024]{2,1,0:T(8,128)(2,1)S(1)} %copy-done, bf16[2,1024,1024]{2,1,0:T(8,128)(2,1)} %bitcast.39, bf16[2,1024,1024]{2,1,0:T(8,128)(2,1)} %all-gather.7.cloned.1.call-done), kind=kOutput, calls=%fused_computation.17 | convolution fusion | flops 4565762048 | bytes 9175048 | tf_op jit(solution)/shard_map/srk,skn->srn/dot_general | solution.py:91
  228.5 2.4 collective-permute-done.1
  230.9 1.4 collective-permute-start.2
  232.2 1.1 collective-permute-done.2
  233.4 2.4 collective-permute-start.3
  235.8 1.1 collective-permute-done.3
  236.8 5.5 %collective-permute-start.4 = (f32[2,2]{1,0:T(2,128)S(1)}, f32[2,2]{1,0:T(2,128)S(1)}, u32[]{:S(2)}, u32[]{:S(2)}) collective-permute-start(f32[2,2]{1,0:T(2,128)S(1)} %add.59), channel_id=1, source_target_pairs={{0,128},{32,160},{64,192},{96,224},{128,0},{160,32},{192,64},{224,... | collective-permute-start | bytes 56 | tf_op jit(solution)/shard_map/ppermute | solution.py:40
  245.2 17.6 %all-to-all-start.2 = ((bf16[2,16,4,1024]{3,2,0,1:T(4,128)(2,1)}), bf16[2,16,4,1024]{3,2,0,1:T(4,128)(2,1)S(1)}, u32[]{:S(2)}, u32[]{:S(2)}) async-start(bf16[2,16,4,1024]{3,2,0,1:T(4,128)(2,1)} %copy.32), calls=%async_computation.2 | async-start | bytes 524288 | tf_op jit(solution)/shard_map/all_to_all | solution.py:110
  262.7 4.3 %fusion.5 = f32[2,64,1024]{2,1,0:T(8,128)} fusion(f32[2,64,1024]{2,1,0:T(8,128)S(1)} %copy-done.2, bf16[2,1024,1024]{2,1,0:T(8,128)(2,1)} %bitcast.40, s32[]{:T(128)S(6)} %select_n.39, pred[2]{0:T(512)(128)(4,1)S(1)} %dynamic_slice.9), kind=kOutput, calls=%fused_computation.7 | convolution fusion | flops 268959744 | bytes 5767174 | tf_op jit(solution)/shard_map/skr,skn->srn/dot_general | solution.py:82
  267.1 4.4 %all-to-all-done.2 = bf16[2,16,4,1024]{3,2,0,1:T(4,128)(2,1)S(1)} async-done(((bf16[2,16,4,1024]{3,2,0,1:T(4,128)(2,1)}), bf16[2,16,4,1024]{3,2,0,1:T(4,128)(2,1)S(1)}, u32[]{:S(2)}, u32[]{:S(2)}) %all-to-all-start.2) | async-done | bytes 262176 | tf_op jit(solution)/shard_map/all_to_all | solution.py:110
  271.4 1.3 gather_fusion.1
  (43 shorter events, 4.9 us)
Async XLA Ops:
  7.2 213.3 %copy-start = (bf16[2,64,1024]{2,1,0:T(8,128)(2,1)S(1)}, bf16[2,64,1024]{2,1,0:T(8,128)(2,1)}, u32[]{:S(2)}) copy-start(bf16[2,64,1024]{2,1,0:T(8,128)(2,1)} %param.13) | copy-start | bytes 786436
  7.2 95.7 %all-gather.9.cloned.1.call-start = ((), (), s32[]{:S(2)}) async-start(), calls=%async_computation.5 | async-start | bytes 1179648 | tf_op jit(solution)/shard_map/all_gather | solution.py:31
  10.0 93.0 %copy-start.7 = (bf16[2,64,1024]{2,1,0:T(8,128)(2,1)S(1)}, bf16[2,64,1024]{2,1,0:T(8,128)(2,1)}, u32[]{:S(2)}) copy-start(bf16[2,64,1024]{2,1,0:T(8,128)(2,1)} %param.14) | copy-start | bytes 786436
  10.0 136.2 %copy-start.8 = (s32[16]{0:T(128)S(1)}, s32[16]{0:T(128)}, u32[]{:S(2)}) copy-start(s32[16]{0:T(128)} %param.10) | copy-start | bytes 196
  70.4 75.7 %all-gather.5.cloned.1.call-start = ((), (), s32[]{:S(2)}) async-start(), calls=%async_computation.3 | async-start | bytes 3145728 | tf_op jit(solution)/shard_map/all_gather | solution.py:32
  102.9 117.6 %all-gather.7.cloned.1.call-start = ((), (), s32[]{:S(2)}) async-start(), calls=%async_computation.4 | async-start | bytes 4718592 | tf_op jit(solution)/shard_map/all_gather | solution.py:73
  103.0 5.3 %collective-permute-start = (bf16[2,64,1024]{2,1,0:T(8,128)(2,1)S(1)}, bf16[2,64,1024]{2,1,0:T(8,128)(2,1)S(1)}, u32[]{:S(2)}, u32[]{:S(2)}) collective-permute-start(bf16[2,64,1024]{2,1,0:T(8,128)(2,1)S(1)} %copy-done.7), channel_id=1, source_target_pairs={{0,16},{16,0},{1,17},{17,1},{2,18},{18,2},{3,19},{19,3},{4,20},{20... | collective-permute-start | bytes 786440 | tf_op jit(solution)/shard_map/ppermute | solution.py:65
  150.7 62.6 %all-to-all-start.1 = ((bf16[16,2,64,1024]{3,2,1,0:T(8,128)(2,1)}), bf16[16,2,64,1024]{3,2,1,0:T(8,128)(2,1)}, u32[]{:S(2)}, u32[]{:S(2)}) async-start(bf16[16,2,64,1024]{3,2,1,0:T(8,128)(2,1)} %bitcast.41), calls=%async_computation.1 | async-start | bytes 8388608 | tf_op jit(solution)/shard_map/all_to_all | solution.py:72
  213.3 2.8 copy-start.3
  213.3 2.8 copy-start.4
  213.3 5.0 %copy-start.5 = (f32[2,64,1024]{2,1,0:T(8,128)S(1)}, f32[2,64,1024]{2,1,0:T(8,128)}, u32[]{:S(2)}) copy-start(f32[2,64,1024]{2,1,0:T(8,128)} %param.11) | copy-start | bytes 1572868
  216.0 2.3 copy-start.1
  220.5 22.8 %copy-start.6 = (f32[2,64,1024]{2,1,0:T(8,128)S(1)}, f32[2,64,1024]{2,1,0:T(8,128)}, u32[]{:S(2)}) copy-start(f32[2,64,1024]{2,1,0:T(8,128)} %param.15) | copy-start | bytes 1572868
  220.5 42.2 %copy-start.2 = (f32[2,64,1024]{2,1,0:T(8,128)S(1)}, f32[2,64,1024]{2,1,0:T(8,128)}, u32[]{:S(2)}) copy-start(f32[2,64,1024]{2,1,0:T(8,128)} %param.12) | copy-start | bytes 1572868
  228.4 2.5 collective-permute-start.1
  230.9 2.5 collective-permute-start.2
  233.4 3.4 %collective-permute-start.3 = (f32[2,2]{1,0:T(2,128)S(1)}, f32[2,2]{1,0:T(2,128)S(1)}, u32[]{:S(2)}, u32[]{:S(2)}) collective-permute-start(f32[2,2]{1,0:T(2,128)S(1)} %fusion.25), channel_id=1, source_target_pairs={{0,64},{32,96},{64,0},{96,32},{128,192},{160,224},{192,128},{224,1... | collective-permute-start | bytes 56 | tf_op jit(solution)/shard_map/ppermute | solution.py:40
  236.8 6.4 %collective-permute-start.4 = (f32[2,2]{1,0:T(2,128)S(1)}, f32[2,2]{1,0:T(2,128)S(1)}, u32[]{:S(2)}, u32[]{:S(2)}) collective-permute-start(f32[2,2]{1,0:T(2,128)S(1)} %add.59), channel_id=1, source_target_pairs={{0,128},{32,160},{64,192},{96,224},{128,0},{160,32},{192,64},{224,... | collective-permute-start | bytes 56 | tf_op jit(solution)/shard_map/ppermute | solution.py:40
  245.2 26.3 %all-to-all-start.2 = ((bf16[2,16,4,1024]{3,2,0,1:T(4,128)(2,1)}), bf16[2,16,4,1024]{3,2,0,1:T(4,128)(2,1)S(1)}, u32[]{:S(2)}, u32[]{:S(2)}) async-start(bf16[2,16,4,1024]{3,2,0,1:T(4,128)(2,1)} %copy.32), calls=%async_computation.2 | async-start | bytes 524288 | tf_op jit(solution)/shard_map/all_to_all | solution.py:110
Sparse Core Ops, SparseCore 0:
  70.5 32.3 all-gather.8
  104.7 41.4 all-gather.4
  148.5 55.7 all-gather.6
